TPU v7x, 128 devices: a whole 4x4x4 slice. The times are simulated.
128 devices in a mesh: row: 8 (over x, core), col: 8 (over z_lo, y), space: 2 (over z_hi).
Axes of the slice: x: 4, y: 4, z: 4 (z_hi: 2, z_lo: 2; z = z_hi * 2 + z_lo), core: 2. Of those that a mesh axis runs over, the one named last changes fastest.
Arguments:
- snapshots: bfloat16 [32768, 8192], P(('row', 'col'), 'space'), may hold values from -10 to 10
- ocean_mask: int32 [8192], P('space'), may hold values 0 or 1
- spread: float32 [], replicated, may hold values from 1 to 2
Outputs:
- affinity: float32 [3, 32768, 512], P(None, ('row', 'col'), 'space')
All inputs are finite; a program needn't handle non-finite values. No bound on the sum of `ocean_mask` on one device may be relied on, other than what follows from the above.
Results may differ from a plain program's by a relative error of at most 0.0003.
Values may be sent and summed in bfloat16 or wider, within the bound.
No kernel may reach another device: no remote copies, remote signals or barrier semaphores. Data moves between devices by JAX's collectives and lax.ppermute only.
A program may use at most 64 MiB of HBM per device.

v0:
```python
import jax
import jax.numpy as jnp
from jax import lax
from jax.sharding import PartitionSpec as P

LAG = 240
BANDS = 3


def passed_along(block, axis, distance):
    devices = range(lax.axis_size(axis))
    route = [(i - distance, i) for i in devices if i - distance in devices]
    return lax.ppermute(block, axis, route)


def shifted(block, axis, distance):
    devices = range(lax.axis_size(axis))
    route = [((i - distance) % len(devices), i) for i in devices]
    return lax.ppermute(block, axis, route)


def combine_lags(earlier, later, extent):
    keep = earlier.shape[0] + later.shape[0] - extent - 1
    return earlier[-keep:, -keep:] + later[:keep, :keep]


def lag_sum(distance, window):
    extent = distance.shape[0]
    summed = None
    doubled = distance
    remaining = window
    while remaining:
        if remaining % 2 == 1:
            summed = doubled if summed is None else combine_lags(summed, doubled, extent)
        remaining = remaining // 2
        if remaining:
            doubled = combine_lags(doubled, doubled, extent)
    return summed


def square_norms(values):
    return jnp.sum(jnp.square(values.astype(jnp.float32)), axis=1)


def per_device(snapshots, ocean_mask, spread):
    block_rows = snapshots.shape[0]
    cells_dev = snapshots.shape[1]
    masked = snapshots * ocean_mask.astype(jnp.bfloat16)[None, :]
    history = passed_along(masked[block_rows - (LAG - 1) :], ("row", "col"), 1)
    own_rows = jnp.concatenate([history, masked], axis=0)
    partners = [own_rows]
    current = own_rows
    for offset in range(1, BANDS):
        current = shifted(current, "col", 1)
        partners.append(current)
    row_sq = square_norms(own_rows)
    lagged_list = []
    for partner in partners:
        col_sq = square_norms(partner)
        gram_tile = lax.dot_general(
            own_rows, partner, (((1,), (1,)), ((), ())), preferred_element_type=jnp.float32
        )
        distance = row_sq[:, None] + col_sq[None, :] - 2.0 * gram_tile
        lagged_list.append(lag_sum(distance, LAG))
    partial_dist = jnp.stack(lagged_list)
    column_width = block_rows // lax.axis_size("space")
    start_col = lax.axis_index("space") * column_width
    summed_dist = lax.psum(partial_dist, "space")
    lagged = lax.dynamic_slice_in_dim(summed_dist, start_col, column_width, 2)
    total_cells = cells_dev * lax.axis_size("space")
    kernel = jnp.exp(-lagged / (LAG * total_cells * spread))
    degree = lax.psum(jnp.sum(kernel, axis=(0, 2)), "space")
    degree_list = [degree]
    current_degree = degree
    for offset in range(1, BANDS):
        current_degree = shifted(current_degree, "col", 1)
        degree_list.append(current_degree)
    column_degrees = lax.dynamic_slice_in_dim(jnp.stack(degree_list), start_col, column_width, 1)
    factor = float(BANDS * block_rows)
    return factor * kernel / jnp.sqrt(degree[None, :, None] * column_degrees[:, None, :])


def solution(mesh):
    placed = (P(("row", "col"), "space"), P("space"), P())
    return jax.shard_map(
        per_device,
        mesh=mesh,
        in_specs=placed,
        out_specs=P(None, ("row", "col"), "space"),
        check_vma=False,
    )
```

profile of v0, /device:TPU:4, one launch (start us, length us, event | category | flops | bytes accessed | tf_op | source)
XLA Modules:
  0.0 480.4 jit_solution(48389655260421391)
XLA Ops:
  6.5 0.7 convert_element_type.13
  7.3 2.5 broadcast_multiply_fusion
  9.7 0.6 slice.244
  10.3 3.5 collective-permute-start
  13.8 42.1 %collective-permute-done = bf16[239,4096]{1,0:T(8,128)(2,1)S(1)} collective-permute-done((bf16[239,4096]{1,0:T(8,128)(2,1)S(1)}, bf16[239,4096]{1,0:T(8,128)(2,1)S(1)}, u32[]{:S(2)}, u32[]{:S(2)}) %collective-permute-start) | collective-permute-done | bytes 1957920 | tf_op jit(solution)/shard_map/ppermute | solution.py:13
  55.9 3.8 pad_maximum_fusion
  59.7 2.5 collective-permute-start.1
  62.1 2.3 multiply_reduce_fusion.2
  64.4 5.0 %multiply_subtract_fusion.2 = f32[751,751]{1,0:T(8,128)S(1)} fusion(f32[751]{0:T(1024)S(1)} %multiply_reduce_fusion.2, bf16[512,4096]{1,0:T(8,128)(2,1)S(1)} %broadcast_multiply_fusion, bf16[239,4096]{1,0:T(8,128)(2,1)S(1)} %collective-permute-done), kind=kOutput, calls=%fused_computation.13 | convolution fusion | flops 4634293248 | bytes 8411200 | tf_op jit(solution)/shard_map/dot_general | solution.py:60
  69.4 0.9 slice_add_fusion.5
  70.3 0.8 slice_add_fusion.4
  71.2 0.8 slice_add_fusion.8
  72.0 124.6 %collective-permute-done.1 = bf16[751,4096]{1,0:T(8,128)(2,1)S(1)} collective-permute-done((bf16[751,4096]{1,0:T(8,128)(2,1)}, bf16[751,4096]{1,0:T(8,128)(2,1)S(1)}, u32[]{:S(2)}, u32[]{:S(2)}) %collective-permute-start.1) | collective-permute-done | bytes 6152224 | tf_op jit(solution)/shard_map/ppermute | solution.py:19
  196.6 0.7 collective-permute-start.2
  197.3 0.7 slice_add_fusion.11
  198.5 0.6 slice_add_fusion.14
  199.6 0.6 slice_add_fusion.17
  200.4 0.5 fusion.9
  200.9 1.3 fusion.5
  202.2 1.3 multiply_reduce_fusion.1
  203.5 5.0 %multiply_subtract_fusion.1 = f32[751,751]{1,0:T(8,128)S(1)} fusion(bf16[751,4096]{1,0:T(8,128)(2,1)S(1)} %collective-permute-done.1, f32[751]{0:T(1024)S(1)} %multiply_reduce_fusion.1, f32[751]{0:T(1024)S(1)} %multiply_reduce_fusion.2, bf16[512,4096]{1,0:T(8,128)(2,1)S(1)} %broadcast_multiply_fusion, bf16[239,4096]{1,0:T(8,128)(2,1)S(1)} %collective-permute-done), kind=kOutput, calls=%fused_computation.12 | convolution fusion | flops 4634293248 | bytes 14566396 | tf_op jit(solution)/shard_map/dot_general | solution.py:60
  208.5 0.9 slice_add_fusion.3
  209.3 0.8 slice_add_fusion.2
  210.2 0.8 slice_add_fusion.7
  211.0 0.7 slice_add_fusion.10
  211.7 0.7 slice.281
  212.3 0.6 slice_add_fusion.13
  213.5 0.6 slice_add_fusion.16
  214.2 2.2 fusion.10
  216.4 117.5 %collective-permute-done.2 = bf16[751,4096]{1,0:T(8,128)(2,1)} collective-permute-done((bf16[751,4096]{1,0:T(8,128)(2,1)S(1)}, bf16[751,4096]{1,0:T(8,128)(2,1)}, u32[]{:S(2)}, u32[]{:S(2)}) %collective-permute-start.2) | collective-permute-done | bytes 6152224 | tf_op jit(solution)/shard_map/ppermute | solution.py:19
  333.9 4.0 multiply_reduce_fusion
  337.9 7.9 %multiply_subtract_fusion = f32[751,751]{1,0:T(8,128)S(1)} fusion(bf16[751,4096]{1,0:T(8,128)(2,1)} %collective-permute-done.2, f32[751]{0:T(1024)S(1)} %multiply_reduce_fusion, f32[751]{0:T(1024)S(1)} %multiply_reduce_fusion.2, bf16[512,4096]{1,0:T(8,128)(2,1)S(1)} %broadcast_multiply_fusion, bf16[239,4096]{1,0:T(8,128)(2,1)S(1)} %collective-permute-done), kind=kOutput, calls=%fused_computation.11 | convolution fusion | flops 4634293248 | bytes 14566396 | tf_op jit(solution)/shard_map/dot_general | solution.py:60
  345.8 0.8 slice_add_fusion.1
  346.7 0.9 slice_add_fusion
  347.5 0.8 slice_add_fusion.6
  348.4 0.7 slice_add_fusion.9
  349.0 0.6 slice_add_fusion.12
  349.7 0.8 slice_add_fusion.15
  352.1 0.9 copy-done
  353.5 0.7 fusion.1
  354.7 2.0 pad_maximum_fusion.1
  357.4 93.3 %all-reduce.2.cloned.1.call-done = f32[3,512,512]{2,1,0:T(8,128)} async-done(((f32[3,512,512]{2,1,0:T(8,128)}), f32[3,512,512]{2,1,0:T(8,128)}) %all-reduce.2.cloned.1.call-update) | async-done | bytes 3145744 | tf_op jit(solution)/shard_map/psum | solution.py:68
  450.7 1.7 fusion.6
  452.5 6.4 %psum.15 = f32[512]{0:T(512)S(1)} all-reduce(f32[512]{0:T(512)S(1)} %fusion.6), channel_id=1, replica_groups=mesh['row'=8,'col'=8,'space'=2] {'space'}, use_global_device_ids=true, to_apply=%region_5.0 | all-reduce | flops 512 | bytes 4096 | tf_op jit(solution)/shard_map/psum | solution.py:72
  458.9 1.5 collective-permute-start.3
  460.4 4.2 collective-permute-done.3
  464.6 5.7 %collective-permute-done.4 = f32[512]{0:T(512)S(1)} collective-permute-done((f32[512]{0:T(512)S(1)}, f32[512]{0:T(512)S(1)}, u32[]{:S(2)}, u32[]{:S(2)}) %collective-permute-start.4) | collective-permute-done | bytes 2080 | tf_op jit(solution)/shard_map/ppermute | solution.py:19
  470.4 3.0 rsqrt_multiply_fusion
  (18 shorter events, 4.3 us)
Async XLA Ops:
  6.5 444.2 %all-reduce.2.cloned.1.call-start = ((), (), s32[]{:S(2)}) async-start(), calls=%async_computation | async-start | bytes 6291456 | tf_op jit(solution)/shard_map/psum | solution.py:68
  10.3 45.5 %collective-permute-start = (bf16[239,4096]{1,0:T(8,128)(2,1)S(1)}, bf16[239,4096]{1,0:T(8,128)(2,1)S(1)}, u32[]{:S(2)}, u32[]{:S(2)}) collective-permute-start(bf16[239,4096]{1,0:T(8,128)(2,1)S(1)} %slice.244), channel_id=1, source_target_pairs={{0,2},{2,4},{4,6},{6,8},{8,10},{10,12},{12,14},{14,16},{16,18},{18... | collective-permute-start | bytes 5873672 | tf_op jit(solution)/shard_map/ppermute | solution.py:13
  59.7 136.9 %collective-permute-start.1 = (bf16[751,4096]{1,0:T(8,128)(2,1)}, bf16[751,4096]{1,0:T(8,128)(2,1)S(1)}, u32[]{:S(2)}, u32[]{:S(2)}) collective-permute-start(bf16[751,4096]{1,0:T(8,128)(2,1)} %pad_maximum_fusion), channel_id=1, source_target_pairs={{14,0},{0,2},{2,4},{4,6},{6,8},{8,10},{10,12},{12,14},{15,1},{1,3}... | collective-permute-start | bytes 18456584 | tf_op jit(solution)/shard_map/ppermute | solution.py:19
  196.6 137.3 %collective-permute-start.2 = (bf16[751,4096]{1,0:T(8,128)(2,1)S(1)}, bf16[751,4096]{1,0:T(8,128)(2,1)}, u32[]{:S(2)}, u32[]{:S(2)}) collective-permute-start(bf16[751,4096]{1,0:T(8,128)(2,1)S(1)} %collective-permute-done.1), channel_id=1, source_target_pairs={{14,0},{0,2},{2,4},{4,6},{6,8},{8,10},{10,12},{12,14},{15,1},{1,3}... | collective-permute-start | bytes 18456584 | tf_op jit(solution)/shard_map/ppermute | solution.py:19
  351.6 1.4 copy-start
  351.6 1.9 copy-start.1
  353.5 1.2 copy-start.2
  458.9 5.7 %collective-permute-start.3 = (f32[512]{0:T(512)S(1)}, f32[512]{0:T(512)S(1)}, u32[]{:S(2)}, u32[]{:S(2)}) collective-permute-start(f32[512]{0:T(512)S(1)} %psum.15), channel_id=1, source_target_pairs={{14,0},{0,2},{2,4},{4,6},{6,8},{8,10},{10,12},{12,14},{15,1},{1,3}... | collective-permute-start | bytes 6152 | tf_op jit(solution)/shard_map/ppermute | solution.py:19
  464.6 5.7 %collective-permute-start.4 = (f32[512]{0:T(512)S(1)}, f32[512]{0:T(512)S(1)}, u32[]{:S(2)}, u32[]{:S(2)}) collective-permute-start(f32[512]{0:T(512)S(1)} %collective-permute-done.3), channel_id=1, source_target_pairs={{14,0},{0,2},{2,4},{4,6},{6,8},{8,10},{10,12},{12,14},{15,1},{1,3}... | collective-permute-start | bytes 6152 | tf_op jit(solution)/shard_map/ppermute | solution.py:19
Sparse Core Ops, SparseCore 0:
  356.9 93.7 all-reduce.1
where the time goes:
time: 489 us; the launch traced here: 480 us
  waiting for transfers between devices  387 us (79%)
  other arithmetic  37 us (8%)
  matrix products  17.9 us (4%)
  between operations  14.5 us (3%)
  local copies, waits for them, and re-layouts  9.09 us (2%)
  starting transfers between devices  8.19 us (2%)
  blocking collectives  6.43 us (1%)
    ppermute x4, waiting for transfers between devices, shifted(): return lax.ppermute(block, axis, route)  252 us
    psum x1, waiting for transfers between devices, per_device(): summed_dist = lax.psum(partial_dist, 'space')  93.3 us
    ppermute x1, waiting for transfers between devices, passed_along(): return lax.ppermute(block, axis, route)  42.1 us
    dot_general x3, matrix products, per_device(): lax.dot_general(own_rows, partner, (((1,), (1,)), ((), ())), preferred_el...  17.9 us
    add x18, other arithmetic, combine_lags(): return earlier[-keep:, -keep:] + later[:keep, :keep]  13.6 us
  transfers between devices with their start and end apart: 6, of which 6 were waited for; matrix products, arithmetic and copies ran while one was open for 6% of the time, Pallas kernels for 0%

commit v1 on v0

v1 whole, which is shorter than its diff:
```python
import jax
import jax.numpy as jnp
from jax import lax
from jax.sharding import PartitionSpec as P

LAG = 240
BANDS = 3


def ring(axis, distance):
    n = lax.axis_size(axis)
    return [(i, (i + distance) % n) for i in range(n)]


def combine_lags(earlier, later, extent):
    keep = earlier.shape[0] + later.shape[0] - extent - 1
    return earlier[-keep:, -keep:] + later[:keep, :keep]


def lag_sum(distance, window):
    extent = distance.shape[0]
    summed = None
    doubled = distance
    remaining = window
    while remaining:
        if remaining % 2 == 1:
            summed = doubled if summed is None else combine_lags(summed, doubled, extent)
        remaining = remaining // 2
        if remaining:
            doubled = combine_lags(doubled, doubled, extent)
    return summed


def square_norms(values):
    return jnp.sum(jnp.square(values.astype(jnp.float32)), axis=1)


def lagged_partial(rows, cols):
    gram_tile = lax.dot_general(
        rows, cols, (((1,), (1,)), ((), ())), preferred_element_type=jnp.float32
    )
    distance = square_norms(rows)[:, None] + square_norms(cols)[None, :] - 2.0 * gram_tile
    return lag_sum(distance, LAG)


def per_device(snapshots, ocean_mask, spread):
    block_rows = snapshots.shape[0]
    cells_dev = snapshots.shape[1]
    hist = LAG - 1
    n_col = lax.axis_size("col")
    n_row = lax.axis_size("row")
    slot = lax.axis_index("col")
    masked = snapshots * ocean_mask.astype(jnp.bfloat16)[None, :]
    tail = masked[block_rows - hist :]
    head = masked[: block_rows - hist]

    flat = ("row", "col")
    to_slot0 = [(n_col * r - 1, n_col * r) for r in range(1, n_row)]
    to_slot7 = [(n_col * r - 1, n_col * r + n_col - 1) for r in range(1, n_row)]
    tail_to_first = lax.ppermute(tail, flat, to_slot0)
    tail_to_last = lax.ppermute(tail, flat, to_slot7)

    up = ring("col", 1)
    down = ring("col", -1)
    tail_prev = lax.ppermute(tail, "col", up)
    own_hist = jnp.where(slot == 0, tail_to_first, tail_prev)
    hist_prev = lax.ppermute(own_hist, "col", up)
    head_prev = lax.ppermute(head, "col", up)
    block_next = lax.ppermute(masked, "col", down)
    hist_next = jnp.where(slot == n_col - 1, tail_to_last, tail)

    own_rows = jnp.concatenate([own_hist, masked], axis=0)
    prev_rows = jnp.concatenate([hist_prev, head_prev, tail_prev], axis=0)
    next_rows = jnp.concatenate([hist_next, block_next], axis=0)

    band0 = lagged_partial(own_rows, own_rows)
    band1 = lagged_partial(own_rows, prev_rows)
    band2_next = lagged_partial(next_rows, prev_rows)
    partial_dist = jnp.stack([band0, band1, band2_next])

    n_space = lax.axis_size("space")
    column_width = block_rows // n_space
    side = lax.axis_index("space")
    start_col = side * column_width
    other_col = (1 - side) * column_width
    mine = lax.dynamic_slice_in_dim(partial_dist, start_col, column_width, 2)
    theirs = lax.dynamic_slice_in_dim(partial_dist, other_col, column_width, 2)
    summed = mine + lax.ppermute(theirs, "space", [(0, 1), (1, 0)])
    band2 = lax.ppermute(summed[2], "col", up)
    lagged = jnp.stack([summed[0], summed[1], band2])

    total_cells = cells_dev * n_space
    kernel = jnp.exp(-lagged / (LAG * total_cells * spread))
    degree = lax.psum(jnp.sum(kernel, axis=(0, 2)), "space")
    degree_half = lax.dynamic_slice_in_dim(degree, start_col, column_width, 0)
    degree_list = [degree_half]
    for offset in range(1, BANDS):
        degree_list.append(lax.ppermute(degree_half, "col", ring("col", offset)))
    column_degrees = jnp.stack(degree_list)
    factor = float(BANDS * block_rows)
    return factor * kernel / jnp.sqrt(degree[None, :, None] * column_degrees[:, None, :])


def solution(mesh):
    placed = (P(("row", "col"), "space"), P("space"), P())
    return jax.shard_map(
        per_device,
        mesh=mesh,
        in_specs=placed,
        out_specs=P(None, ("row", "col"), "space"),
        check_vma=False,
    )
```

time: 489 us -> 299 us (0.61)
  waiting for transfers between devices: 387 us -> 186 us
  between operations: 14.5 us -> 1.12 us
  local copies, waits for them, and re-layouts: 9.09 us -> 22.1 us
  matrix products: 17.9 us -> 25.6 us
  starting transfers between devices: 8.19 us -> 14 us
    ppermute x5 -> x10, waiting for transfers between devices: 294 us -> 186 us  [the longest x1 65.3 us: per_device(): head_prev = lax.ppermute(head, 'col', up)]
    psum x1 -> x0, waiting for transfers between devices: 93.3 us -> none  [per_device(): summed_dist = lax.psum(partial_dist, 'space')]
    dot_general x3, matrix products: 17.9 us -> 25.6 us  [lagged_partial(): lax.dot_general(rows, cols, (((1,), (1,)), ((), ())), preferred_element_t...]
    slice x1 -> x3, local copies, waits for them, and re-layouts: 0.58 us -> 7.9 us  [the longest x1 3.3 us: per_device(): head = masked[:block_rows - hist]]
    ppermute x5 -> x10, starting transfers between devices: 8.19 us -> 14 us  [the longest x1 5.2 us: per_device(): block_next = lax.ppermute(masked, 'col', down)]
    reduce_sum x3, other arithmetic: 7.56 us -> 12.6 us  [square_norms(): return jnp.sum(jnp.square(values.astype(jnp.float32)), axis=1)]
  transfers between devices with their start and end apart: 6 -> 10, of which waited for: 6 -> 6; matrix products, arithmetic and copies ran while one was open for 6% -> 17% of each run, Pallas kernels for 0% -> 0%
where the time goes in v1:
time: 299 us; the launch traced here: 295 us
  waiting for transfers between devices  186 us (62%)
  other arithmetic  39.6 us (13%)
  matrix products  25.6 us (9%)
  local copies, waits for them, and re-layouts  22.1 us (7%)
  starting transfers between devices  14 us (5%)
  blocking collectives  6.43 us (2%)
    ppermute x1, waiting for transfers between devices, per_device(): head_prev = lax.ppermute(head, 'col', up)  65.3 us
    ppermute x1, waiting for transfers between devices, per_device(): tail_prev = lax.ppermute(tail, 'col', up)  56 us
    ppermute x1, waiting for transfers between devices, per_device(): summed = mine + lax.ppermute(theirs, 'space', [(0, 1), (1, 0)])  28.4 us
    dot_general x3, matrix products, lagged_partial(): lax.dot_general(rows, cols, (((1,), (1,)), ((), ())), preferred_element_t...  25.6 us
    ppermute x1, waiting for transfers between devices, per_device(): hist_prev = lax.ppermute(own_hist, 'col', up)  21.4 us
    add x18, other arithmetic, combine_lags(): return earlier[-keep:, -keep:] + later[:keep, :keep]  13.3 us
    reduce_sum x3, other arithmetic, square_norms(): return jnp.sum(jnp.square(values.astype(jnp.float32)), axis=1)  12.6 us
    ppermute x1, waiting for transfers between devices, per_device(): band2 = lax.ppermute(summed[2], 'col', up)  9.33 us
  transfers between devices with their start and end apart: 10, of which 6 were waited for; matrix products, arithmetic and copies ran while one was open for 17% of the time, Pallas kernels for 0%

profile of v1, /device:TPU:4, one launch (start us, length us, event | category | flops | bytes accessed | tf_op | source)
XLA Modules:
  0.0 295.2 jit_solution(6695025749173172026)
XLA Ops:
  0.0 0.7 convert_element_type.15
  0.7 4.4 %broadcast_multiply_fusion = bf16[512,4096]{1,0:T(8,128)(2,1)} fusion(bf16[512,4096]{1,0:T(8,128)(2,1)} %param.3, bf16[4096]{0:T(1024)(128)(2,1)S(1)} %convert_element_type.15), kind=kLoop, calls=%fused_computation.29 | loop fusion | flops 2097152 | bytes 8396800 | tf_op jit(solution)/shard_map/mul | solution.py:53
  5.1 3.3 %slice.258 = bf16[239,4096]{1,0:T(8,128)(2,1)} slice(bf16[512,4096]{1,0:T(8,128)(2,1)} %broadcast_multiply_fusion), slice={[273:512], [0:4096]} | slice | bytes 3915776 | tf_op jit(solution)/shard_map/slice | solution.py:54
  8.4 1.6 collective-permute-start.1
  10.0 1.3 collective-permute-start
  11.3 5.2 %collective-permute-start.5 = (bf16[512,4096]{1,0:T(8,128)(2,1)}, bf16[512,4096]{1,0:T(8,128)(2,1)}, u32[]{:S(2)}, u32[]{:S(2)}) collective-permute-start(bf16[512,4096]{1,0:T(8,128)(2,1)} %broadcast_multiply_fusion), channel_id=1, source_target_pairs={{0,14},{2,0},{4,2},{6,4},{8,6},{10,8},{12,10},{14,12},{1,15},{3,1}... | collective-permute-start | bytes 12582920 | tf_op jit(solution)/shard_map/ppermute | solution.py:69
  16.5 1.9 collective-permute-start.4
  18.4 3.3 %slice.283 = bf16[273,4096]{1,0:T(8,128)(2,1)} slice(bf16[512,4096]{1,0:T(8,128)(2,1)} %broadcast_multiply_fusion), slice={[0:273], [0:4096]} | slice | bytes 4472832 | tf_op jit(solution)/shard_map/slice | solution.py:55
  21.7 56.0 %collective-permute-done.1 = bf16[239,4096]{1,0:T(8,128)(2,1)S(1)} collective-permute-done((bf16[239,4096]{1,0:T(8,128)(2,1)}, bf16[239,4096]{1,0:T(8,128)(2,1)S(1)}, u32[]{:S(2)}, u32[]{:S(2)}) %collective-permute-start.1) | collective-permute-done | bytes 1957920 | tf_op jit(solution)/shard_map/ppermute | solution.py:65
  77.7 1.8 broadcast_select_fusion.1
  79.8 4.4 %multiply_reduce_fusion.2 = f32[751]{0:T(1024)S(1)} fusion(bf16[512,4096]{1,0:T(8,128)(2,1)} %broadcast_multiply_fusion, bf16[239,4096]{1,0:T(8,128)(2,1)S(1)} %broadcast_select_fusion.1), kind=kLoop, calls=%fused_computation.2 | loop fusion | flops 18455824 | bytes 6155196 | tf_op jit(solution)/shard_map/reduce_sum | solution.py:35
  84.2 8.5 %multiply_subtract_fusion.2 = f32[751,751]{0,1:T(8,128)S(1)} fusion(bf16[512,4096]{1,0:T(8,128)(2,1)} %broadcast_multiply_fusion, bf16[239,4096]{1,0:T(8,128)(2,1)S(1)} %broadcast_select_fusion.1, f32[751]{0:T(1024)S(1)} %multiply_reduce_fusion.2), kind=kOutput, calls=%fused_computation.16 | convolution fusion | flops 4634293248 | bytes 8411200 | tf_op jit(solution)/shard_map/dot_general | solution.py:39
  92.6 0.9 slice_add_fusion.5
  93.5 0.8 slice_add_fusion.4
  94.4 0.8 slice_add_fusion.8
  95.2 0.6 slice_add_fusion.11
  98.2 0.9 fusion.15
  99.1 2.1 broadcast_select_fusion
  101.2 1.3 fusion.10
  102.5 65.3 %collective-permute-done.3 = bf16[273,4096]{1,0:T(8,128)(2,1)} collective-permute-done((bf16[273,4096]{1,0:T(8,128)(2,1)}, bf16[273,4096]{1,0:T(8,128)(2,1)}, u32[]{:S(2)}, u32[]{:S(2)}) %collective-permute-start.3) | collective-permute-done | bytes 2236448 | tf_op jit(solution)/shard_map/ppermute | solution.py:68
  167.8 21.4 %collective-permute-done.2 = bf16[239,4096]{1,0:T(8,128)(2,1)S(1)} collective-permute-done((bf16[239,4096]{1,0:T(8,128)(2,1)S(1)}, bf16[239,4096]{1,0:T(8,128)(2,1)S(1)}, u32[]{:S(2)}, u32[]{:S(2)}) %collective-permute-start.2) | collective-permute-done | bytes 1957920 | tf_op jit(solution)/shard_map/ppermute | solution.py:67
  189.2 1.3 copy-done.4
  190.5 3.7 %multiply_reduce_fusion.1 = f32[751]{0:T(1024)S(1)} fusion(bf16[239,4096]{1,0:T(8,128)(2,1)S(1)} %collective-permute-done.1, bf16[273,4096]{1,0:T(8,128)(2,1)} %collective-permute-done.3, bf16[239,4096]{1,0:T(8,128)(2,1)S(1)} %collective-permute-done.2), kind=kLoop, calls=%fused_computation.1 | loop fusion | flops 24608016 | bytes 6155196 | tf_op jit(solution)/shard_map/reduce_sum | solution.py:35
  194.3 8.5 %multiply_subtract_fusion.1 = f32[751,751]{0,1:T(8,128)S(1)} fusion(bf16[512,4096]{1,0:T(8,128)(2,1)} %broadcast_multiply_fusion, bf16[239,4096]{1,0:T(8,128)(2,1)S(1)} %broadcast_select_fusion.1, f32[751]{0:T(1024)S(1)} %multiply_reduce_fusion.1, f32[751]{0:T(1024)S(1)} %multiply_reduce_fusion.2, bf16[239,4096]{1,0:T(8,128)(2,1)S(1)} %collective-permute-done.1, ...), kind=kOutput, calls=%fused_computation.15 | convolution fusion | flops 4652749824 | bytes 14566396 | tf_op jit(solution)/shard_map/dot_general | solution.py:39
  202.7 0.8 slice_add_fusion.3
  203.6 0.8 slice_add_fusion.2
  204.4 0.8 slice_add_fusion.7
  205.3 0.7 slice_add_fusion.10
  206.4 0.6 slice_add_fusion.13
  208.3 2.2 fusion.16
  210.5 4.4 %multiply_reduce_fusion = f32[751]{0:T(1024)S(1)} fusion(bf16[512,4096]{1,0:T(8,128)(2,1)} %collective-permute-done.5, bf16[239,4096]{1,0:T(8,128)(2,1)S(1)} %broadcast_select_fusion), kind=kLoop, calls=%fused_computation | loop fusion | flops 18455824 | bytes 6155196 | tf_op jit(solution)/shard_map/reduce_sum | solution.py:35
  214.9 8.7 %multiply_subtract_fusion = f32[751,751]{0,1:T(8,128)S(1)} fusion(bf16[512,4096]{1,0:T(8,128)(2,1)} %collective-permute-done.5, bf16[239,4096]{1,0:T(8,128)(2,1)S(1)} %broadcast_select_fusion, f32[751]{0:T(1024)S(1)} %multiply_reduce_fusion, f32[751]{0:T(1024)S(1)} %multiply_reduce_fusion.1, bf16[239,4096]{1,0:T(8,128)(2,1)S(1)} %collective-permute-done.1, ...), kind=kOutput, calls=%fused_computation.14 | convolution fusion | flops 4652749824 | bytes 14566396 | tf_op jit(solution)/shard_map/dot_general | solution.py:39
  223.5 0.8 slice_add_fusion.1
  224.4 0.8 slice_add_fusion
  225.3 0.8 slice_add_fusion.6
  226.1 0.7 slice_add_fusion.9
  229.6 0.9 copy-done.1
  231.0 0.7 fusion.6
  232.6 1.3 constant_dynamic-slice_fusion
  233.8 3.6 %collective-permute-start.6 = (f32[3,512,256]{1,2,0:T(8,128)}, f32[3,512,256]{1,2,0:T(8,128)}, u32[]{:S(2)}, u32[]{:S(2)}) collective-permute-start(f32[3,512,256]{1,2,0:T(8,128)} %constant_dynamic-slice_fusion), channel_id=1, source_target_pairs={{0,1},{1,0},{2,3},{3,2},{4,5},{5,4},{6,7},{7,6},{8,9},{9,8},{10,11... | collective-permute-start | bytes 4718600 | tf_op jit(solution)/shard_map/ppermute | solution.py:88
  237.4 28.4 %collective-permute-done.6 = f32[3,512,256]{1,2,0:T(8,128)} collective-permute-done((f32[3,512,256]{1,2,0:T(8,128)}, f32[3,512,256]{1,2,0:T(8,128)}, u32[]{:S(2)}, u32[]{:S(2)}) %collective-permute-start.6) | collective-permute-done | bytes 1572896 | tf_op jit(solution)/shard_map/ppermute | solution.py:88
  265.8 1.8 dynamic-slice_add_fusion
  267.6 1.1 copy-done
  269.5 1.3 slice.332
  270.8 9.3 %collective-permute-done.7 = f32[512,256]{0,1:T(8,128)S(1)} collective-permute-done((f32[512,256]{0,1:T(8,128)S(1)}, f32[512,256]{0,1:T(8,128)S(1)}, u32[]{:S(2)}, u32[]{:S(2)}) %collective-permute-start.7) | collective-permute-done | bytes 524320 | tf_op jit(solution)/shard_map/ppermute | solution.py:89
  280.4 6.4 %psum.7 = f32[512]{0:T(512)S(1)} all-reduce(f32[512]{0:T(512)S(1)} %fusion.11), channel_id=1, replica_groups=mesh['row'=8,'col'=8,'space'=2] {'space'}, use_global_device_ids=true, to_apply=%region_4.5 | all-reduce | flops 512 | bytes 4096 | tf_op jit(solution)/shard_map/psum | solution.py:94
  287.0 5.9 %collective-permute-done.9 = f32[256]{0:T(256)S(1)} collective-permute-done((f32[256]{0:T(256)S(1)}, f32[256]{0:T(256)S(1)}, u32[]{:S(2)}, u32[]{:S(2)}) %collective-permute-start.9) | collective-permute-done | bytes 1056 | tf_op jit(solution)/shard_map/ppermute | solution.py:98
  293.4 1.6 copy.4
  (37 shorter events, 9.5 us)
Async XLA Ops:
  8.4 69.3 %collective-permute-start.1 = (bf16[239,4096]{1,0:T(8,128)(2,1)}, bf16[239,4096]{1,0:T(8,128)(2,1)S(1)}, u32[]{:S(2)}, u32[]{:S(2)}) collective-permute-start(bf16[239,4096]{1,0:T(8,128)(2,1)} %slice.258), channel_id=1, source_target_pairs={{0,2},{2,4},{4,6},{6,8},{8,10},{10,12},{12,14},{14,0},{1,3},{3,5},... | collective-permute-start | bytes 5873672 | tf_op jit(solution)/shard_map/ppermute | solution.py:65
  10.0 67.7 %collective-permute-start = (bf16[239,4096]{1,0:T(8,128)(2,1)}, bf16[239,4096]{1,0:T(8,128)(2,1)}, u32[]{:S(2)}, u32[]{:S(2)}) collective-permute-start(bf16[239,4096]{1,0:T(8,128)(2,1)} %slice.258), channel_id=1, source_target_pairs={{14,16},{30,32},{46,48},{62,64},{78,80},{94,96},{110,112},{15,17},... | collective-permute-start | bytes 5873672 | tf_op jit(solution)/shard_map/ppermute | solution.py:60
  11.3 199.2 %collective-permute-start.5 = (bf16[512,4096]{1,0:T(8,128)(2,1)}, bf16[512,4096]{1,0:T(8,128)(2,1)}, u32[]{:S(2)}, u32[]{:S(2)}) collective-permute-start(bf16[512,4096]{1,0:T(8,128)(2,1)} %broadcast_multiply_fusion), channel_id=1, source_target_pairs={{0,14},{2,0},{4,2},{6,4},{8,6},{10,8},{12,10},{14,12},{1,15},{3,1}... | collective-permute-start | bytes 12582920 | tf_op jit(solution)/shard_map/ppermute | solution.py:69
  16.5 82.6 %collective-permute-start.4 = (bf16[239,4096]{1,0:T(8,128)(2,1)}, bf16[239,4096]{1,0:T(8,128)(2,1)}, u32[]{:S(2)}, u32[]{:S(2)}) collective-permute-start(bf16[239,4096]{1,0:T(8,128)(2,1)} %slice.258), channel_id=1, source_target_pairs={{14,30},{30,46},{46,62},{62,78},{78,94},{94,110},{110,126},{15,31}... | collective-permute-start | bytes 5873672 | tf_op jit(solution)/shard_map/ppermute | solution.py:61
  21.7 146.1 %collective-permute-start.3 = (bf16[273,4096]{1,0:T(8,128)(2,1)}, bf16[273,4096]{1,0:T(8,128)(2,1)}, u32[]{:S(2)}, u32[]{:S(2)}) collective-permute-start(bf16[273,4096]{1,0:T(8,128)(2,1)} %slice.283), channel_id=1, source_target_pairs={{0,2},{2,4},{4,6},{6,8},{8,10},{10,12},{12,14},{14,0},{1,3},{3,5},... | collective-permute-start | bytes 6709256 | tf_op jit(solution)/shard_map/ppermute | solution.py:68
  79.5 109.7 %collective-permute-start.2 = (bf16[239,4096]{1,0:T(8,128)(2,1)S(1)}, bf16[239,4096]{1,0:T(8,128)(2,1)S(1)}, u32[]{:S(2)}, u32[]{:S(2)}) collective-permute-start(bf16[239,4096]{1,0:T(8,128)(2,1)S(1)} %broadcast_select_fusion.1), channel_id=1, source_target_pairs={{0,2},{2,4},{4,6},{6,8},{8,10},{10,12},{12,14},{14,0},{1,3},{3,5},... | collective-permute-start | bytes 5873672 | tf_op jit(solution)/shard_map/ppermute | solution.py:67
  189.2 1.3 copy-start.4
  229.1 1.4 copy-start.1
  229.1 1.9 copy-start.2
  231.0 1.2 copy-start.3
  233.8 32.0 %collective-permute-start.6 = (f32[3,512,256]{1,2,0:T(8,128)}, f32[3,512,256]{1,2,0:T(8,128)}, u32[]{:S(2)}, u32[]{:S(2)}) collective-permute-start(f32[3,512,256]{1,2,0:T(8,128)} %constant_dynamic-slice_fusion), channel_id=1, source_target_pairs={{0,1},{1,0},{2,3},{3,2},{4,5},{5,4},{6,7},{7,6},{8,9},{9,8},{10,11... | collective-permute-start | bytes 4718600 | tf_op jit(solution)/shard_map/ppermute | solution.py:88
  267.6 1.1 copy-start
  268.8 11.4 %collective-permute-start.7 = (f32[512,256]{0,1:T(8,128)S(1)}, f32[512,256]{0,1:T(8,128)S(1)}, u32[]{:S(2)}, u32[]{:S(2)}) collective-permute-start(f32[512,256]{0,1:T(8,128)S(1)} %slice_bitcast_fusion), channel_id=1, source_target_pairs={{0,2},{2,4},{4,6},{6,8},{8,10},{10,12},{12,14},{14,0},{1,3},{3,5},... | collective-permute-start | bytes 1572872 | tf_op jit(solution)/shard_map/ppermute | solution.py:89
  287.0 6.0 %collective-permute-start.9 = (f32[256]{0:T(256)S(1)}, f32[256]{0:T(256)S(1)}, u32[]{:S(2)}, u32[]{:S(2)}) collective-permute-start(f32[256]{0:T(256)S(1)} %dynamic_slice.11), channel_id=1, source_target_pairs={{0,4},{2,6},{4,8},{6,10},{8,12},{10,14},{12,0},{14,2},{1,5},{3,7},... | collective-permute-start | bytes 3080 | tf_op jit(solution)/shard_map/ppermute | solution.py:98
  287.0 6.0 %collective-permute-start.8 = (f32[256]{0:T(256)S(1)}, f32[256]{0:T(256)S(1)}, u32[]{:S(2)}, u32[]{:S(2)}) collective-permute-start(f32[256]{0:T(256)S(1)} %dynamic_slice.11), channel_id=1, source_target_pairs={{0,2},{2,4},{4,6},{6,8},{8,10},{10,12},{12,14},{14,0},{1,3},{3,5},... | collective-permute-start | bytes 3080 | tf_op jit(solution)/shard_map/ppermute | solution.py:98

commit v2 on v1

--- a/solution.py
+++ b/solution.py
@@ -50,9 +50,8 @@
     n_col = lax.axis_size("col")
     n_row = lax.axis_size("row")
     slot = lax.axis_index("col")
-    masked = snapshots * ocean_mask.astype(jnp.bfloat16)[None, :]
-    tail = masked[block_rows - hist :]
-    head = masked[: block_rows - hist]
+    mask = ocean_mask.astype(jnp.bfloat16)[None, :]
+    tail = snapshots[block_rows - hist :]
 
     flat = ("row", "col")
     to_slot0 = [(n_col * r - 1, n_col * r) for r in range(1, n_row)]
@@ -62,40 +61,50 @@
 
     up = ring("col", 1)
     down = ring("col", -1)
-    tail_prev = lax.ppermute(tail, "col", up)
-    own_hist = jnp.where(slot == 0, tail_to_first, tail_prev)
+    block_prev = lax.ppermute(snapshots, "col", up)
+    block_next = lax.ppermute(snapshots, "col", down)
+    own_hist = jnp.where(slot == 0, tail_to_first, block_prev[block_rows - hist :])
     hist_prev = lax.ppermute(own_hist, "col", up)
-    head_prev = lax.ppermute(head, "col", up)
-    block_next = lax.ppermute(masked, "col", down)
     hist_next = jnp.where(slot == n_col - 1, tail_to_last, tail)
 
-    own_rows = jnp.concatenate([own_hist, masked], axis=0)
-    prev_rows = jnp.concatenate([hist_prev, head_prev, tail_prev], axis=0)
-    next_rows = jnp.concatenate([hist_next, block_next], axis=0)
+    own_rows = jnp.concatenate([own_hist, snapshots], axis=0) * mask
+    prev_rows = jnp.concatenate([hist_prev, block_prev], axis=0) * mask
+    next_rows = jnp.concatenate([hist_next, block_next], axis=0) * mask
 
     band0 = lagged_partial(own_rows, own_rows)
     band1 = lagged_partial(own_rows, prev_rows)
     band2_next = lagged_partial(next_rows, prev_rows)
-    partial_dist = jnp.stack([band0, band1, band2_next])
 
     n_space = lax.axis_size("space")
     column_width = block_rows // n_space
     side = lax.axis_index("space")
     start_col = side * column_width
     other_col = (1 - side) * column_width
-    mine = lax.dynamic_slice_in_dim(partial_dist, start_col, column_width, 2)
-    theirs = lax.dynamic_slice_in_dim(partial_dist, other_col, column_width, 2)
-    summed = mine + lax.ppermute(theirs, "space", [(0, 1), (1, 0)])
-    band2 = lax.ppermute(summed[2], "col", up)
+    swap = [(0, 1), (1, 0)]
+    own_bands = jnp.stack([band0, band1])
+    mine = lax.dynamic_slice_in_dim(own_bands, start_col, column_width, 2)
+    theirs = lax.dynamic_slice_in_dim(own_bands, other_col, column_width, 2)
+    summed = mine + lax.ppermute(theirs, "space", swap)
+
+    cs = ("col", "space")
+    same_side = [(n_space * c + p, n_space * ((c + 1) % n_col) + p) for c in range(n_col) for p in range(n_space)]
+    cross_side = [(n_space * c + p, n_space * ((c + 1) % n_col) + 1 - p) for c in range(n_col) for p in range(n_space)]
+    b2_same = lax.ppermute(lax.dynamic_slice_in_dim(band2_next, start_col, column_width, 1), cs, same_side)
+    b2_cross = lax.ppermute(lax.dynamic_slice_in_dim(band2_next, other_col, column_width, 1), cs, cross_side)
+    band2 = b2_same + b2_cross
     lagged = jnp.stack([summed[0], summed[1], band2])
 
     total_cells = cells_dev * n_space
     kernel = jnp.exp(-lagged / (LAG * total_cells * spread))
-    degree = lax.psum(jnp.sum(kernel, axis=(0, 2)), "space")
-    degree_half = lax.dynamic_slice_in_dim(degree, start_col, column_width, 0)
-    degree_list = [degree_half]
+    part_degree = jnp.sum(kernel, axis=(0, 2))
+    degree = part_degree + lax.ppermute(part_degree, "space", swap)
+    degree_list = [lax.dynamic_slice_in_dim(degree, start_col, column_width, 0)]
     for offset in range(1, BANDS):
-        degree_list.append(lax.ppermute(degree_half, "col", ring("col", offset)))
+        shift_same = [(n_space * c + p, n_space * ((c + offset) % n_col) + p) for c in range(n_col) for p in range(n_space)]
+        shift_cross = [(n_space * c + p, n_space * ((c + offset) % n_col) + 1 - p) for c in range(n_col) for p in range(n_space)]
+        d_same = lax.ppermute(lax.dynamic_slice_in_dim(part_degree, start_col, column_width, 0), cs, shift_same)
+        d_cross = lax.ppermute(lax.dynamic_slice_in_dim(part_degree, other_col, column_width, 0), cs, shift_cross)
+        degree_list.append(d_same + d_cross)
     column_degrees = jnp.stack(degree_list)
     factor = float(BANDS * block_rows)
     return factor * kernel / jnp.sqrt(degree[None, :, None] * column_degrees[:, None, :])

time: 299 us -> 301 us (level)
  the two profiles are of different devices: /device:TPU:4 before, /device:TPU:39 now
where the time goes in v2:
time: 301 us; the launch traced here: 296 us
  waiting for transfers between devices  159 us (53%)
  starting transfers between devices  60.2 us (20%)
  other arithmetic  31.1 us (10%)
  matrix products  23.9 us (8%)
  local copies, waits for them, and re-layouts  20.7 us (7%)
    ppermute x1, waiting for transfers between devices, per_device(): block_prev = lax.ppermute(snapshots, 'col', up)  82.8 us
    ppermute x1, waiting for transfers between devices, per_device(): hist_prev = lax.ppermute(own_hist, 'col', up)  42.8 us
    ppermute x2, starting transfers between devices, per_device(): lax.ppermute(lax.dynamic_slice_in_dim(part_degree, start_col, column_widt...  34.7 us
    dot_general x3, matrix products, lagged_partial(): lax.dot_general(rows, cols, (((1,), (1,)), ((), ())), preferred_element_t...  23.9 us
    ppermute x1, waiting for transfers between devices, per_device(): lax.ppermute(lax.dynamic_slice_in_dim(band2_next, other_col, column_width...  16.7 us
    ppermute x2, starting transfers between devices, per_device(): lax.ppermute(lax.dynamic_slice_in_dim(part_degree, other_col, column_widt...  15.9 us
    add x19, other arithmetic, combine_lags(): return earlier[-keep:, -keep:] + later[:keep, :keep]  13.7 us
    ppermute x1, waiting for transfers between devices, per_device(): lax.ppermute(lax.dynamic_slice_in_dim(band2_next, start_col, column_width...  12.4 us
  transfers between devices with their start and end apart: 13, of which 6 were waited for; matrix products, arithmetic and copies ran while one was open for 4% of the time, Pallas kernels for 0%

profile of v2, /device:TPU:39, one launch (start us, length us, event | category | flops | bytes accessed | tf_op | source)
XLA Modules:
  0.0 296.5 jit_solution(9105049909301936969)
XLA Ops:
  0.0 1.3 collective-permute-start.1
  1.3 3.4 %slice.189 = bf16[239,4096]{1,0:T(8,128)(2,1)} slice(bf16[512,4096]{1,0:T(8,128)(2,1)} %param.3), slice={[273:512], [0:4096]} | slice | bytes 3915776 | tf_op jit(solution)/shard_map/slice | solution.py:54
  4.7 0.8 collective-permute-start
  5.5 2.3 collective-permute-start.5
  7.8 1.9 collective-permute-start.4
  9.7 1.3 copy-done.8
  11.1 82.8 %collective-permute-done.1 = bf16[512,4096]{1,0:T(8,128)(2,1)} collective-permute-done((bf16[512,4096]{1,0:T(8,128)(2,1)}, bf16[512,4096]{1,0:T(8,128)(2,1)}, u32[]{:S(2)}, u32[]{:S(2)}) %collective-permute-start.1) | collective-permute-done | bytes 4194336 | tf_op jit(solution)/shard_map/ppermute | solution.py:64
  93.9 2.1 slice_select_fusion
  96.1 2.2 broadcast_select_fusion
  98.3 42.8 %collective-permute-done.2 = bf16[239,4096]{1,0:T(8,128)(2,1)} collective-permute-done((bf16[239,4096]{1,0:T(8,128)(2,1)S(1)}, bf16[239,4096]{1,0:T(8,128)(2,1)}, u32[]{:S(2)}, u32[]{:S(2)}) %collective-permute-start.2) | collective-permute-done | bytes 1957920 | tf_op jit(solution)/shard_map/ppermute | solution.py:67
  141.1 9.1 %multiply_reduce_fusion.2 = (f32[751]{0:T(1024)S(1)}, f32[751]{0:T(1024)S(1)}, f32[751]{0:T(1024)S(1)}) fusion(bf16[4096]{0:T(1024)(128)(2,1)S(1)} %convert_element_type.15, bf16[512,4096]{1,0:T(8,128)(2,1)S(1)} %copy-done, bf16[239,4096]{1,0:T(8,128)(2,1)S(1)} %slice_select_fusion, bf16[512,4096]{1,0:T(8,128)(2,1)} %collective-permute-done.1, ...), kind=kLoop, calls=%fused_computation.2 | loop fusion | flops 67671856 | bytes 18473780 | tf_op jit(solution)/shard_map/reduce_sum | solution.py:35
  150.2 9.5 %multiply_subtract_fusion = f32[751,751]{0,1:T(8,128)S(1)} fusion(bf16[512,4096]{1,0:T(8,128)(2,1)} %collective-permute-done.5, bf16[239,4096]{1,0:T(8,128)(2,1)S(1)} %broadcast_select_fusion, bf16[4096]{0:T(1024)(128)(2,1)S(1)} %convert_element_type.15, f32[751]{0:T(1024)S(1)} %get-tuple-element.7, f32[751]{0:T(1024)S(1)} %get-tuple-element.6, ...), kind=kOutput, calls=%fused_computation.18 | convolution fusion | flops 4658902016 | bytes 14574588 | tf_op jit(solution)/shard_map/dot_general | solution.py:39
  159.7 0.9 slice_add_fusion.1
  160.6 0.9 slice_add_fusion
  161.4 0.8 slice_add_fusion.6
  162.3 0.7 slice_add_fusion.9
  162.9 0.6 slice_add_fusion.12
  164.2 2.2 fusion.18
  166.4 1.3 slice.316
  167.7 1.7 slice.313
  169.4 1.7 slice.312
  171.1 8.7 %multiply_subtract_fusion.1 = f32[751,751]{0,1:T(8,128)S(1)} fusion(f32[751]{0:T(1024)S(1)} %get-tuple-element.6, f32[751]{0:T(1024)S(1)} %get-tuple-element.5, bf16[512,4096]{1,0:T(8,128)(2,1)} %collective-permute-done.1, bf16[239,4096]{1,0:T(8,128)(2,1)} %collective-permute-done.2, bf16[4096]{0:T(1024)(128)(2,1)S(1)} %convert_element_type.15, ...), kind=kOutput, calls=%fused_computation.19 | convolution fusion | flops 4658902016 | bytes 14574588 | tf_op jit(solution)/shard_map/dot_general | solution.py:39
  179.8 0.9 slice_add_fusion.3
  180.7 0.9 slice_add_fusion.2
  181.6 0.8 slice_add_fusion.7
  182.4 0.7 slice_add_fusion.10
  183.1 0.6 slice_add_fusion.13
  184.3 2.2 fusion.16
  187.6 5.7 %multiply_subtract_fusion.2 = f32[751,751]{0,1:T(8,128)S(1)} fusion(f32[751]{0:T(1024)S(1)} %get-tuple-element.5, bf16[512,4096]{1,0:T(8,128)(2,1)S(1)} %copy-done, bf16[239,4096]{1,0:T(8,128)(2,1)S(1)} %slice_select_fusion, bf16[4096]{0:T(1024)(128)(2,1)S(1)} %convert_element_type.15), kind=kOutput, calls=%fused_computation.20 | convolution fusion | flops 4640445440 | bytes 8419392 | tf_op jit(solution)/shard_map/dot_general | solution.py:39
  193.3 0.9 slice_add_fusion.5
  194.2 0.8 slice_add_fusion.4
  195.0 0.8 slice_add_fusion.8
  195.9 0.7 slice_add_fusion.11
  196.5 0.6 slice_add_fusion.14
  199.4 0.9 copy-done.4
  200.8 0.7 fusion.9
  201.5 1.0 fusion.4
  202.6 2.7 collective-permute-start.3
  205.6 1.1 constant_dynamic-slice_fusion
  207.6 12.4 %collective-permute-done.6 = f32[512,256]{0,1:T(8,128)} collective-permute-done((f32[512,256]{0,1:T(8,128)}, f32[512,256]{0,1:T(8,128)}, u32[]{:S(2)}, u32[]{:S(2)}) %collective-permute-start.6) | collective-permute-done | bytes 524320 | tf_op jit(solution)/shard_map/ppermute | solution.py:92
  219.9 16.7 %collective-permute-done.7 = f32[512,256]{0,1:T(8,128)} collective-permute-done((f32[512,256]{0,1:T(8,128)}, f32[512,256]{0,1:T(8,128)}, u32[]{:S(2)}, u32[]{:S(2)}) %collective-permute-start.7) | collective-permute-done | bytes 524320 | tf_op jit(solution)/shard_map/ppermute | solution.py:93
  236.6 1.3 add_bitcast_fusion
  238.8 34.7 %collective-permute-start.11 = (f32[256]{0:T(256)S(1)}, f32[256]{0:T(256)S(1)}, u32[]{:S(2)}, u32[]{:S(2)}) collective-permute-start(f32[256]{0:T(256)S(1)} %get-tuple-element.17), channel_id=1, source_target_pairs={{0,4},{1,5},{2,6},{3,7},{4,8},{5,9},{6,10},{7,11},{8,12},{9,13},{1... | collective-permute-start | bytes 3080 | tf_op jit(solution)/shard_map/ppermute | solution.py:105
  273.4 14.0 %collective-permute-start.12 = (f32[256]{0:T(256)S(1)}, f32[256]{0:T(256)S(1)}, u32[]{:S(2)}, u32[]{:S(2)}) collective-permute-start(f32[256]{0:T(256)S(1)} %get-tuple-element.16), channel_id=1, source_target_pairs={{0,5},{1,4},{2,7},{3,6},{4,9},{5,8},{6,11},{7,10},{8,13},{9,12},{1... | collective-permute-start | bytes 3080 | tf_op jit(solution)/shard_map/ppermute | solution.py:106
  287.5 1.9 collective-permute-start.10
  289.4 2.9 collective-permute-done.9
  292.3 1.9 collective-permute-done.10
  294.7 1.6 copy.5
  (51 shorter events, 7.1 us)
Async XLA Ops:
  0.0 93.9 %collective-permute-start.1 = (bf16[512,4096]{1,0:T(8,128)(2,1)}, bf16[512,4096]{1,0:T(8,128)(2,1)}, u32[]{:S(2)}, u32[]{:S(2)}) collective-permute-start(bf16[512,4096]{1,0:T(8,128)(2,1)} %param.3), channel_id=1, source_target_pairs={{0,2},{2,4},{4,6},{6,8},{8,10},{10,12},{12,14},{14,0},{1,3},{3,5},... | collective-permute-start | bytes 12582920 | tf_op jit(solution)/shard_map/ppermute | solution.py:64
  4.7 5.1 %collective-permute-start = (bf16[239,4096]{1,0:T(8,128)(2,1)}, bf16[239,4096]{1,0:T(8,128)(2,1)S(1)}, u32[]{:S(2)}, u32[]{:S(2)}) collective-permute-start(bf16[239,4096]{1,0:T(8,128)(2,1)} %slice.189), channel_id=1, source_target_pairs={{14,16},{30,32},{46,48},{62,64},{78,80},{94,96},{110,112},{15,17},... | collective-permute-start | bytes 5873672 | tf_op jit(solution)/shard_map/ppermute | solution.py:59
  5.5 92.8 %collective-permute-start.5 = (bf16[512,4096]{1,0:T(8,128)(2,1)}, bf16[512,4096]{1,0:T(8,128)(2,1)}, u32[]{:S(2)}, u32[]{:S(2)}) collective-permute-start(bf16[512,4096]{1,0:T(8,128)(2,1)} %param.3), channel_id=1, source_target_pairs={{0,14},{2,0},{4,2},{6,4},{8,6},{10,8},{12,10},{14,12},{1,15},{3,1}... | collective-permute-start | bytes 12582920 | tf_op jit(solution)/shard_map/ppermute | solution.py:65
  7.8 88.3 %collective-permute-start.4 = (bf16[239,4096]{1,0:T(8,128)(2,1)}, bf16[239,4096]{1,0:T(8,128)(2,1)}, u32[]{:S(2)}, u32[]{:S(2)}) collective-permute-start(bf16[239,4096]{1,0:T(8,128)(2,1)} %slice.189), channel_id=1, source_target_pairs={{14,30},{30,46},{46,62},{62,78},{78,94},{94,110},{110,126},{15,31}... | collective-permute-start | bytes 5873672 | tf_op jit(solution)/shard_map/ppermute | solution.py:60
  9.7 86.3 %copy-start.9 = (s32[4096]{0:T(1024)S(1)}, s32[4096]{0:T(1024)}, u32[]{:S(2)}) copy-start(s32[4096]{0:T(1024)} %param.4) | copy-start | bytes 49156
  9.7 1.3 copy-start.8
  95.9 45.1 %collective-permute-start.2 = (bf16[239,4096]{1,0:T(8,128)(2,1)S(1)}, bf16[239,4096]{1,0:T(8,128)(2,1)}, u32[]{:S(2)}, u32[]{:S(2)}) collective-permute-start(bf16[239,4096]{1,0:T(8,128)(2,1)S(1)} %slice_select_fusion), channel_id=1, source_target_pairs={{0,2},{2,4},{4,6},{6,8},{8,10},{10,12},{12,14},{14,0},{1,3},{3,5},... | collective-permute-start | bytes 5873672 | tf_op jit(solution)/shard_map/ppermute | solution.py:67
  96.1 45.0 %copy-start = (bf16[512,4096]{1,0:T(8,128)(2,1)S(1)}, bf16[512,4096]{1,0:T(8,128)(2,1)}, u32[]{:S(2)}) copy-start(bf16[512,4096]{1,0:T(8,128)(2,1)} %param.3) | copy-start | bytes 12582916
  198.9 1.4 copy-start.4
  198.9 1.9 copy-start.5
  200.8 4.5 %copy-start.2 = (f32[640,640]{0,1:T(8,128)S(1)}, f32[640,640]{0,1:T(8,128)}, u32[]{:S(2)}) copy-start(f32[640,640]{0,1:T(8,128)} %slice.313) | copy-start | bytes 4915204
  200.8 4.5 %copy-start.3 = (f32[640,640]{0,1:T(8,128)S(1)}, f32[640,640]{0,1:T(8,128)}, u32[]{:S(2)}) copy-start(f32[640,640]{0,1:T(8,128)} %slice.312) | copy-start | bytes 4915204
  200.8 4.5 %copy-start.6 = (f32[624,624]{0,1:T(8,128)S(1)}, f32[624,624]{0,1:T(8,128)}, u32[]{:S(2)}) copy-start(f32[624,624]{0,1:T(8,128)} %get-tuple-element.12) | copy-start | bytes 4672516
  200.8 4.5 %copy-start.7 = (f32[624,624]{0,1:T(8,128)S(1)}, f32[624,624]{0,1:T(8,128)}, u32[]{:S(2)}) copy-start(f32[624,624]{0,1:T(8,128)} %get-tuple-element.13) | copy-start | bytes 4672516
  201.5 3.8 %copy-start.1 = (f32[640,640]{0,1:T(8,128)S(1)}, f32[640,640]{0,1:T(8,128)}, u32[]{:S(2)}) copy-start(f32[640,640]{0,1:T(8,128)} %slice.316) | copy-start | bytes 4915204
  202.6 35.3 %collective-permute-start.3 = (f32[2,512,256]{1,2,0:T(8,128)}, f32[2,512,256]{1,2,0:T(8,128)S(1)}, u32[]{:S(2)}, u32[]{:S(2)}) collective-permute-start(f32[2,512,256]{1,2,0:T(8,128)} %fusion.4), channel_id=1, source_target_pairs={{0,1},{1,0},{2,3},{3,2},{4,5},{5,4},{6,7},{7,6},{8,9},{9,8},{10,11... | collective-permute-start | bytes 3145736 | tf_op jit(solution)/shard_map/ppermute | solution.py:87
  206.7 13.2 %collective-permute-start.6 = (f32[512,256]{0,1:T(8,128)}, f32[512,256]{0,1:T(8,128)}, u32[]{:S(2)}, u32[]{:S(2)}) collective-permute-start(f32[512,256]{0,1:T(8,128)} %get-tuple-element.15), channel_id=1, source_target_pairs={{0,2},{1,3},{2,4},{3,5},{4,6},{5,7},{6,8},{7,9},{8,10},{9,11},{10,... | collective-permute-start | bytes 1572872 | tf_op jit(solution)/shard_map/ppermute | solution.py:92
  206.7 29.9 %collective-permute-start.7 = (f32[512,256]{0,1:T(8,128)}, f32[512,256]{0,1:T(8,128)}, u32[]{:S(2)}, u32[]{:S(2)}) collective-permute-start(f32[512,256]{0,1:T(8,128)} %get-tuple-element.14), channel_id=1, source_target_pairs={{0,3},{1,2},{2,5},{3,4},{4,7},{5,6},{6,9},{7,8},{8,11},{9,10},{10,... | collective-permute-start | bytes 1572872 | tf_op jit(solution)/shard_map/ppermute | solution.py:93
  238.4 55.7 %collective-permute-start.8 = (f32[512]{0:T(512)S(1)}, f32[512]{0:T(512)S(1)}, u32[]{:S(2)}, u32[]{:S(2)}) collective-permute-start(f32[512]{0:T(512)S(1)} %fusion.12), channel_id=1, source_target_pairs={{0,1},{1,0},{2,3},{3,2},{4,5},{5,4},{6,7},{7,6},{8,9},{9,8},{10,11... | collective-permute-start | bytes 6152 | tf_op jit(solution)/shard_map/ppermute | solution.py:100
  238.8 50.6 %collective-permute-start.11 = (f32[256]{0:T(256)S(1)}, f32[256]{0:T(256)S(1)}, u32[]{:S(2)}, u32[]{:S(2)}) collective-permute-start(f32[256]{0:T(256)S(1)} %get-tuple-element.17), channel_id=1, source_target_pairs={{0,4},{1,5},{2,6},{3,7},{4,8},{5,9},{6,10},{7,11},{8,12},{9,13},{1... | collective-permute-start | bytes 3080 | tf_op jit(solution)/shard_map/ppermute | solution.py:105
  273.4 15.9 %collective-permute-start.12 = (f32[256]{0:T(256)S(1)}, f32[256]{0:T(256)S(1)}, u32[]{:S(2)}, u32[]{:S(2)}) collective-permute-start(f32[256]{0:T(256)S(1)} %get-tuple-element.16), channel_id=1, source_target_pairs={{0,5},{1,4},{2,7},{3,6},{4,9},{5,8},{6,11},{7,10},{8,13},{9,12},{1... | collective-permute-start | bytes 3080 | tf_op jit(solution)/shard_map/ppermute | solution.py:106
  287.5 4.8 %collective-permute-start.9 = (f32[256]{0:T(256)S(1)}, f32[256]{0:T(256)S(1)}, u32[]{:S(2)}, u32[]{:S(2)}) collective-permute-start(f32[256]{0:T(256)S(1)} %get-tuple-element.17), channel_id=1, source_target_pairs={{0,2},{1,3},{2,4},{3,5},{4,6},{5,7},{6,8},{7,9},{8,10},{9,11},{10,... | collective-permute-start | bytes 3080 | tf_op jit(solution)/shard_map/ppermute | solution.py:105
  287.5 6.7 %collective-permute-start.10 = (f32[256]{0:T(256)S(1)}, f32[256]{0:T(256)S(1)}, u32[]{:S(2)}, u32[]{:S(2)}) collective-permute-start(f32[256]{0:T(256)S(1)} %get-tuple-element.16), channel_id=1, source_target_pairs={{0,3},{1,2},{2,5},{3,4},{4,7},{5,6},{6,9},{7,8},{8,11},{9,10},{10,... | collective-permute-start | bytes 3080 | tf_op jit(solution)/shard_map/ppermute | solution.py:106

commit v3 on v2

v3 whole, which is shorter than its diff:
```python
import jax
import jax.numpy as jnp
from jax import lax
from jax.sharding import PartitionSpec as P

LAG = 240
BANDS = 3


def ring(axis, distance):
    n = lax.axis_size(axis)
    return [(i, (i + distance) % n) for i in range(n)]


def combine_lags(earlier, later, extent):
    keep = earlier.shape[0] + later.shape[0] - extent - 1
    return earlier[-keep:, -keep:] + later[:keep, :keep]


def lag_sum(distance, window):
    extent = distance.shape[0]
    summed = None
    doubled = distance
    remaining = window
    while remaining:
        if remaining % 2 == 1:
            summed = doubled if summed is None else combine_lags(summed, doubled, extent)
        remaining = remaining // 2
        if remaining:
            doubled = combine_lags(doubled, doubled, extent)
    return summed


def square_norms(values):
    return jnp.sum(jnp.square(values.astype(jnp.float32)), axis=1)


def lagged_partial(rows, cols):
    gram_tile = lax.dot_general(
        rows, cols, (((1,), (1,)), ((), ())), preferred_element_type=jnp.float32
    )
    distance = square_norms(rows)[:, None] + square_norms(cols)[None, :] - 2.0 * gram_tile
    return lag_sum(distance, LAG)


def lagged_split(rows, late_cols, early_cols):
    early = lax.dot_general(
        rows, early_cols, (((1,), (1,)), ((), ())), preferred_element_type=jnp.float32
    )
    late = lax.dot_general(
        rows, late_cols, (((1,), (1,)), ((), ())), preferred_element_type=jnp.float32
    )
    gram_tile = jnp.concatenate([late, early], axis=1)
    col_sq = jnp.concatenate([square_norms(late_cols), square_norms(early_cols)])
    distance = square_norms(rows)[:, None] + col_sq[None, :] - 2.0 * gram_tile
    return lag_sum(distance, LAG)


def per_device(snapshots, ocean_mask, spread):
    block_rows = snapshots.shape[0]
    cells_dev = snapshots.shape[1]
    hist = LAG - 1
    n_col = lax.axis_size("col")
    n_row = lax.axis_size("row")
    slot = lax.axis_index("col")
    mask = ocean_mask.astype(jnp.bfloat16)[None, :]
    tail = snapshots[block_rows - hist :]
    head = snapshots[: block_rows - hist]

    flat = ("row", "col")
    to_slot0 = [(n_col * r - 1, n_col * r) for r in range(1, n_row)]
    to_slot7 = [(n_col * r - 1, n_col * r + n_col - 1) for r in range(1, n_row)]
    up = ring("col", 1)
    down = ring("col", -1)
    tail_prev = lax.ppermute(tail, "col", up)
    tail_to_first = lax.ppermute(tail, flat, to_slot0)
    own_hist = jnp.where(slot == 0, tail_to_first, tail_prev)
    hist_prev = lax.ppermute(own_hist, "col", up)
    head_prev = lax.ppermute(head, "col", up)
    block_next = lax.ppermute(snapshots, "col", down)
    tail_to_last = lax.ppermute(tail, flat, to_slot7)
    hist_next = jnp.where(slot == n_col - 1, tail_to_last, tail)

    own_rows = jnp.concatenate([own_hist, snapshots], axis=0) * mask
    prev_early = jnp.concatenate([head_prev, tail_prev], axis=0) * mask
    prev_late = hist_prev * mask
    next_rows = jnp.concatenate([hist_next, block_next], axis=0) * mask

    n_space = lax.axis_size("space")
    column_width = block_rows // n_space
    side = lax.axis_index("space")
    start_col = side * column_width
    other_col = (1 - side) * column_width
    swap = [(0, 1), (1, 0)]

    def space_sum(band):
        mine = lax.dynamic_slice_in_dim(band, start_col, column_width, 1)
        theirs = lax.dynamic_slice_in_dim(band, other_col, column_width, 1)
        return mine + lax.ppermute(theirs, "space", swap)

    band0 = space_sum(lagged_partial(own_rows, own_rows))
    band1 = space_sum(lagged_split(own_rows, prev_late, prev_early))
    band2_next = lagged_split(next_rows, prev_late, prev_early)

    cs = ("col", "space")

    def col_shift(offset, flip):
        return [
            (n_space * c + p, n_space * ((c + offset) % n_col) + (1 - p if flip else p))
            for c in range(n_col)
            for p in range(n_space)
        ]

    b2_same = lax.ppermute(lax.dynamic_slice_in_dim(band2_next, start_col, column_width, 1), cs, col_shift(1, False))
    b2_cross = lax.ppermute(lax.dynamic_slice_in_dim(band2_next, other_col, column_width, 1), cs, col_shift(1, True))
    band2 = b2_same + b2_cross
    lagged = jnp.stack([band0, band1, band2])

    total_cells = cells_dev * n_space
    kernel = jnp.exp(-lagged / (LAG * total_cells * spread))
    part_degree = jnp.sum(kernel, axis=(0, 2))
    degree = part_degree + lax.ppermute(part_degree, "space", swap)
    degree_list = [lax.dynamic_slice_in_dim(degree, start_col, column_width, 0)]
    for offset in range(1, BANDS):
        d_same = lax.ppermute(lax.dynamic_slice_in_dim(part_degree, start_col, column_width, 0), cs, col_shift(offset, False))
        d_cross = lax.ppermute(lax.dynamic_slice_in_dim(part_degree, other_col, column_width, 0), cs, col_shift(offset, True))
        degree_list.append(d_same + d_cross)
    column_degrees = jnp.stack(degree_list)
    factor = float(BANDS * block_rows)
    return factor * kernel / jnp.sqrt(degree[None, :, None] * column_degrees[:, None, :])


def solution(mesh):
    placed = (P(("row", "col"), "space"), P("space"), P())
    return jax.shard_map(
        per_device,
        mesh=mesh,
        in_specs=placed,
        out_specs=P(None, ("row", "col"), "space"),
        check_vma=False,
    )
```

time: 301 us -> 285 us (0.947)
  the two profiles are of different devices: /device:TPU:39 before, /device:TPU:4 now
where the time goes in v3:
time: 285 us; the launch traced here: 280 us
  waiting for transfers between devices  176 us (62%)
  matrix products  34.7 us (12%)
  other arithmetic  33.8 us (12%)
  starting transfers between devices  17.6 us (6%)
  local copies, waits for them, and re-layouts  16.1 us (6%)
    ppermute x1, waiting for transfers between devices, per_device(): head_prev = lax.ppermute(head, 'col', up)  85.9 us
    ppermute x1, waiting for transfers between devices, per_device(): tail_prev = lax.ppermute(tail, 'col', up)  54.4 us
    ppermute x2, waiting for transfers between devices, space_sum(): return mine + lax.ppermute(theirs, 'space', swap)  16.1 us
    add x20, other arithmetic, combine_lags(): return earlier[-keep:, -keep:] + later[:keep, :keep]  14.1 us
    dot_general x2, matrix products, lagged_split(): lax.dot_general(rows, early_cols, (((1,), (1,)), ((), ())), preferred_ele...  13.6 us
    dot_general x2, matrix products, lagged_split(): lax.dot_general(rows, late_cols, (((1,), (1,)), ((), ())), preferred_elem...  12.1 us
    reduce_sum x3, other arithmetic, square_norms(): return jnp.sum(jnp.square(values.astype(jnp.float32)), axis=1)  12 us
    ppermute x1, waiting for transfers between devices, per_device(): hist_prev = lax.ppermute(own_hist, 'col', up)  11.6 us
  transfers between devices with their start and end apart: 15, of which 7 were waited for; matrix products, arithmetic and copies ran while one was open for 10% of the time, Pallas kernels for 0%

profile of v3, /device:TPU:4, one launch (start us, length us, event | category | flops | bytes accessed | tf_op | source)
XLA Modules:
  0.0 279.9 jit_solution(16697061051105375706)
XLA Ops:
  0.0 3.3 %slice.186 = bf16[239,4096]{1,0:T(8,128)(2,1)} slice(bf16[512,4096]{1,0:T(8,128)(2,1)} %param.3), slice={[273:512], [0:4096]} | slice | bytes 3915776 | tf_op jit(solution)/shard_map/slice | solution.py:67
  3.3 1.6 collective-permute-start.1
  4.9 1.3 collective-permute-start
  6.2 2.0 collective-permute-start.6
  8.2 3.3 %slice.207 = bf16[273,4096]{1,0:T(8,128)(2,1)} slice(bf16[512,4096]{1,0:T(8,128)(2,1)} %param.3), slice={[0:273], [0:4096]} | slice | bytes 4472832 | tf_op jit(solution)/shard_map/slice | solution.py:68
  11.5 2.2 collective-permute-start.4
  13.7 4.5 %collective-permute-start.7 = (bf16[512,4096]{1,0:T(8,128)(2,1)}, bf16[512,4096]{1,0:T(8,128)(2,1)}, u32[]{:S(2)}, u32[]{:S(2)}) collective-permute-start(bf16[512,4096]{1,0:T(8,128)(2,1)} %param.3), channel_id=1, source_target_pairs={{0,14},{2,0},{4,2},{6,4},{8,6},{10,8},{12,10},{14,12},{1,15},{3,1}... | collective-permute-start | bytes 12582920 | tf_op jit(solution)/shard_map/ppermute | solution.py:80
  18.2 54.4 %collective-permute-done.1 = bf16[239,4096]{1,0:T(8,128)(2,1)S(1)} collective-permute-done((bf16[239,4096]{1,0:T(8,128)(2,1)}, bf16[239,4096]{1,0:T(8,128)(2,1)S(1)}, u32[]{:S(2)}, u32[]{:S(2)}) %collective-permute-start.1) | collective-permute-done | bytes 1957920 | tf_op jit(solution)/shard_map/ppermute | solution.py:75
  72.7 1.8 broadcast_select_fusion.1
  74.7 2.1 broadcast_select_fusion
  76.8 85.9 %collective-permute-done.4 = bf16[273,4096]{1,0:T(8,128)(2,1)} collective-permute-done((bf16[273,4096]{1,0:T(8,128)(2,1)}, bf16[273,4096]{1,0:T(8,128)(2,1)}, u32[]{:S(2)}, u32[]{:S(2)}) %collective-permute-start.4) | collective-permute-done | bytes 2236448 | tf_op jit(solution)/shard_map/ppermute | solution.py:79
  162.7 3.1 %multiply_reduce_fusion.2 = f32[512]{0:T(512)S(1)} fusion(bf16[4096]{0:T(1024)(128)(2,1)S(1)} %convert_element_type.19, bf16[239,4096]{1,0:T(8,128)(2,1)S(1)} %collective-permute-done.1, bf16[273,4096]{1,0:T(8,128)(2,1)} %collective-permute-done.4), kind=kLoop, calls=%fused_computation.2 | loop fusion | flops 16776704 | bytes 4204544 | tf_op jit(solution)/shard_map/reduce_sum | solution.py:35
  165.8 6.7 %fusion.14 = f32[751,512]{0,1:T(8,128)S(1)} fusion(bf16[239,4096]{1,0:T(8,128)(2,1)S(1)} %collective-permute-done.1, bf16[273,4096]{1,0:T(8,128)(2,1)} %collective-permute-done.4, bf16[4096]{0:T(1024)(128)(2,1)S(1)} %convert_element_type.19, bf16[512,4096]{1,0:T(8,128)(2,1)} %param.3, bf16[239,4096]{1,0:T(8,128)(2,1)S(1)} %broadcast_select_fusion.1), kind=kOutput, calls=%fused_computation.58 | convolution fusion | flops 3180961792 | bytes 11892736 | tf_op jit(solution)/shard_map/dot_general | solution.py:47
  172.5 11.6 %collective-permute-done.3 = bf16[239,4096]{1,0:T(8,128)(2,1)S(1)} collective-permute-done((bf16[239,4096]{1,0:T(8,128)(2,1)S(1)}, bf16[239,4096]{1,0:T(8,128)(2,1)S(1)}, u32[]{:S(2)}, u32[]{:S(2)}) %collective-permute-start.3) | collective-permute-done | bytes 1957920 | tf_op jit(solution)/shard_map/ppermute | solution.py:78
  184.8 6.1 %fusion.6 = f32[751,239]{0,1:T(8,128)S(1)} fusion(bf16[239,4096]{1,0:T(8,128)(2,1)S(1)} %collective-permute-done.3, bf16[4096]{0:T(1024)(128)(2,1)S(1)} %convert_element_type.19, bf16[512,4096]{1,0:T(8,128)(2,1)} %param.3, bf16[239,4096]{1,0:T(8,128)(2,1)S(1)} %broadcast_select_fusion.1), kind=kOutput, calls=%fused_computation.38 | convolution fusion | flops 1489809408 | bytes 8836228 | tf_op jit(solution)/shard_map/dot_general | solution.py:50
  190.9 8.3 %multiply_reduce_fusion.1 = (f32[751]{0:T(1024)S(1)}, f32[751]{0:T(1024)S(1)}) fusion(bf16[4096]{0:T(1024)(128)(2,1)S(1)} %convert_element_type.19, bf16[512,4096]{1,0:T(8,128)(2,1)} %param.3, bf16[239,4096]{1,0:T(8,128)(2,1)S(1)} %broadcast_select_fusion.1, bf16[512,4096]{1,0:T(8,128)(2,1)} %collective-permute-done.7, ...), kind=kLoop, calls=%fused_computation.1 | loop fusion | flops 46139936 | bytes 12318584 | tf_op jit(solution)/shard_map/reduce_sum | solution.py:35
  199.2 8.9 %multiply_subtract_fusion = f32[751,751]{0,1:T(8,128)S(1)} fusion(f32[751]{0:T(1024)S(1)} %get-tuple-element.5, bf16[512,4096]{1,0:T(8,128)(2,1)} %param.3, bf16[239,4096]{1,0:T(8,128)(2,1)S(1)} %broadcast_select_fusion.1, bf16[4096]{0:T(1024)(128)(2,1)S(1)} %convert_element_type.19), kind=kOutput, calls=%fused_computation.17 | convolution fusion | flops 4640445440 | bytes 8419392 | tf_op jit(solution)/shard_map/dot_general | solution.py:39
  208.2 0.9 slice_add_fusion.5
  209.0 0.8 slice_add_fusion.4
  209.9 0.8 slice_add_fusion.8
  210.7 0.7 slice_add_fusion.11
  211.9 0.6 slice_add_fusion.14
  214.2 6.9 %fusion.13 = f32[751,512]{0,1:T(8,128)S(1)} fusion(bf16[512,4096]{1,0:T(8,128)(2,1)} %collective-permute-done.7, bf16[239,4096]{1,0:T(8,128)(2,1)S(1)} %broadcast_select_fusion, bf16[4096]{0:T(1024)(128)(2,1)S(1)} %convert_element_type.19, bf16[239,4096]{1,0:T(8,128)(2,1)S(1)} %collective-permute-done.1, bf16[273,4096]{1,0:T(8,128)(2,1)} %collective-permute-done.4), kind=kOutput, calls=%fused_computation.57 | convolution fusion | flops 3180961792 | bytes 11892736 | tf_op jit(solution)/shard_map/dot_general | solution.py:47
  221.2 6.1 %fusion.4 = f32[751,239]{0,1:T(8,128)S(1)} fusion(bf16[239,4096]{1,0:T(8,128)(2,1)S(1)} %collective-permute-done.3, bf16[4096]{0:T(1024)(128)(2,1)S(1)} %convert_element_type.19, bf16[512,4096]{1,0:T(8,128)(2,1)} %collective-permute-done.7, bf16[239,4096]{1,0:T(8,128)(2,1)S(1)} %broadcast_select_fusion), kind=kOutput, calls=%fused_computation.36 | convolution fusion | flops 1489809408 | bytes 8836228 | tf_op jit(solution)/shard_map/dot_general | solution.py:50
  227.2 0.8 fusion
  228.0 1.3 slice_add_fusion.1
  229.3 0.8 slice_add_fusion
  230.2 0.8 slice_add_fusion.6
  231.0 0.7 slice_add_fusion.9
  232.2 0.6 slice_add_fusion.12
  234.5 0.8 slice_add_fusion.2
  235.4 0.8 slice_add_fusion.7
  236.2 0.7 slice_add_fusion.10
  237.4 0.6 slice_add_fusion.13
  239.3 0.7 fusion.20
  240.4 0.8 constant_dynamic-slice_fusion.3
  241.2 3.6 %collective-permute-start.2 = (f32[512,256]{0,1:T(8,128)}, f32[512,256]{0,1:T(8,128)}, u32[]{:S(2)}, u32[]{:S(2)}) collective-permute-start(f32[512,256]{0,1:T(8,128)} %constant_dynamic-slice_fusion.3), channel_id=1, source_target_pairs={{0,1},{1,0},{2,3},{3,2},{4,5},{5,4},{6,7},{7,6},{8,9},{9,8},{10,11... | collective-permute-start | bytes 1572872 | tf_op jit(solution)/shard_map/ppermute | solution.py:99
  245.2 0.8 constant_dynamic-slice_fusion.2
  246.3 1.0 constant_dynamic-slice_fusion
  248.0 5.9 %collective-permute-done.2 = f32[512,256]{0,1:T(8,128)} collective-permute-done((f32[512,256]{0,1:T(8,128)}, f32[512,256]{0,1:T(8,128)}, u32[]{:S(2)}, u32[]{:S(2)}) %collective-permute-start.2) | collective-permute-done | bytes 524320 | tf_op jit(solution)/shard_map/ppermute | solution.py:99
  254.0 1.1 add_bitcast_fusion.2
  255.1 10.2 %collective-permute-done.5 = f32[512,256]{0,1:T(8,128)} collective-permute-done((f32[512,256]{0,1:T(8,128)}, f32[512,256]{0,1:T(8,128)}, u32[]{:S(2)}, u32[]{:S(2)}) %collective-permute-start.5) | collective-permute-done | bytes 524320 | tf_op jit(solution)/shard_map/ppermute | solution.py:99
  265.2 1.1 add_bitcast_fusion.1
  266.4 2.1 collective-permute-done.8
  268.8 1.3 collective-permute-start.10
  270.4 0.7 collective-permute-start.11
  271.1 6.3 %collective-permute-done.14 = f32[256]{0:T(256)S(1)} collective-permute-done((f32[256]{0:T(256)S(1)}, f32[256]{0:T(256)S(1)}, u32[]{:S(2)}, u32[]{:S(2)}) %collective-permute-start.14) | collective-permute-done | bytes 1056 | tf_op jit(solution)/shard_map/ppermute | solution.py:126
  278.0 1.6 copy.6
  (46 shorter events, 9.4 us)
Async XLA Ops:
  3.3 14.9 %copy-start = (s32[4096]{0:T(1024)S(1)}, s32[4096]{0:T(1024)}, u32[]{:S(2)}) copy-start(s32[4096]{0:T(1024)} %param.4) | copy-start | bytes 49156
  3.3 69.3 %collective-permute-start.1 = (bf16[239,4096]{1,0:T(8,128)(2,1)}, bf16[239,4096]{1,0:T(8,128)(2,1)S(1)}, u32[]{:S(2)}, u32[]{:S(2)}) collective-permute-start(bf16[239,4096]{1,0:T(8,128)(2,1)} %slice.186), channel_id=1, source_target_pairs={{0,2},{2,4},{4,6},{6,8},{8,10},{10,12},{12,14},{14,0},{1,3},{3,5},... | collective-permute-start | bytes 5873672 | tf_op jit(solution)/shard_map/ppermute | solution.py:75
  4.9 67.7 %collective-permute-start = (bf16[239,4096]{1,0:T(8,128)(2,1)}, bf16[239,4096]{1,0:T(8,128)(2,1)}, u32[]{:S(2)}, u32[]{:S(2)}) collective-permute-start(bf16[239,4096]{1,0:T(8,128)(2,1)} %slice.186), channel_id=1, source_target_pairs={{14,16},{30,32},{46,48},{62,64},{78,80},{94,96},{110,112},{15,17},... | collective-permute-start | bytes 5873672 | tf_op jit(solution)/shard_map/ppermute | solution.py:76
  6.2 68.5 %collective-permute-start.6 = (bf16[239,4096]{1,0:T(8,128)(2,1)}, bf16[239,4096]{1,0:T(8,128)(2,1)}, u32[]{:S(2)}, u32[]{:S(2)}) collective-permute-start(bf16[239,4096]{1,0:T(8,128)(2,1)} %slice.186), channel_id=1, source_target_pairs={{14,30},{30,46},{46,62},{62,78},{78,94},{94,110},{110,126},{15,31}... | collective-permute-start | bytes 5873672 | tf_op jit(solution)/shard_map/ppermute | solution.py:81
  11.5 151.2 %collective-permute-start.4 = (bf16[273,4096]{1,0:T(8,128)(2,1)}, bf16[273,4096]{1,0:T(8,128)(2,1)}, u32[]{:S(2)}, u32[]{:S(2)}) collective-permute-start(bf16[273,4096]{1,0:T(8,128)(2,1)} %slice.207), channel_id=1, source_target_pairs={{0,2},{2,4},{4,6},{6,8},{8,10},{10,12},{12,14},{14,0},{1,3},{3,5},... | collective-permute-start | bytes 6709256 | tf_op jit(solution)/shard_map/ppermute | solution.py:79
  13.7 177.2 %collective-permute-start.7 = (bf16[512,4096]{1,0:T(8,128)(2,1)}, bf16[512,4096]{1,0:T(8,128)(2,1)}, u32[]{:S(2)}, u32[]{:S(2)}) collective-permute-start(bf16[512,4096]{1,0:T(8,128)(2,1)} %param.3), channel_id=1, source_target_pairs={{0,14},{2,0},{4,2},{6,4},{8,6},{10,8},{12,10},{14,12},{1,15},{3,1}... | collective-permute-start | bytes 12582920 | tf_op jit(solution)/shard_map/ppermute | solution.py:80
  74.4 109.7 %collective-permute-start.3 = (bf16[239,4096]{1,0:T(8,128)(2,1)S(1)}, bf16[239,4096]{1,0:T(8,128)(2,1)S(1)}, u32[]{:S(2)}, u32[]{:S(2)}) collective-permute-start(bf16[239,4096]{1,0:T(8,128)(2,1)S(1)} %broadcast_select_fusion.1), channel_id=1, source_target_pairs={{0,2},{2,4},{4,6},{6,8},{8,10},{10,12},{12,14},{14,0},{1,3},{3,5},... | collective-permute-start | bytes 5873672 | tf_op jit(solution)/shard_map/ppermute | solution.py:78
  241.2 12.7 %collective-permute-start.2 = (f32[512,256]{0,1:T(8,128)}, f32[512,256]{0,1:T(8,128)}, u32[]{:S(2)}, u32[]{:S(2)}) collective-permute-start(f32[512,256]{0,1:T(8,128)} %constant_dynamic-slice_fusion.3), channel_id=1, source_target_pairs={{0,1},{1,0},{2,3},{3,2},{4,5},{5,4},{6,7},{7,6},{8,9},{9,8},{10,11... | collective-permute-start | bytes 1572872 | tf_op jit(solution)/shard_map/ppermute | solution.py:99
  246.0 19.2 %collective-permute-start.5 = (f32[512,256]{0,1:T(8,128)}, f32[512,256]{0,1:T(8,128)}, u32[]{:S(2)}, u32[]{:S(2)}) collective-permute-start(f32[512,256]{0,1:T(8,128)} %constant_dynamic-slice_fusion.2), channel_id=1, source_target_pairs={{0,1},{1,0},{2,3},{3,2},{4,5},{5,4},{6,7},{7,6},{8,9},{9,8},{10,11... | collective-permute-start | bytes 1572872 | tf_op jit(solution)/shard_map/ppermute | solution.py:99
  247.4 19.0 %collective-permute-start.9 = (f32[512,256]{0,1:T(8,128)}, f32[512,256]{0,1:T(8,128)S(1)}, u32[]{:S(2)}, u32[]{:S(2)}) collective-permute-start(f32[512,256]{0,1:T(8,128)} %get-tuple-element.13), channel_id=1, source_target_pairs={{0,3},{1,2},{2,5},{3,4},{4,7},{5,6},{6,9},{7,8},{8,11},{9,10},{10,... | collective-permute-start | bytes 1572872 | tf_op jit(solution)/shard_map/ppermute | solution.py:115
  247.4 21.1 %collective-permute-start.8 = (f32[512,256]{0,1:T(8,128)}, f32[512,256]{0,1:T(8,128)S(1)}, u32[]{:S(2)}, u32[]{:S(2)}) collective-permute-start(f32[512,256]{0,1:T(8,128)} %get-tuple-element.14), channel_id=1, source_target_pairs={{0,2},{1,3},{2,4},{3,5},{4,6},{5,7},{6,8},{7,9},{8,10},{9,11},{10,... | collective-permute-start | bytes 1572872 | tf_op jit(solution)/shard_map/ppermute | solution.py:114
  268.8 8.6 %collective-permute-start.10 = (f32[512]{0:T(512)S(1)}, f32[512]{0:T(512)S(1)}, u32[]{:S(2)}, u32[]{:S(2)}) collective-permute-start(f32[512]{0:T(512)S(1)} %fusion.18), channel_id=1, source_target_pairs={{0,1},{1,0},{2,3},{3,2},{4,5},{5,4},{6,7},{7,6},{8,9},{9,8},{10,11... | collective-permute-start | bytes 6152 | tf_op jit(solution)/shard_map/ppermute | solution.py:122
  270.2 7.2 %collective-permute-start.14 = (f32[256]{0:T(256)S(1)}, f32[256]{0:T(256)S(1)}, u32[]{:S(2)}, u32[]{:S(2)}) collective-permute-start(f32[256]{0:T(256)S(1)} %get-tuple-element.17), channel_id=1, source_target_pairs={{0,5},{1,4},{2,7},{3,6},{4,9},{5,8},{6,11},{7,10},{8,13},{9,12},{1... | collective-permute-start | bytes 3080 | tf_op jit(solution)/shard_map/ppermute | solution.py:126
  270.2 7.2 %collective-permute-start.13 = (f32[256]{0:T(256)S(1)}, f32[256]{0:T(256)S(1)}, u32[]{:S(2)}, u32[]{:S(2)}) collective-permute-start(f32[256]{0:T(256)S(1)} %get-tuple-element.18), channel_id=1, source_target_pairs={{0,4},{1,5},{2,6},{3,7},{4,8},{5,9},{6,10},{7,11},{8,12},{9,13},{1... | collective-permute-start | bytes 3080 | tf_op jit(solution)/shard_map/ppermute | solution.py:125
  270.3 7.1 %collective-permute-start.12 = (f32[256]{0:T(256)S(1)}, f32[256]{0:T(256)S(1)}, u32[]{:S(2)}, u32[]{:S(2)}) collective-permute-start(f32[256]{0:T(256)S(1)} %get-tuple-element.17), channel_id=1, source_target_pairs={{0,3},{1,2},{2,5},{3,4},{4,7},{5,6},{6,9},{7,8},{8,11},{9,10},{10,... | collective-permute-start | bytes 3080 | tf_op jit(solution)/shard_map/ppermute | solution.py:126
  270.4 7.0 %collective-permute-start.11 = (f32[256]{0:T(256)S(1)}, f32[256]{0:T(256)S(1)}, u32[]{:S(2)}, u32[]{:S(2)}) collective-permute-start(f32[256]{0:T(256)S(1)} %get-tuple-element.18), channel_id=1, source_target_pairs={{0,2},{1,3},{2,4},{3,5},{4,6},{5,7},{6,8},{7,9},{8,10},{9,11},{10,... | collective-permute-start | bytes 3080 | tf_op jit(solution)/shard_map/ppermute | solution.py:125

commit v4 on v3

--- a/solution.py
+++ b/solution.py
@@ -43,15 +43,15 @@
     return lag_sum(distance, LAG)
 
 
-def lagged_split(rows, late_cols, early_cols):
-    early = lax.dot_general(
-        rows, early_cols, (((1,), (1,)), ((), ())), preferred_element_type=jnp.float32
+def gram(rows, cols):
+    return lax.dot_general(
+        rows, cols, (((1,), (1,)), ((), ())), preferred_element_type=jnp.float32
     )
-    late = lax.dot_general(
-        rows, late_cols, (((1,), (1,)), ((), ())), preferred_element_type=jnp.float32
-    )
-    gram_tile = jnp.concatenate([late, early], axis=1)
-    col_sq = jnp.concatenate([square_norms(late_cols), square_norms(early_cols)])
+
+
+def lagged_split(rows, late_cols, early_gram, early_sq):
+    gram_tile = jnp.concatenate([gram(rows, late_cols), early_gram], axis=1)
+    col_sq = jnp.concatenate([square_norms(late_cols), early_sq])
     distance = square_norms(rows)[:, None] + col_sq[None, :] - 2.0 * gram_tile
     return lag_sum(distance, LAG)
 
@@ -74,17 +74,22 @@
     down = ring("col", -1)
     tail_prev = lax.ppermute(tail, "col", up)
     tail_to_first = lax.ppermute(tail, flat, to_slot0)
-    own_hist = jnp.where(slot == 0, tail_to_first, tail_prev)
-    hist_prev = lax.ppermute(own_hist, "col", up)
     head_prev = lax.ppermute(head, "col", up)
     block_next = lax.ppermute(snapshots, "col", down)
     tail_to_last = lax.ppermute(tail, flat, to_slot7)
+    own_hist = jnp.where(slot == 0, tail_to_first, tail_prev)
+    own_rows = jnp.concatenate([own_hist, snapshots], axis=0) * mask
+    band0_part = lagged_partial(own_rows, own_rows)
+    hist_send, band0_part = lax.optimization_barrier((own_hist, band0_part))
+    hist_prev = lax.ppermute(hist_send, "col", up)
     hist_next = jnp.where(slot == n_col - 1, tail_to_last, tail)
+    block_next, _ = lax.optimization_barrier((block_next, band0_part))
 
-    own_rows = jnp.concatenate([own_hist, snapshots], axis=0) * mask
     prev_early = jnp.concatenate([head_prev, tail_prev], axis=0) * mask
-    prev_late = hist_prev * mask
     next_rows = jnp.concatenate([hist_next, block_next], axis=0) * mask
+    early1 = gram(own_rows, prev_early)
+    early2 = gram(next_rows, prev_early)
+    early_sq = square_norms(prev_early)
 
     n_space = lax.axis_size("space")
     column_width = block_rows // n_space
@@ -98,9 +103,11 @@
         theirs = lax.dynamic_slice_in_dim(band, other_col, column_width, 1)
         return mine + lax.ppermute(theirs, "space", swap)
 
-    band0 = space_sum(lagged_partial(own_rows, own_rows))
-    band1 = space_sum(lagged_split(own_rows, prev_late, prev_early))
-    band2_next = lagged_split(next_rows, prev_late, prev_early)
+    band0_part, early1, early2, early_sq = lax.optimization_barrier((band0_part, early1, early2, early_sq))
+    band0 = space_sum(band0_part)
+    prev_late = hist_prev * mask
+    band1 = space_sum(lagged_split(own_rows, prev_late, early1, early_sq))
+    band2_next = lagged_split(next_rows, prev_late, early2, early_sq)
 
     cs = ("col", "space")
 

time: 285 us -> 264 us (0.926)
  the two profiles are of different devices: /device:TPU:4 before, /device:TPU:28 now
where the time goes in v4:
time: 264 us; the launch traced here: 261 us
  waiting for transfers between devices  127 us (48%)
  starting transfers between devices  62.1 us (24%)
  other arithmetic  31.9 us (12%)
  matrix products  24.5 us (9%)
  local copies, waits for them, and re-layouts  14.5 us (5%)
    ppermute x1, waiting for transfers between devices, per_device(): tail_prev = lax.ppermute(tail, 'col', up)  34.9 us
    ppermute x1, waiting for transfers between devices, per_device(): hist_prev = lax.ppermute(hist_send, 'col', up)  32.7 us
    ppermute x1, waiting for transfers between devices, per_device(): head_prev = lax.ppermute(head, 'col', up)  29.3 us
    ppermute x2, starting transfers between devices, per_device(): lax.ppermute(lax.dynamic_slice_in_dim(part_degree, start_col, column_widt...  24.8 us
    ppermute x2, waiting for transfers between devices, space_sum(): return mine + lax.ppermute(theirs, 'space', swap)  24.4 us
    dot_general x4, matrix products, gram(): lax.dot_general(rows, cols, (((1,), (1,)), ((), ())), preferred_element_t...  19 us
    add x20, other arithmetic, combine_lags(): return earlier[-keep:, -keep:] + later[:keep, :keep]  14 us
    reduce_sum x4, other arithmetic, square_norms(): return jnp.sum(jnp.square(values.astype(jnp.float32)), axis=1)  11.5 us
  transfers between devices with their start and end apart: 15, of which 7 were waited for; matrix products, arithmetic and copies ran while one was open for 13% of the time, Pallas kernels for 0%

profile of v4, /device:TPU:28, one launch (start us, length us, event | category | flops | bytes accessed | tf_op | source)
XLA Modules:
  0.0 261.0 jit_solution(8296417547225057989)
XLA Ops:
  0.0 3.3 %slice.186 = bf16[239,4096]{1,0:T(8,128)(2,1)} slice(bf16[512,4096]{1,0:T(8,128)(2,1)} %param.3), slice={[273:512], [0:4096]} | slice | bytes 3915776 | tf_op jit(solution)/shard_map/slice | solution.py:67
  3.3 2.1 collective-permute-start
  5.4 1.6 collective-permute-start.1
  7.5 1.9 collective-permute-start.3
  9.4 3.3 %slice.207 = bf16[273,4096]{1,0:T(8,128)(2,1)} slice(bf16[512,4096]{1,0:T(8,128)(2,1)} %param.3), slice={[0:273], [0:4096]} | slice | bytes 4472832 | tf_op jit(solution)/shard_map/slice | solution.py:68
  12.7 3.7 %collective-permute-start.2 = (bf16[273,4096]{1,0:T(8,128)(2,1)}, bf16[273,4096]{1,0:T(8,128)(2,1)}, u32[]{:S(2)}, u32[]{:S(2)}) collective-permute-start(bf16[273,4096]{1,0:T(8,128)(2,1)} %slice.207), channel_id=1, source_target_pairs={{0,2},{2,4},{4,6},{6,8},{8,10},{10,12},{12,14},{14,0},{1,3},{3,5},... | collective-permute-start | bytes 6709256 | tf_op jit(solution)/shard_map/ppermute | solution.py:77
  16.4 34.9 %collective-permute-done.1 = bf16[239,4096]{1,0:T(8,128)(2,1)S(1)} collective-permute-done((bf16[239,4096]{1,0:T(8,128)(2,1)}, bf16[239,4096]{1,0:T(8,128)(2,1)S(1)}, u32[]{:S(2)}, u32[]{:S(2)}) %collective-permute-start.1) | collective-permute-done | bytes 1957920 | tf_op jit(solution)/shard_map/ppermute | solution.py:75
  51.6 3.1 %multiply_reduce_fusion.1 = f32[751]{0:T(1024)S(1)} fusion(bf16[4096]{0:T(1024)(128)(2,1)S(1)} %convert_element_type.18, bf16[512,4096]{1,0:T(8,128)(2,1)S(1)} %copy-done, bf16[239,4096]{1,0:T(8,128)(2,1)S(1)} %broadcast_select_fusion.1), kind=kLoop, calls=%fused_computation.1 | loop fusion | flops 24608016 | bytes 6163388 | tf_op jit(solution)/shard_map/reduce_sum | solution.py:35
  54.7 5.5 %multiply_subtract_fusion = f32[751,751]{1,0:T(8,128)S(1)} fusion(f32[751]{0:T(1024)S(1)} %multiply_reduce_fusion.1, bf16[512,4096]{1,0:T(8,128)(2,1)S(1)} %copy-done, bf16[239,4096]{1,0:T(8,128)(2,1)S(1)} %broadcast_select_fusion.1, bf16[4096]{0:T(1024)(128)(2,1)S(1)} %convert_element_type.18), kind=kOutput, calls=%fused_computation.17 | convolution fusion | flops 4640445440 | bytes 8419392 | tf_op jit(solution)/shard_map/dot_general | solution.py:39
  60.2 0.9 slice_add_fusion.5
  61.0 0.8 slice_add_fusion.4
  61.9 0.8 slice_add_fusion.8
  62.7 0.7 slice_add_fusion.11
  66.6 4.2 %collective-permute-start.6 = (bf16[239,4096]{1,0:T(8,128)(2,1)S(1)}, bf16[239,4096]{1,0:T(8,128)(2,1)S(1)}, u32[]{:S(2)}, u32[]{:S(2)}) collective-permute-start(bf16[239,4096]{1,0:T(8,128)(2,1)S(1)} %broadcast_select_fusion.1), channel_id=1, source_target_pairs={{0,2},{2,4},{4,6},{6,8},{8,10},{10,12},{12,14},{14,0},{1,3},{3,5},... | collective-permute-start | bytes 5873672 | tf_op jit(solution)/shard_map/ppermute | solution.py:84
  71.3 29.3 %collective-permute-done.2 = bf16[273,4096]{1,0:T(8,128)(2,1)} collective-permute-done((bf16[273,4096]{1,0:T(8,128)(2,1)}, bf16[273,4096]{1,0:T(8,128)(2,1)}, u32[]{:S(2)}, u32[]{:S(2)}) %collective-permute-start.2) | collective-permute-done | bytes 2236448 | tf_op jit(solution)/shard_map/ppermute | solution.py:77
  100.6 3.1 %multiply_reduce_fusion.2 = f32[512]{0:T(512)S(1)} fusion(bf16[4096]{0:T(1024)(128)(2,1)S(1)} %convert_element_type.18, bf16[239,4096]{1,0:T(8,128)(2,1)S(1)} %collective-permute-done.1, bf16[273,4096]{1,0:T(8,128)(2,1)} %collective-permute-done.2), kind=kLoop, calls=%fused_computation.2 | loop fusion | flops 16776704 | bytes 4204544 | tf_op jit(solution)/shard_map/reduce_sum | solution.py:35
  103.7 5.0 %fusion.14 = f32[751,512]{1,0:T(8,128)S(1)} fusion(bf16[239,4096]{1,0:T(8,128)(2,1)S(1)} %collective-permute-done.1, bf16[273,4096]{1,0:T(8,128)(2,1)} %collective-permute-done.2, bf16[4096]{0:T(1024)(128)(2,1)S(1)} %convert_element_type.18, bf16[512,4096]{1,0:T(8,128)(2,1)S(1)} %copy-done, bf16[239,4096]{1,0:T(8,128)(2,1)S(1)} %broadcast_select_fusion.1), kind=kOutput, calls=%fused_computation.58 | convolution fusion | flops 3180961792 | bytes 11892736 | tf_op jit(solution)/shard_map/dot_general | solution.py:47
  108.7 32.7 %collective-permute-done.6 = bf16[239,4096]{1,0:T(8,128)(2,1)S(1)} collective-permute-done((bf16[239,4096]{1,0:T(8,128)(2,1)S(1)}, bf16[239,4096]{1,0:T(8,128)(2,1)S(1)}, u32[]{:S(2)}, u32[]{:S(2)}) %collective-permute-start.6) | collective-permute-done | bytes 1957920 | tf_op jit(solution)/shard_map/ppermute | solution.py:84
  142.1 1.9 fusion.6
  144.0 4.7 %multiply_reduce_fusion = f32[751]{0:T(1024)S(1)} fusion(bf16[4096]{0:T(1024)(128)(2,1)S(1)} %convert_element_type.18, bf16[512,4096]{1,0:T(8,128)(2,1)} %collective-permute-done.4, bf16[239,4096]{1,0:T(8,128)(2,1)S(1)} %broadcast_select_fusion), kind=kLoop, calls=%fused_computation | loop fusion | flops 24608016 | bytes 6163388 | tf_op jit(solution)/shard_map/reduce_sum | solution.py:35
  148.6 6.3 %fusion.13 = f32[751,512]{1,0:T(8,128)S(1)} fusion(bf16[512,4096]{1,0:T(8,128)(2,1)} %collective-permute-done.4, bf16[239,4096]{1,0:T(8,128)(2,1)S(1)} %broadcast_select_fusion, bf16[4096]{0:T(1024)(128)(2,1)S(1)} %convert_element_type.18, bf16[239,4096]{1,0:T(8,128)(2,1)S(1)} %collective-permute-done.1, bf16[273,4096]{1,0:T(8,128)(2,1)} %collective-permute-done.2), kind=kOutput, calls=%fused_computation.57 | convolution fusion | flops 3180961792 | bytes 11892736 | tf_op jit(solution)/shard_map/dot_general | solution.py:47
  155.0 5.8 %fusion.4 = f32[751,239]{1,0:T(8,128)S(1)} fusion(bf16[239,4096]{1,0:T(8,128)(2,1)S(1)} %collective-permute-done.6, bf16[4096]{0:T(1024)(128)(2,1)S(1)} %convert_element_type.18, bf16[512,4096]{1,0:T(8,128)(2,1)} %collective-permute-done.4, bf16[239,4096]{1,0:T(8,128)(2,1)S(1)} %broadcast_select_fusion), kind=kOutput, calls=%fused_computation.36 | convolution fusion | flops 1489809408 | bytes 8836228 | tf_op jit(solution)/shard_map/dot_general | solution.py:47
  160.8 1.4 fusion
  162.2 1.3 slice_add_fusion.1
  163.5 0.8 slice_add_fusion
  164.4 0.8 slice_add_fusion.6
  165.2 0.7 slice_add_fusion.9
  168.7 0.9 slice_add_fusion.2
  169.6 0.8 slice_add_fusion.7
  170.4 0.7 slice_add_fusion.10
  173.0 0.7 slice.285
  174.5 0.8 constant_dynamic-slice_fusion.2
  175.3 3.9 %collective-permute-start.7 = (f32[512,256]{1,0:T(8,128)}, f32[512,256]{1,0:T(8,128)}, u32[]{:S(2)}, u32[]{:S(2)}) collective-permute-start(f32[512,256]{1,0:T(8,128)} %constant_dynamic-slice_fusion.2), channel_id=1, source_target_pairs={{0,1},{1,0},{2,3},{3,2},{4,5},{5,4},{6,7},{7,6},{8,9},{9,8},{10,11... | collective-permute-start | bytes 1572872 | tf_op jit(solution)/shard_map/ppermute | solution.py:104
  179.2 0.8 constant_dynamic-slice_fusion.3
  180.4 1.1 constant_dynamic-slice_fusion
  181.5 3.3 %collective-permute-start.8 = (f32[512,256]{1,0:T(8,128)}, f32[512,256]{1,0:T(8,128)S(1)}, u32[]{:S(2)}, u32[]{:S(2)}) collective-permute-start(f32[512,256]{1,0:T(8,128)} %get-tuple-element.26), channel_id=1, source_target_pairs={{0,2},{1,3},{2,4},{3,5},{4,6},{5,7},{6,8},{7,9},{8,10},{9,11},{10,... | collective-permute-start | bytes 1572872 | tf_op jit(solution)/shard_map/ppermute | solution.py:121
  184.8 2.1 collective-permute-start.9
  187.6 4.7 %collective-permute-done.7 = f32[512,256]{1,0:T(8,128)} collective-permute-done((f32[512,256]{1,0:T(8,128)}, f32[512,256]{1,0:T(8,128)}, u32[]{:S(2)}, u32[]{:S(2)}) %collective-permute-start.7) | collective-permute-done | bytes 524320 | tf_op jit(solution)/shard_map/ppermute | solution.py:104
  192.3 1.1 add_bitcast_fusion.1
  193.4 19.6 %collective-permute-done.5 = f32[512,256]{1,0:T(8,128)} collective-permute-done((f32[512,256]{1,0:T(8,128)}, f32[512,256]{1,0:T(8,128)}, u32[]{:S(2)}, u32[]{:S(2)}) %collective-permute-start.5) | collective-permute-done | bytes 524320 | tf_op jit(solution)/shard_map/ppermute | solution.py:104
  213.1 1.1 add_bitcast_fusion.2
  214.6 3.4 %collective-permute-start.10 = (f32[512]{0:T(512)S(1)}, f32[512]{0:T(512)S(1)}, u32[]{:S(2)}, u32[]{:S(2)}) collective-permute-start(f32[512]{0:T(512)S(1)} %fusion.18), channel_id=1, source_target_pairs={{0,1},{1,0},{2,3},{3,2},{4,5},{5,4},{6,7},{7,6},{8,9},{9,8},{10,11... | collective-permute-start | bytes 6152 | tf_op jit(solution)/shard_map/ppermute | solution.py:129
  218.1 19.2 %collective-permute-start.13 = (f32[256]{0:T(256)S(1)}, f32[256]{0:T(256)S(1)}, u32[]{:S(2)}, u32[]{:S(2)}) collective-permute-start(f32[256]{0:T(256)S(1)} %get-tuple-element.30), channel_id=1, source_target_pairs={{0,4},{1,5},{2,6},{3,7},{4,8},{5,9},{6,10},{7,11},{8,12},{9,13},{1... | collective-permute-start | bytes 3080 | tf_op jit(solution)/shard_map/ppermute | solution.py:132
  237.3 10.2 %collective-permute-start.14 = (f32[256]{0:T(256)S(1)}, f32[256]{0:T(256)S(1)}, u32[]{:S(2)}, u32[]{:S(2)}) collective-permute-start(f32[256]{0:T(256)S(1)} %get-tuple-element.29), channel_id=1, source_target_pairs={{0,5},{1,4},{2,7},{3,6},{4,9},{5,8},{6,11},{7,10},{8,13},{9,12},{1... | collective-permute-start | bytes 3080 | tf_op jit(solution)/shard_map/ppermute | solution.py:133
  247.6 5.6 %collective-permute-start.11 = (f32[256]{0:T(256)S(1)}, f32[256]{0:T(256)S(1)}, u32[]{:S(2)}, u32[]{:S(2)}) collective-permute-start(f32[256]{0:T(256)S(1)} %get-tuple-element.30), channel_id=1, source_target_pairs={{0,2},{1,3},{2,4},{3,5},{4,6},{5,7},{6,8},{7,9},{8,10},{9,11},{10,... | collective-permute-start | bytes 3080 | tf_op jit(solution)/shard_map/ppermute | solution.py:132
  253.6 0.8 collective-permute-done.11
  254.4 4.7 %collective-permute-done.12 = f32[256]{0:T(256)S(1)} collective-permute-done((f32[256]{0:T(256)S(1)}, f32[256]{0:T(256)S(1)}, u32[]{:S(2)}, u32[]{:S(2)}) %collective-permute-start.12) | collective-permute-done | bytes 1056 | tf_op jit(solution)/shard_map/ppermute | solution.py:133
  259.2 1.6 rsqrt_multiply_fusion
  (48 shorter events, 12.1 us)
Async XLA Ops:
  3.3 13.0 %copy-start.1 = (s32[4096]{0:T(1024)S(1)}, s32[4096]{0:T(1024)}, u32[]{:S(2)}) copy-start(s32[4096]{0:T(1024)} %param.4) | copy-start | bytes 49156
  3.3 13.1 %collective-permute-start = (bf16[239,4096]{1,0:T(8,128)(2,1)}, bf16[239,4096]{1,0:T(8,128)(2,1)}, u32[]{:S(2)}, u32[]{:S(2)}) collective-permute-start(bf16[239,4096]{1,0:T(8,128)(2,1)} %slice.186), channel_id=1, source_target_pairs={{14,16},{30,32},{46,48},{62,64},{78,80},{94,96},{110,112},{15,17},... | collective-permute-start | bytes 5873672 | tf_op jit(solution)/shard_map/ppermute | solution.py:76
  5.4 45.9 %collective-permute-start.1 = (bf16[239,4096]{1,0:T(8,128)(2,1)}, bf16[239,4096]{1,0:T(8,128)(2,1)S(1)}, u32[]{:S(2)}, u32[]{:S(2)}) collective-permute-start(bf16[239,4096]{1,0:T(8,128)(2,1)} %slice.186), channel_id=1, source_target_pairs={{0,2},{2,4},{4,6},{6,8},{8,10},{10,12},{12,14},{14,0},{1,3},{3,5},... | collective-permute-start | bytes 5873672 | tf_op jit(solution)/shard_map/ppermute | solution.py:75
  7.0 137.0 %collective-permute-start.4 = (bf16[512,4096]{1,0:T(8,128)(2,1)}, bf16[512,4096]{1,0:T(8,128)(2,1)}, u32[]{:S(2)}, u32[]{:S(2)}) collective-permute-start(bf16[512,4096]{1,0:T(8,128)(2,1)} %param.3), channel_id=1, source_target_pairs={{0,14},{2,0},{4,2},{6,4},{8,6},{10,8},{12,10},{14,12},{1,15},{3,1}... | collective-permute-start | bytes 12582920 | tf_op jit(solution)/shard_map/ppermute | solution.py:78
  7.5 63.3 %collective-permute-start.3 = (bf16[239,4096]{1,0:T(8,128)(2,1)}, bf16[239,4096]{1,0:T(8,128)(2,1)}, u32[]{:S(2)}, u32[]{:S(2)}) collective-permute-start(bf16[239,4096]{1,0:T(8,128)(2,1)} %slice.186), channel_id=1, source_target_pairs={{14,30},{30,46},{46,62},{62,78},{78,94},{94,110},{110,126},{15,31}... | collective-permute-start | bytes 5873672 | tf_op jit(solution)/shard_map/ppermute | solution.py:79
  12.7 87.9 %collective-permute-start.2 = (bf16[273,4096]{1,0:T(8,128)(2,1)}, bf16[273,4096]{1,0:T(8,128)(2,1)}, u32[]{:S(2)}, u32[]{:S(2)}) collective-permute-start(bf16[273,4096]{1,0:T(8,128)(2,1)} %slice.207), channel_id=1, source_target_pairs={{0,2},{2,4},{4,6},{6,8},{8,10},{10,12},{12,14},{14,0},{1,3},{3,5},... | collective-permute-start | bytes 6709256 | tf_op jit(solution)/shard_map/ppermute | solution.py:77
  16.4 35.1 %copy-start = (bf16[512,4096]{1,0:T(8,128)(2,1)S(1)}, bf16[512,4096]{1,0:T(8,128)(2,1)}, u32[]{:S(2)}) copy-start(bf16[512,4096]{1,0:T(8,128)(2,1)} %param.3) | copy-start | bytes 12582916
  66.6 74.9 %collective-permute-start.6 = (bf16[239,4096]{1,0:T(8,128)(2,1)S(1)}, bf16[239,4096]{1,0:T(8,128)(2,1)S(1)}, u32[]{:S(2)}, u32[]{:S(2)}) collective-permute-start(bf16[239,4096]{1,0:T(8,128)(2,1)S(1)} %broadcast_select_fusion.1), channel_id=1, source_target_pairs={{0,2},{2,4},{4,6},{6,8},{8,10},{10,12},{12,14},{14,0},{1,3},{3,5},... | collective-permute-start | bytes 5873672 | tf_op jit(solution)/shard_map/ppermute | solution.py:84
  175.3 17.0 %collective-permute-start.7 = (f32[512,256]{1,0:T(8,128)}, f32[512,256]{1,0:T(8,128)}, u32[]{:S(2)}, u32[]{:S(2)}) collective-permute-start(f32[512,256]{1,0:T(8,128)} %constant_dynamic-slice_fusion.2), channel_id=1, source_target_pairs={{0,1},{1,0},{2,3},{3,2},{4,5},{5,4},{6,7},{7,6},{8,9},{9,8},{10,11... | collective-permute-start | bytes 1572872 | tf_op jit(solution)/shard_map/ppermute | solution.py:104
  180.0 33.0 %collective-permute-start.5 = (f32[512,256]{1,0:T(8,128)}, f32[512,256]{1,0:T(8,128)}, u32[]{:S(2)}, u32[]{:S(2)}) collective-permute-start(f32[512,256]{1,0:T(8,128)} %constant_dynamic-slice_fusion.3), channel_id=1, source_target_pairs={{0,1},{1,0},{2,3},{3,2},{4,5},{5,4},{6,7},{7,6},{8,9},{9,8},{10,11... | collective-permute-start | bytes 1572872 | tf_op jit(solution)/shard_map/ppermute | solution.py:104
  181.5 32.7 %collective-permute-start.8 = (f32[512,256]{1,0:T(8,128)}, f32[512,256]{1,0:T(8,128)S(1)}, u32[]{:S(2)}, u32[]{:S(2)}) collective-permute-start(f32[512,256]{1,0:T(8,128)} %get-tuple-element.26), channel_id=1, source_target_pairs={{0,2},{1,3},{2,4},{3,5},{4,6},{5,7},{6,8},{7,9},{8,10},{9,11},{10,... | collective-permute-start | bytes 1572872 | tf_op jit(solution)/shard_map/ppermute | solution.py:121
  184.8 29.4 %collective-permute-start.9 = (f32[512,256]{1,0:T(8,128)}, f32[512,256]{1,0:T(8,128)S(1)}, u32[]{:S(2)}, u32[]{:S(2)}) collective-permute-start(f32[512,256]{1,0:T(8,128)} %get-tuple-element.25), channel_id=1, source_target_pairs={{0,3},{1,2},{2,5},{3,4},{4,7},{5,6},{6,9},{7,8},{8,11},{9,10},{10,... | collective-permute-start | bytes 1572872 | tf_op jit(solution)/shard_map/ppermute | solution.py:122
  214.6 44.5 %collective-permute-start.10 = (f32[512]{0:T(512)S(1)}, f32[512]{0:T(512)S(1)}, u32[]{:S(2)}, u32[]{:S(2)}) collective-permute-start(f32[512]{0:T(512)S(1)} %fusion.18), channel_id=1, source_target_pairs={{0,1},{1,0},{2,3},{3,2},{4,5},{5,4},{6,7},{7,6},{8,9},{9,8},{10,11... | collective-permute-start | bytes 6152 | tf_op jit(solution)/shard_map/ppermute | solution.py:129
  218.1 35.5 %collective-permute-start.13 = (f32[256]{0:T(256)S(1)}, f32[256]{0:T(256)S(1)}, u32[]{:S(2)}, u32[]{:S(2)}) collective-permute-start(f32[256]{0:T(256)S(1)} %get-tuple-element.30), channel_id=1, source_target_pairs={{0,4},{1,5},{2,6},{3,7},{4,8},{5,9},{6,10},{7,11},{8,12},{9,13},{1... | collective-permute-start | bytes 3080 | tf_op jit(solution)/shard_map/ppermute | solution.py:132
  237.3 16.3 %collective-permute-start.14 = (f32[256]{0:T(256)S(1)}, f32[256]{0:T(256)S(1)}, u32[]{:S(2)}, u32[]{:S(2)}) collective-permute-start(f32[256]{0:T(256)S(1)} %get-tuple-element.29), channel_id=1, source_target_pairs={{0,5},{1,4},{2,7},{3,6},{4,9},{5,8},{6,11},{7,10},{8,13},{9,12},{1... | collective-permute-start | bytes 3080 | tf_op jit(solution)/shard_map/ppermute | solution.py:133
  247.6 6.9 %collective-permute-start.11 = (f32[256]{0:T(256)S(1)}, f32[256]{0:T(256)S(1)}, u32[]{:S(2)}, u32[]{:S(2)}) collective-permute-start(f32[256]{0:T(256)S(1)} %get-tuple-element.30), channel_id=1, source_target_pairs={{0,2},{1,3},{2,4},{3,5},{4,6},{5,7},{6,8},{7,9},{8,10},{9,11},{10,... | collective-permute-start | bytes 3080 | tf_op jit(solution)/shard_map/ppermute | solution.py:132
  253.1 6.0 %collective-permute-start.12 = (f32[256]{0:T(256)S(1)}, f32[256]{0:T(256)S(1)}, u32[]{:S(2)}, u32[]{:S(2)}) collective-permute-start(f32[256]{0:T(256)S(1)} %get-tuple-element.29), channel_id=1, source_target_pairs={{0,3},{1,2},{2,5},{3,4},{4,7},{5,6},{6,9},{7,8},{8,11},{9,10},{10,... | collective-permute-start | bytes 3080 | tf_op jit(solution)/shard_map/ppermute | solution.py:133

commit v5 on v4

--- a/solution.py
+++ b/solution.py
@@ -103,7 +103,6 @@
         theirs = lax.dynamic_slice_in_dim(band, other_col, column_width, 1)
         return mine + lax.ppermute(theirs, "space", swap)
 
-    band0_part, early1, early2, early_sq = lax.optimization_barrier((band0_part, early1, early2, early_sq))
     band0 = space_sum(band0_part)
     prev_late = hist_prev * mask
     band1 = space_sum(lagged_split(own_rows, prev_late, early1, early_sq))

time: 264 us -> 264 us (level)
  the two profiles are of different devices: /device:TPU:28 before, /device:TPU:98 now
where the time goes in v5:
time: 264 us; the launch traced here: 261 us
  waiting for transfers between devices  132 us (50%)
  starting transfers between devices  56.1 us (21%)
  other arithmetic  32.1 us (12%)
  matrix products  24.5 us (9%)
  local copies, waits for them, and re-layouts  14.4 us (5%)
    ppermute x1, waiting for transfers between devices, per_device(): tail_prev = lax.ppermute(tail, 'col', up)  36.6 us
    ppermute x1, waiting for transfers between devices, per_device(): hist_prev = lax.ppermute(hist_send, 'col', up)  32.7 us
    ppermute x1, waiting for transfers between devices, per_device(): head_prev = lax.ppermute(head, 'col', up)  31.4 us
    ppermute x2, waiting for transfers between devices, space_sum(): return mine + lax.ppermute(theirs, 'space', swap)  24.3 us
    ppermute x2, starting transfers between devices, per_device(): lax.ppermute(lax.dynamic_slice_in_dim(part_degree, start_col, column_widt...  19.2 us
    dot_general x4, matrix products, gram(): lax.dot_general(rows, cols, (((1,), (1,)), ((), ())), preferred_element_t...  19 us
    add x20, other arithmetic, combine_lags(): return earlier[-keep:, -keep:] + later[:keep, :keep]  14 us
    ppermute x1, starting transfers between devices, per_device(): lax.ppermute(lax.dynamic_slice_in_dim(band2_next, other_col, column_width...  13 us
  transfers between devices with their start and end apart: 15, of which 7 were waited for; matrix products, arithmetic and copies ran while one was open for 25% of the time, Pallas kernels for 0%

profile of v5, /device:TPU:98, one launch (start us, length us, event | category | flops | bytes accessed | tf_op | source)
XLA Modules:
  0.0 260.8 jit_solution(2527397726665559693)
XLA Ops:
  0.0 3.3 %slice.186 = bf16[239,4096]{1,0:T(8,128)(2,1)} slice(bf16[512,4096]{1,0:T(8,128)(2,1)} %param.3), slice={[273:512], [0:4096]} | slice | bytes 3915776 | tf_op jit(solution)/shard_map/slice | solution.py:67
  3.3 1.6 collective-permute-start.1
  4.9 1.9 collective-permute-start
  6.9 2.6 collective-permute-start.7
  9.4 1.9 collective-permute-start.6
  11.4 3.4 %slice.207 = bf16[273,4096]{1,0:T(8,128)(2,1)} slice(bf16[512,4096]{1,0:T(8,128)(2,1)} %param.3), slice={[0:273], [0:4096]} | slice | bytes 4472832 | tf_op jit(solution)/shard_map/slice | solution.py:68
  14.8 36.6 %collective-permute-done.1 = bf16[239,4096]{1,0:T(8,128)(2,1)S(1)} collective-permute-done((bf16[239,4096]{1,0:T(8,128)(2,1)}, bf16[239,4096]{1,0:T(8,128)(2,1)S(1)}, u32[]{:S(2)}, u32[]{:S(2)}) %collective-permute-start.1) | collective-permute-done | bytes 1957920 | tf_op jit(solution)/shard_map/ppermute | solution.py:75
  51.6 3.2 %multiply_reduce_fusion.1 = f32[751]{0:T(1024)S(1)} fusion(bf16[4096]{0:T(1024)(128)(2,1)S(1)} %convert_element_type.18, bf16[512,4096]{1,0:T(8,128)(2,1)S(1)} %copy-done, bf16[239,4096]{1,0:T(8,128)(2,1)S(1)} %broadcast_select_fusion.1), kind=kLoop, calls=%fused_computation.1 | loop fusion | flops 24608016 | bytes 6163388 | tf_op jit(solution)/shard_map/reduce_sum | solution.py:35
  54.8 5.5 %multiply_subtract_fusion = f32[751,751]{1,0:T(8,128)S(1)} fusion(f32[751]{0:T(1024)S(1)} %multiply_reduce_fusion.1, bf16[512,4096]{1,0:T(8,128)(2,1)S(1)} %copy-done, bf16[239,4096]{1,0:T(8,128)(2,1)S(1)} %broadcast_select_fusion.1, bf16[4096]{0:T(1024)(128)(2,1)S(1)} %convert_element_type.18), kind=kOutput, calls=%fused_computation.17 | convolution fusion | flops 4640445440 | bytes 8419392 | tf_op jit(solution)/shard_map/dot_general | solution.py:39
  60.3 0.9 slice_add_fusion.5
  61.2 0.8 slice_add_fusion.4
  62.0 0.8 slice_add_fusion.8
  62.9 0.7 slice_add_fusion.11
  63.5 0.6 slice_add_fusion.14
  66.8 0.9 constant_dynamic-slice_fusion.3
  67.7 1.1 collective-permute-start.2
  69.3 31.4 %collective-permute-done.4 = bf16[273,4096]{1,0:T(8,128)(2,1)} collective-permute-done((bf16[273,4096]{1,0:T(8,128)(2,1)}, bf16[273,4096]{1,0:T(8,128)(2,1)}, u32[]{:S(2)}, u32[]{:S(2)}) %collective-permute-start.4) | collective-permute-done | bytes 2236448 | tf_op jit(solution)/shard_map/ppermute | solution.py:77
  100.7 3.1 %multiply_reduce_fusion.2 = f32[512]{0:T(512)S(1)} fusion(bf16[4096]{0:T(1024)(128)(2,1)S(1)} %convert_element_type.18, bf16[239,4096]{1,0:T(8,128)(2,1)S(1)} %collective-permute-done.1, bf16[273,4096]{1,0:T(8,128)(2,1)} %collective-permute-done.4), kind=kLoop, calls=%fused_computation.2 | loop fusion | flops 16776704 | bytes 4204544 | tf_op jit(solution)/shard_map/reduce_sum | solution.py:35
  103.8 5.0 %fusion.14 = f32[751,512]{1,0:T(8,128)S(1)} fusion(bf16[239,4096]{1,0:T(8,128)(2,1)S(1)} %collective-permute-done.1, bf16[273,4096]{1,0:T(8,128)(2,1)} %collective-permute-done.4, bf16[4096]{0:T(1024)(128)(2,1)S(1)} %convert_element_type.18, bf16[512,4096]{1,0:T(8,128)(2,1)S(1)} %copy-done, bf16[239,4096]{1,0:T(8,128)(2,1)S(1)} %broadcast_select_fusion.1), kind=kOutput, calls=%fused_computation.58 | convolution fusion | flops 3180961792 | bytes 11892736 | tf_op jit(solution)/shard_map/dot_general | solution.py:47
  108.9 32.7 %collective-permute-done.3 = bf16[239,4096]{1,0:T(8,128)(2,1)S(1)} collective-permute-done((bf16[239,4096]{1,0:T(8,128)(2,1)S(1)}, bf16[239,4096]{1,0:T(8,128)(2,1)S(1)}, u32[]{:S(2)}, u32[]{:S(2)}) %collective-permute-start.3) | collective-permute-done | bytes 1957920 | tf_op jit(solution)/shard_map/ppermute | solution.py:84
  142.3 1.9 fusion.6
  144.2 4.7 %multiply_reduce_fusion = f32[751]{0:T(1024)S(1)} fusion(bf16[4096]{0:T(1024)(128)(2,1)S(1)} %convert_element_type.18, bf16[512,4096]{1,0:T(8,128)(2,1)} %collective-permute-done.7, bf16[239,4096]{1,0:T(8,128)(2,1)S(1)} %broadcast_select_fusion), kind=kLoop, calls=%fused_computation | loop fusion | flops 24608016 | bytes 6163388 | tf_op jit(solution)/shard_map/reduce_sum | solution.py:35
  148.9 5.8 %fusion.4 = f32[751,239]{1,0:T(8,128)S(1)} fusion(bf16[239,4096]{1,0:T(8,128)(2,1)S(1)} %collective-permute-done.3, bf16[4096]{0:T(1024)(128)(2,1)S(1)} %convert_element_type.18, bf16[512,4096]{1,0:T(8,128)(2,1)} %collective-permute-done.7, bf16[239,4096]{1,0:T(8,128)(2,1)S(1)} %broadcast_select_fusion), kind=kOutput, calls=%fused_computation.36 | convolution fusion | flops 1489809408 | bytes 8836228 | tf_op jit(solution)/shard_map/dot_general | solution.py:47
  154.6 6.3 %fusion.13 = f32[751,512]{1,0:T(8,128)S(1)} fusion(bf16[512,4096]{1,0:T(8,128)(2,1)} %collective-permute-done.7, bf16[239,4096]{1,0:T(8,128)(2,1)S(1)} %broadcast_select_fusion, bf16[4096]{0:T(1024)(128)(2,1)S(1)} %convert_element_type.18, bf16[239,4096]{1,0:T(8,128)(2,1)S(1)} %collective-permute-done.1, bf16[273,4096]{1,0:T(8,128)(2,1)} %collective-permute-done.4), kind=kOutput, calls=%fused_computation.57 | convolution fusion | flops 3180961792 | bytes 11892736 | tf_op jit(solution)/shard_map/dot_general | solution.py:47
  161.0 1.4 fusion
  162.4 1.3 slice_add_fusion.1
  163.7 0.8 slice_add_fusion.2
  164.5 0.8 slice_add_fusion.7
  165.4 0.7 slice_add_fusion.10
  166.0 0.6 slice_add_fusion.13
  168.9 0.9 slice_add_fusion
  170.0 0.8 slice_add_fusion.6
  170.8 0.7 slice_add_fusion.9
  171.5 0.6 slice_add_fusion.12
  174.7 0.8 constant_dynamic-slice_fusion.2
  176.4 1.1 constant_dynamic-slice_fusion
  177.5 13.0 %collective-permute-start.9 = (f32[512,256]{1,0:T(8,128)}, f32[512,256]{1,0:T(8,128)S(1)}, u32[]{:S(2)}, u32[]{:S(2)}) collective-permute-start(f32[512,256]{1,0:T(8,128)} %get-tuple-element.17), channel_id=1, source_target_pairs={{0,3},{1,2},{2,5},{3,4},{4,7},{5,6},{6,9},{7,8},{8,11},{9,10},{10,... | collective-permute-start | bytes 1572872 | tf_op jit(solution)/shard_map/ppermute | solution.py:121
  191.1 5.9 %collective-permute-done.2 = f32[512,256]{1,0:T(8,128)} collective-permute-done((f32[512,256]{1,0:T(8,128)}, f32[512,256]{1,0:T(8,128)}, u32[]{:S(2)}, u32[]{:S(2)}) %collective-permute-start.2) | collective-permute-done | bytes 524320 | tf_op jit(solution)/shard_map/ppermute | solution.py:104
  197.0 1.2 add_bitcast_fusion.2
  198.2 18.4 %collective-permute-done.5 = f32[512,256]{1,0:T(8,128)} collective-permute-done((f32[512,256]{1,0:T(8,128)}, f32[512,256]{1,0:T(8,128)}, u32[]{:S(2)}, u32[]{:S(2)}) %collective-permute-start.5) | collective-permute-done | bytes 524320 | tf_op jit(solution)/shard_map/ppermute | solution.py:104
  216.6 1.2 add_bitcast_fusion.1
  218.2 3.0 %collective-permute-start.10 = (f32[512]{0:T(512)S(1)}, f32[512]{0:T(512)S(1)}, u32[]{:S(2)}, u32[]{:S(2)}) collective-permute-start(f32[512]{0:T(512)S(1)} %fusion.18), channel_id=1, source_target_pairs={{0,1},{1,0},{2,3},{3,2},{4,5},{5,4},{6,7},{7,6},{8,9},{9,8},{10,11... | collective-permute-start | bytes 6152 | tf_op jit(solution)/shard_map/ppermute | solution.py:128
  221.3 8.9 %collective-permute-start.11 = (f32[256]{0:T(256)S(1)}, f32[256]{0:T(256)S(1)}, u32[]{:S(2)}, u32[]{:S(2)}) collective-permute-start(f32[256]{0:T(256)S(1)} %get-tuple-element.22), channel_id=1, source_target_pairs={{0,2},{1,3},{2,4},{3,5},{4,6},{5,7},{6,8},{7,9},{8,10},{9,11},{10,... | collective-permute-start | bytes 3080 | tf_op jit(solution)/shard_map/ppermute | solution.py:131
  230.2 11.2 %collective-permute-start.12 = (f32[256]{0:T(256)S(1)}, f32[256]{0:T(256)S(1)}, u32[]{:S(2)}, u32[]{:S(2)}) collective-permute-start(f32[256]{0:T(256)S(1)} %get-tuple-element.21), channel_id=1, source_target_pairs={{0,3},{1,2},{2,5},{3,4},{4,7},{5,6},{6,9},{7,8},{8,11},{9,10},{10,... | collective-permute-start | bytes 3080 | tf_op jit(solution)/shard_map/ppermute | solution.py:132
  241.5 10.2 %collective-permute-start.13 = (f32[256]{0:T(256)S(1)}, f32[256]{0:T(256)S(1)}, u32[]{:S(2)}, u32[]{:S(2)}) collective-permute-start(f32[256]{0:T(256)S(1)} %get-tuple-element.22), channel_id=1, source_target_pairs={{0,4},{1,5},{2,6},{3,7},{4,8},{5,9},{6,10},{7,11},{8,12},{9,13},{1... | collective-permute-start | bytes 3080 | tf_op jit(solution)/shard_map/ppermute | solution.py:131
  251.7 1.3 collective-permute-done.13
  253.0 5.9 %collective-permute-done.14 = f32[256]{0:T(256)S(1)} collective-permute-done((f32[256]{0:T(256)S(1)}, f32[256]{0:T(256)S(1)}, u32[]{:S(2)}, u32[]{:S(2)}) %collective-permute-start.14) | collective-permute-done | bytes 1056 | tf_op jit(solution)/shard_map/ppermute | solution.py:132
  259.0 1.6 rsqrt_multiply_fusion
  (48 shorter events, 10.3 us)
Async XLA Ops:
  3.3 11.4 %copy-start.1 = (s32[4096]{0:T(1024)S(1)}, s32[4096]{0:T(1024)}, u32[]{:S(2)}) copy-start(s32[4096]{0:T(1024)} %param.4) | copy-start | bytes 49156
  3.3 48.0 %collective-permute-start.1 = (bf16[239,4096]{1,0:T(8,128)(2,1)}, bf16[239,4096]{1,0:T(8,128)(2,1)S(1)}, u32[]{:S(2)}, u32[]{:S(2)}) collective-permute-start(bf16[239,4096]{1,0:T(8,128)(2,1)} %slice.186), channel_id=1, source_target_pairs={{0,2},{2,4},{4,6},{6,8},{8,10},{10,12},{12,14},{14,0},{1,3},{3,5},... | collective-permute-start | bytes 5873672 | tf_op jit(solution)/shard_map/ppermute | solution.py:75
  4.9 46.4 %collective-permute-start = (bf16[239,4096]{1,0:T(8,128)(2,1)}, bf16[239,4096]{1,0:T(8,128)(2,1)}, u32[]{:S(2)}, u32[]{:S(2)}) collective-permute-start(bf16[239,4096]{1,0:T(8,128)(2,1)} %slice.186), channel_id=1, source_target_pairs={{14,16},{30,32},{46,48},{62,64},{78,80},{94,96},{110,112},{15,17},... | collective-permute-start | bytes 5873672 | tf_op jit(solution)/shard_map/ppermute | solution.py:76
  6.9 137.3 %collective-permute-start.7 = (bf16[512,4096]{1,0:T(8,128)(2,1)}, bf16[512,4096]{1,0:T(8,128)(2,1)}, u32[]{:S(2)}, u32[]{:S(2)}) collective-permute-start(bf16[512,4096]{1,0:T(8,128)(2,1)} %param.3), channel_id=1, source_target_pairs={{0,14},{2,0},{4,2},{6,4},{8,6},{10,8},{12,10},{14,12},{1,15},{3,1}... | collective-permute-start | bytes 12582920 | tf_op jit(solution)/shard_map/ppermute | solution.py:78
  9.4 59.3 %collective-permute-start.6 = (bf16[239,4096]{1,0:T(8,128)(2,1)}, bf16[239,4096]{1,0:T(8,128)(2,1)}, u32[]{:S(2)}, u32[]{:S(2)}) collective-permute-start(bf16[239,4096]{1,0:T(8,128)(2,1)} %slice.186), channel_id=1, source_target_pairs={{14,30},{30,46},{46,62},{62,78},{78,94},{94,110},{110,126},{15,31}... | collective-permute-start | bytes 5873672 | tf_op jit(solution)/shard_map/ppermute | solution.py:79
  14.7 86.0 %collective-permute-start.4 = (bf16[273,4096]{1,0:T(8,128)(2,1)}, bf16[273,4096]{1,0:T(8,128)(2,1)}, u32[]{:S(2)}, u32[]{:S(2)}) collective-permute-start(bf16[273,4096]{1,0:T(8,128)(2,1)} %slice.207), channel_id=1, source_target_pairs={{0,2},{2,4},{4,6},{6,8},{8,10},{10,12},{12,14},{14,0},{1,3},{3,5},... | collective-permute-start | bytes 6709256 | tf_op jit(solution)/shard_map/ppermute | solution.py:77
  14.8 36.8 %copy-start = (bf16[512,4096]{1,0:T(8,128)(2,1)S(1)}, bf16[512,4096]{1,0:T(8,128)(2,1)}, u32[]{:S(2)}) copy-start(bf16[512,4096]{1,0:T(8,128)(2,1)} %param.3) | copy-start | bytes 12582916
  66.7 74.9 %collective-permute-start.3 = (bf16[239,4096]{1,0:T(8,128)(2,1)S(1)}, bf16[239,4096]{1,0:T(8,128)(2,1)S(1)}, u32[]{:S(2)}, u32[]{:S(2)}) collective-permute-start(bf16[239,4096]{1,0:T(8,128)(2,1)S(1)} %broadcast_select_fusion.1), channel_id=1, source_target_pairs={{0,2},{2,4},{4,6},{6,8},{8,10},{10,12},{12,14},{14,0},{1,3},{3,5},... | collective-permute-start | bytes 5873672 | tf_op jit(solution)/shard_map/ppermute | solution.py:84
  67.7 129.3 %collective-permute-start.2 = (f32[512,256]{1,0:T(8,128)}, f32[512,256]{1,0:T(8,128)}, u32[]{:S(2)}, u32[]{:S(2)}) collective-permute-start(f32[512,256]{1,0:T(8,128)} %constant_dynamic-slice_fusion.3), channel_id=1, source_target_pairs={{0,1},{1,0},{2,3},{3,2},{4,5},{5,4},{6,7},{7,6},{8,9},{9,8},{10,11... | collective-permute-start | bytes 1572872 | tf_op jit(solution)/shard_map/ppermute | solution.py:104
  175.5 41.1 %collective-permute-start.5 = (f32[512,256]{1,0:T(8,128)}, f32[512,256]{1,0:T(8,128)}, u32[]{:S(2)}, u32[]{:S(2)}) collective-permute-start(f32[512,256]{1,0:T(8,128)} %constant_dynamic-slice_fusion.2), channel_id=1, source_target_pairs={{0,1},{1,0},{2,3},{3,2},{4,5},{5,4},{6,7},{7,6},{8,9},{9,8},{10,11... | collective-permute-start | bytes 1572872 | tf_op jit(solution)/shard_map/ppermute | solution.py:104
  177.5 40.3 %collective-permute-start.8 = (f32[512,256]{1,0:T(8,128)}, f32[512,256]{1,0:T(8,128)S(1)}, u32[]{:S(2)}, u32[]{:S(2)}) collective-permute-start(f32[512,256]{1,0:T(8,128)} %get-tuple-element.18), channel_id=1, source_target_pairs={{0,2},{1,3},{2,4},{3,5},{4,6},{5,7},{6,8},{7,9},{8,10},{9,11},{10,... | collective-permute-start | bytes 1572872 | tf_op jit(solution)/shard_map/ppermute | solution.py:120
  177.5 40.3 %collective-permute-start.9 = (f32[512,256]{1,0:T(8,128)}, f32[512,256]{1,0:T(8,128)S(1)}, u32[]{:S(2)}, u32[]{:S(2)}) collective-permute-start(f32[512,256]{1,0:T(8,128)} %get-tuple-element.17), channel_id=1, source_target_pairs={{0,3},{1,2},{2,5},{3,4},{4,7},{5,6},{6,9},{7,8},{8,11},{9,10},{10,... | collective-permute-start | bytes 1572872 | tf_op jit(solution)/shard_map/ppermute | solution.py:121
  218.2 40.7 %collective-permute-start.10 = (f32[512]{0:T(512)S(1)}, f32[512]{0:T(512)S(1)}, u32[]{:S(2)}, u32[]{:S(2)}) collective-permute-start(f32[512]{0:T(512)S(1)} %fusion.18), channel_id=1, source_target_pairs={{0,1},{1,0},{2,3},{3,2},{4,5},{5,4},{6,7},{7,6},{8,9},{9,8},{10,11... | collective-permute-start | bytes 6152 | tf_op jit(solution)/shard_map/ppermute | solution.py:128
  221.3 30.4 %collective-permute-start.11 = (f32[256]{0:T(256)S(1)}, f32[256]{0:T(256)S(1)}, u32[]{:S(2)}, u32[]{:S(2)}) collective-permute-start(f32[256]{0:T(256)S(1)} %get-tuple-element.22), channel_id=1, source_target_pairs={{0,2},{1,3},{2,4},{3,5},{4,6},{5,7},{6,8},{7,9},{8,10},{9,11},{10,... | collective-permute-start | bytes 3080 | tf_op jit(solution)/shard_map/ppermute | solution.py:131
  230.2 21.5 %collective-permute-start.12 = (f32[256]{0:T(256)S(1)}, f32[256]{0:T(256)S(1)}, u32[]{:S(2)}, u32[]{:S(2)}) collective-permute-start(f32[256]{0:T(256)S(1)} %get-tuple-element.21), channel_id=1, source_target_pairs={{0,3},{1,2},{2,5},{3,4},{4,7},{5,6},{6,9},{7,8},{8,11},{9,10},{10,... | collective-permute-start | bytes 3080 | tf_op jit(solution)/shard_map/ppermute | solution.py:132
  241.5 11.5 %collective-permute-start.13 = (f32[256]{0:T(256)S(1)}, f32[256]{0:T(256)S(1)}, u32[]{:S(2)}, u32[]{:S(2)}) collective-permute-start(f32[256]{0:T(256)S(1)} %get-tuple-element.22), channel_id=1, source_target_pairs={{0,4},{1,5},{2,6},{3,7},{4,8},{5,9},{6,10},{7,11},{8,12},{9,13},{1... | collective-permute-start | bytes 3080 | tf_op jit(solution)/shard_map/ppermute | solution.py:131
  251.7 7.2 %collective-permute-start.14 = (f32[256]{0:T(256)S(1)}, f32[256]{0:T(256)S(1)}, u32[]{:S(2)}, u32[]{:S(2)}) collective-permute-start(f32[256]{0:T(256)S(1)} %get-tuple-element.21), channel_id=1, source_target_pairs={{0,5},{1,4},{2,7},{3,6},{4,9},{5,8},{6,11},{7,10},{8,13},{9,12},{1... | collective-permute-start | bytes 3080 | tf_op jit(solution)/shard_map/ppermute | solution.py:132

commit v6 on v5

--- a/solution.py
+++ b/solution.py
@@ -105,8 +105,10 @@
 
     band0 = space_sum(band0_part)
     prev_late = hist_prev * mask
-    band1 = space_sum(lagged_split(own_rows, prev_late, early1, early_sq))
-    band2_next = lagged_split(next_rows, prev_late, early2, early_sq)
+    band1_part = lagged_split(own_rows, prev_late, early1, early_sq)
+    band1 = space_sum(band1_part)
+    prev_late_b2, _ = lax.optimization_barrier((prev_late, band1_part))
+    band2_next = lagged_split(next_rows, prev_late_b2, early2, early_sq)
 
     cs = ("col", "space")
 

time: 264 us -> 265 us (level)
  the two profiles are of different devices: /device:TPU:98 before, /device:TPU:38 now
where the time goes in v6:
time: 265 us; the launch traced here: 262 us
  waiting for transfers between devices  125 us (47%)
  starting transfers between devices  62.8 us (24%)
  other arithmetic  33.7 us (13%)
  matrix products  24.3 us (9%)
  local copies, waits for them, and re-layouts  14.6 us (6%)
    ppermute x1, waiting for transfers between devices, per_device(): tail_prev = lax.ppermute(tail, 'col', up)  36.6 us
    ppermute x1, waiting for transfers between devices, per_device(): hist_prev = lax.ppermute(hist_send, 'col', up)  32.3 us
    ppermute x1, waiting for transfers between devices, per_device(): head_prev = lax.ppermute(head, 'col', up)  29.6 us
    ppermute x2, starting transfers between devices, per_device(): lax.ppermute(lax.dynamic_slice_in_dim(part_degree, other_col, column_widt...  27 us
    ppermute x2, waiting for transfers between devices, space_sum(): return mine + lax.ppermute(theirs, 'space', swap)  21.2 us
    dot_general x4, matrix products, gram(): lax.dot_general(rows, cols, (((1,), (1,)), ((), ())), preferred_element_t...  18.8 us
    add x21, other arithmetic, combine_lags(): return earlier[-keep:, -keep:] + later[:keep, :keep]  14.6 us
    ppermute x1, starting transfers between devices, per_device(): lax.ppermute(lax.dynamic_slice_in_dim(band2_next, start_col, column_width...  14.3 us
  transfers between devices with their start and end apart: 15, of which 7 were waited for; matrix products, arithmetic and copies ran while one was open for 26% of the time, Pallas kernels for 0%

profile of v6, /device:TPU:38, one launch (start us, length us, event | category | flops | bytes accessed | tf_op | source)
XLA Modules:
  0.0 261.8 jit_solution(6423819399232988478)
XLA Ops:
  0.0 3.3 %slice.186 = bf16[239,4096]{1,0:T(8,128)(2,1)} slice(bf16[512,4096]{1,0:T(8,128)(2,1)} %param.3), slice={[273:512], [0:4096]} | slice | bytes 3915776 | tf_op jit(solution)/shard_map/slice | solution.py:67
  3.3 1.6 collective-permute-start.1
  4.9 1.9 collective-permute-start
  6.9 1.9 collective-permute-start.6
  8.8 2.6 collective-permute-start.7
  11.4 3.4 %slice.207 = bf16[273,4096]{1,0:T(8,128)(2,1)} slice(bf16[512,4096]{1,0:T(8,128)(2,1)} %param.3), slice={[0:273], [0:4096]} | slice | bytes 4472832 | tf_op jit(solution)/shard_map/slice | solution.py:68
  14.8 36.6 %collective-permute-done.1 = bf16[239,4096]{1,0:T(8,128)(2,1)S(1)} collective-permute-done((bf16[239,4096]{1,0:T(8,128)(2,1)}, bf16[239,4096]{1,0:T(8,128)(2,1)S(1)}, u32[]{:S(2)}, u32[]{:S(2)}) %collective-permute-start.1) | collective-permute-done | bytes 1957920 | tf_op jit(solution)/shard_map/ppermute | solution.py:75
  51.6 3.1 %multiply_reduce_fusion.1 = f32[751]{0:T(1024)S(1)} fusion(bf16[4096]{0:T(1024)(128)(2,1)S(1)} %convert_element_type.20, bf16[512,4096]{1,0:T(8,128)(2,1)S(1)} %copy-done, bf16[239,4096]{1,0:T(8,128)(2,1)S(1)} %broadcast_select_fusion.1), kind=kLoop, calls=%fused_computation.1 | loop fusion | flops 24608016 | bytes 6163388 | tf_op jit(solution)/shard_map/reduce_sum | solution.py:35
  54.7 5.5 %multiply_subtract_fusion = f32[751,751]{1,0:T(8,128)S(1)} fusion(f32[751]{0:T(1024)S(1)} %multiply_reduce_fusion.1, bf16[512,4096]{1,0:T(8,128)(2,1)S(1)} %copy-done, bf16[239,4096]{1,0:T(8,128)(2,1)S(1)} %broadcast_select_fusion.1, bf16[4096]{0:T(1024)(128)(2,1)S(1)} %convert_element_type.20), kind=kOutput, calls=%fused_computation.18 | convolution fusion | flops 4640445440 | bytes 8419392 | tf_op jit(solution)/shard_map/dot_general | solution.py:39
  60.2 0.9 slice_add_fusion.5
  61.0 0.8 slice_add_fusion.4
  61.9 0.8 slice_add_fusion.8
  62.7 0.7 slice_add_fusion.11
  66.6 0.9 constant_dynamic-slice_fusion.3
  67.6 3.0 %collective-permute-start.2 = (f32[512,256]{1,0:T(8,128)}, f32[512,256]{1,0:T(8,128)}, u32[]{:S(2)}, u32[]{:S(2)}) collective-permute-start(f32[512,256]{1,0:T(8,128)} %constant_dynamic-slice_fusion.3), channel_id=1, source_target_pairs={{0,1},{1,0},{2,3},{3,2},{4,5},{5,4},{6,7},{7,6},{8,9},{9,8},{10,11... | collective-permute-start | bytes 1572872 | tf_op jit(solution)/shard_map/ppermute | solution.py:104
  71.1 29.6 %collective-permute-done.4 = bf16[273,4096]{1,0:T(8,128)(2,1)} collective-permute-done((bf16[273,4096]{1,0:T(8,128)(2,1)}, bf16[273,4096]{1,0:T(8,128)(2,1)}, u32[]{:S(2)}, u32[]{:S(2)}) %collective-permute-start.4) | collective-permute-done | bytes 2236448 | tf_op jit(solution)/shard_map/ppermute | solution.py:77
  100.7 3.5 %multiply_reduce_fusion.2 = f32[512]{0:T(512)S(1)} fusion(bf16[4096]{0:T(1024)(128)(2,1)S(1)} %convert_element_type.20, bf16[239,4096]{1,0:T(8,128)(2,1)S(1)} %collective-permute-done.1, bf16[273,4096]{1,0:T(8,128)(2,1)} %collective-permute-done.4), kind=kLoop, calls=%fused_computation.2 | loop fusion | flops 16776704 | bytes 4204544 | tf_op jit(solution)/shard_map/reduce_sum | solution.py:35
  104.2 5.0 %fusion.9 = f32[751,512]{1,0:T(8,128)S(1)} fusion(bf16[239,4096]{1,0:T(8,128)(2,1)S(1)} %collective-permute-done.1, bf16[273,4096]{1,0:T(8,128)(2,1)} %collective-permute-done.4, bf16[4096]{0:T(1024)(128)(2,1)S(1)} %convert_element_type.20, bf16[512,4096]{1,0:T(8,128)(2,1)S(1)} %copy-done, bf16[239,4096]{1,0:T(8,128)(2,1)S(1)} %broadcast_select_fusion.1), kind=kOutput, calls=%fused_computation.55 | convolution fusion | flops 3180961792 | bytes 11892736 | tf_op jit(solution)/shard_map/dot_general | solution.py:47
  109.3 32.3 %collective-permute-done.3 = bf16[239,4096]{1,0:T(8,128)(2,1)S(1)} collective-permute-done((bf16[239,4096]{1,0:T(8,128)(2,1)S(1)}, bf16[239,4096]{1,0:T(8,128)(2,1)S(1)}, u32[]{:S(2)}, u32[]{:S(2)}) %collective-permute-start.3) | collective-permute-done | bytes 1957920 | tf_op jit(solution)/shard_map/ppermute | solution.py:84
  141.6 0.8 multiply_reduce_fusion.4
  142.5 2.0 fusion.14
  144.5 0.7 fusion
  145.2 0.8 slice_add_fusion.3
  146.1 0.8 slice_add_fusion.2
  146.9 0.8 slice_add_fusion.7
  150.0 0.8 slice_add_fusion.16
  151.8 0.8 constant_dynamic-slice_fusion.2
  152.7 3.0 %collective-permute-start.5 = (f32[512,256]{1,0:T(8,128)}, f32[512,256]{1,0:T(8,128)}, u32[]{:S(2)}, u32[]{:S(2)}) collective-permute-start(f32[512,256]{1,0:T(8,128)} %constant_dynamic-slice_fusion.2), channel_id=1, source_target_pairs={{0,1},{1,0},{2,3},{3,2},{4,5},{5,4},{6,7},{7,6},{8,9},{9,8},{10,11... | collective-permute-start | bytes 1572872 | tf_op jit(solution)/shard_map/ppermute | solution.py:104
  156.2 5.5 %fusion.8 = f32[751,239]{1,0:T(8,128)S(1)} fusion(bf16[239,4096]{1,0:T(8,128)(2,1)S(1)} %get-tuple-element.12, bf16[512,4096]{1,0:T(8,128)(2,1)} %collective-permute-done.7, bf16[239,4096]{1,0:T(8,128)(2,1)S(1)} %broadcast_select_fusion, bf16[4096]{0:T(1024)(128)(2,1)S(1)} %convert_element_type.20), kind=kOutput, calls=%fused_computation.54 | convolution fusion | flops 1488830464 | bytes 8836228 | tf_op jit(solution)/shard_map/dot_general | solution.py:47
  161.7 4.7 %multiply_reduce_fusion = f32[751]{0:T(1024)S(1)} fusion(bf16[4096]{0:T(1024)(128)(2,1)S(1)} %convert_element_type.20, bf16[512,4096]{1,0:T(8,128)(2,1)} %collective-permute-done.7, bf16[239,4096]{1,0:T(8,128)(2,1)S(1)} %broadcast_select_fusion), kind=kLoop, calls=%fused_computation | loop fusion | flops 24608016 | bytes 6163388 | tf_op jit(solution)/shard_map/reduce_sum | solution.py:35
  166.4 6.3 %fusion.7 = f32[751,512]{1,0:T(8,128)S(1)} fusion(bf16[512,4096]{1,0:T(8,128)(2,1)} %collective-permute-done.7, bf16[239,4096]{1,0:T(8,128)(2,1)S(1)} %broadcast_select_fusion, bf16[4096]{0:T(1024)(128)(2,1)S(1)} %convert_element_type.20, bf16[239,4096]{1,0:T(8,128)(2,1)S(1)} %collective-permute-done.1, bf16[273,4096]{1,0:T(8,128)(2,1)} %collective-permute-done.4), kind=kOutput, calls=%fused_computation.53 | convolution fusion | flops 3180961792 | bytes 11892736 | tf_op jit(solution)/shard_map/dot_general | solution.py:47
  172.7 0.7 fusion.1
  173.4 0.8 slice_add_fusion.1
  174.3 0.8 slice_add_fusion
  175.1 0.8 slice_add_fusion.6
  179.9 1.2 constant_dynamic-slice_fusion
  181.0 14.3 %collective-permute-start.8 = (f32[512,256]{1,0:T(8,128)}, f32[512,256]{1,0:T(8,128)S(1)}, u32[]{:S(2)}, u32[]{:S(2)}) collective-permute-start(f32[512,256]{1,0:T(8,128)} %get-tuple-element.22), channel_id=1, source_target_pairs={{0,2},{1,3},{2,4},{3,5},{4,6},{5,7},{6,8},{7,9},{8,10},{9,11},{10,... | collective-permute-start | bytes 1572872 | tf_op jit(solution)/shard_map/ppermute | solution.py:122
  196.0 11.2 %collective-permute-done.2 = f32[512,256]{1,0:T(8,128)} collective-permute-done((f32[512,256]{1,0:T(8,128)}, f32[512,256]{1,0:T(8,128)}, u32[]{:S(2)}, u32[]{:S(2)}) %collective-permute-start.2) | collective-permute-done | bytes 524320 | tf_op jit(solution)/shard_map/ppermute | solution.py:104
  207.1 1.1 add_bitcast_fusion.2
  208.3 10.0 %collective-permute-done.5 = f32[512,256]{1,0:T(8,128)} collective-permute-done((f32[512,256]{1,0:T(8,128)}, f32[512,256]{1,0:T(8,128)}, u32[]{:S(2)}, u32[]{:S(2)}) %collective-permute-start.5) | collective-permute-done | bytes 524320 | tf_op jit(solution)/shard_map/ppermute | solution.py:104
  218.3 1.1 add_bitcast_fusion.1
  219.8 1.4 collective-permute-start.10
  221.3 26.7 %collective-permute-start.14 = (f32[256]{0:T(256)S(1)}, f32[256]{0:T(256)S(1)}, u32[]{:S(2)}, u32[]{:S(2)}) collective-permute-start(f32[256]{0:T(256)S(1)} %get-tuple-element.23), channel_id=1, source_target_pairs={{0,5},{1,4},{2,7},{3,6},{4,9},{5,8},{6,11},{7,10},{8,13},{9,12},{1... | collective-permute-start | bytes 3080 | tf_op jit(solution)/shard_map/ppermute | solution.py:134
  248.1 4.9 %collective-permute-start.13 = (f32[256]{0:T(256)S(1)}, f32[256]{0:T(256)S(1)}, u32[]{:S(2)}, u32[]{:S(2)}) collective-permute-start(f32[256]{0:T(256)S(1)} %get-tuple-element.24), channel_id=1, source_target_pairs={{0,4},{1,5},{2,6},{3,7},{4,8},{5,9},{6,10},{7,11},{8,12},{9,13},{1... | collective-permute-start | bytes 3080 | tf_op jit(solution)/shard_map/ppermute | solution.py:133
  253.3 1.2 collective-permute-start.11
  254.5 4.2 %collective-permute-done.12 = f32[256]{0:T(256)S(1)} collective-permute-done((f32[256]{0:T(256)S(1)}, f32[256]{0:T(256)S(1)}, u32[]{:S(2)}, u32[]{:S(2)}) %collective-permute-start.12) | collective-permute-done | bytes 1056 | tf_op jit(solution)/shard_map/ppermute | solution.py:134
  258.7 1.3 collective-permute-done.11
  260.0 1.6 rsqrt_multiply_fusion
  (56 shorter events, 12.6 us)
Async XLA Ops:
  3.3 11.4 %copy-start.3 = (s32[4096]{0:T(1024)S(1)}, s32[4096]{0:T(1024)}, u32[]{:S(2)}) copy-start(s32[4096]{0:T(1024)} %param.4) | copy-start | bytes 49156
  3.3 48.0 %collective-permute-start.1 = (bf16[239,4096]{1,0:T(8,128)(2,1)}, bf16[239,4096]{1,0:T(8,128)(2,1)S(1)}, u32[]{:S(2)}, u32[]{:S(2)}) collective-permute-start(bf16[239,4096]{1,0:T(8,128)(2,1)} %slice.186), channel_id=1, source_target_pairs={{0,2},{2,4},{4,6},{6,8},{8,10},{10,12},{12,14},{14,0},{1,3},{3,5},... | collective-permute-start | bytes 5873672 | tf_op jit(solution)/shard_map/ppermute | solution.py:75
  4.9 46.4 %collective-permute-start = (bf16[239,4096]{1,0:T(8,128)(2,1)}, bf16[239,4096]{1,0:T(8,128)(2,1)}, u32[]{:S(2)}, u32[]{:S(2)}) collective-permute-start(bf16[239,4096]{1,0:T(8,128)(2,1)} %slice.186), channel_id=1, source_target_pairs={{14,16},{30,32},{46,48},{62,64},{78,80},{94,96},{110,112},{15,17},... | collective-permute-start | bytes 5873672 | tf_op jit(solution)/shard_map/ppermute | solution.py:76
  6.9 63.7 %collective-permute-start.6 = (bf16[239,4096]{1,0:T(8,128)(2,1)}, bf16[239,4096]{1,0:T(8,128)(2,1)}, u32[]{:S(2)}, u32[]{:S(2)}) collective-permute-start(bf16[239,4096]{1,0:T(8,128)(2,1)} %slice.186), channel_id=1, source_target_pairs={{14,30},{30,46},{46,62},{62,78},{78,94},{94,110},{110,126},{15,31}... | collective-permute-start | bytes 5873672 | tf_op jit(solution)/shard_map/ppermute | solution.py:79
  8.8 147.4 %collective-permute-start.7 = (bf16[512,4096]{1,0:T(8,128)(2,1)}, bf16[512,4096]{1,0:T(8,128)(2,1)}, u32[]{:S(2)}, u32[]{:S(2)}) collective-permute-start(bf16[512,4096]{1,0:T(8,128)(2,1)} %param.3), channel_id=1, source_target_pairs={{0,14},{2,0},{4,2},{6,4},{8,6},{10,8},{12,10},{14,12},{1,15},{3,1}... | collective-permute-start | bytes 12582920 | tf_op jit(solution)/shard_map/ppermute | solution.py:78
  14.7 86.0 %collective-permute-start.4 = (bf16[273,4096]{1,0:T(8,128)(2,1)}, bf16[273,4096]{1,0:T(8,128)(2,1)}, u32[]{:S(2)}, u32[]{:S(2)}) collective-permute-start(bf16[273,4096]{1,0:T(8,128)(2,1)} %slice.207), channel_id=1, source_target_pairs={{0,2},{2,4},{4,6},{6,8},{8,10},{10,12},{12,14},{14,0},{1,3},{3,5},... | collective-permute-start | bytes 6709256 | tf_op jit(solution)/shard_map/ppermute | solution.py:77
  14.8 36.8 %copy-start = (bf16[512,4096]{1,0:T(8,128)(2,1)S(1)}, bf16[512,4096]{1,0:T(8,128)(2,1)}, u32[]{:S(2)}) copy-start(bf16[512,4096]{1,0:T(8,128)(2,1)} %param.3) | copy-start | bytes 12582916
  66.6 3.9 %copy-start.1 = (f32[512,512]{1,0:T(8,128)}, f32[512,512]{1,0:T(8,128)S(1)}, u32[]{:S(2)}) copy-start(f32[512,512]{1,0:T(8,128)S(1)} %fusion.6) | copy-start | bytes 3145732
  67.6 139.6 %collective-permute-start.2 = (f32[512,256]{1,0:T(8,128)}, f32[512,256]{1,0:T(8,128)}, u32[]{:S(2)}, u32[]{:S(2)}) collective-permute-start(f32[512,256]{1,0:T(8,128)} %constant_dynamic-slice_fusion.3), channel_id=1, source_target_pairs={{0,1},{1,0},{2,3},{3,2},{4,5},{5,4},{6,7},{7,6},{8,9},{9,8},{10,11... | collective-permute-start | bytes 1572872 | tf_op jit(solution)/shard_map/ppermute | solution.py:104
  70.5 71.1 %collective-permute-start.3 = (bf16[239,4096]{1,0:T(8,128)(2,1)S(1)}, bf16[239,4096]{1,0:T(8,128)(2,1)S(1)}, u32[]{:S(2)}, u32[]{:S(2)}) collective-permute-start(bf16[239,4096]{1,0:T(8,128)(2,1)S(1)} %broadcast_select_fusion.1), channel_id=1, source_target_pairs={{0,2},{2,4},{4,6},{6,8},{8,10},{10,12},{12,14},{14,0},{1,3},{3,5},... | collective-permute-start | bytes 5873672 | tf_op jit(solution)/shard_map/ppermute | solution.py:84
  152.7 65.6 %collective-permute-start.5 = (f32[512,256]{1,0:T(8,128)}, f32[512,256]{1,0:T(8,128)}, u32[]{:S(2)}, u32[]{:S(2)}) collective-permute-start(f32[512,256]{1,0:T(8,128)} %constant_dynamic-slice_fusion.2), channel_id=1, source_target_pairs={{0,1},{1,0},{2,3},{3,2},{4,5},{5,4},{6,7},{7,6},{8,9},{9,8},{10,11... | collective-permute-start | bytes 1572872 | tf_op jit(solution)/shard_map/ppermute | solution.py:104
  179.8 27.3 %copy-start.2 = (f32[512,512]{1,0:T(8,128)S(1)}, f32[512,512]{1,0:T(8,128)}, u32[]{:S(2)}) copy-start(f32[512,512]{1,0:T(8,128)} %copy-done.1) | copy-start | bytes 3145732
  181.0 38.4 %collective-permute-start.9 = (f32[512,256]{1,0:T(8,128)}, f32[512,256]{1,0:T(8,128)S(1)}, u32[]{:S(2)}, u32[]{:S(2)}) collective-permute-start(f32[512,256]{1,0:T(8,128)} %get-tuple-element.21), channel_id=1, source_target_pairs={{0,3},{1,2},{2,5},{3,4},{4,7},{5,6},{6,9},{7,8},{8,11},{9,10},{10,... | collective-permute-start | bytes 1572872 | tf_op jit(solution)/shard_map/ppermute | solution.py:123
  181.0 38.4 %collective-permute-start.8 = (f32[512,256]{1,0:T(8,128)}, f32[512,256]{1,0:T(8,128)S(1)}, u32[]{:S(2)}, u32[]{:S(2)}) collective-permute-start(f32[512,256]{1,0:T(8,128)} %get-tuple-element.22), channel_id=1, source_target_pairs={{0,2},{1,3},{2,4},{3,5},{4,6},{5,7},{6,8},{7,9},{8,10},{9,11},{10,... | collective-permute-start | bytes 1572872 | tf_op jit(solution)/shard_map/ppermute | solution.py:122
  219.8 40.1 %collective-permute-start.10 = (f32[512]{0:T(512)S(1)}, f32[512]{0:T(512)S(1)}, u32[]{:S(2)}, u32[]{:S(2)}) collective-permute-start(f32[512]{0:T(512)S(1)} %fusion.13), channel_id=1, source_target_pairs={{0,1},{1,0},{2,3},{3,2},{4,5},{5,4},{6,7},{7,6},{8,9},{9,8},{10,11... | collective-permute-start | bytes 6152 | tf_op jit(solution)/shard_map/ppermute | solution.py:130
  221.3 33.1 %collective-permute-start.14 = (f32[256]{0:T(256)S(1)}, f32[256]{0:T(256)S(1)}, u32[]{:S(2)}, u32[]{:S(2)}) collective-permute-start(f32[256]{0:T(256)S(1)} %get-tuple-element.23), channel_id=1, source_target_pairs={{0,5},{1,4},{2,7},{3,6},{4,9},{5,8},{6,11},{7,10},{8,13},{9,12},{1... | collective-permute-start | bytes 3080 | tf_op jit(solution)/shard_map/ppermute | solution.py:134
  248.1 6.4 %collective-permute-start.13 = (f32[256]{0:T(256)S(1)}, f32[256]{0:T(256)S(1)}, u32[]{:S(2)}, u32[]{:S(2)}) collective-permute-start(f32[256]{0:T(256)S(1)} %get-tuple-element.24), channel_id=1, source_target_pairs={{0,4},{1,5},{2,6},{3,7},{4,8},{5,9},{6,10},{7,11},{8,12},{9,13},{1... | collective-permute-start | bytes 3080 | tf_op jit(solution)/shard_map/ppermute | solution.py:133
  253.0 5.7 %collective-permute-start.12 = (f32[256]{0:T(256)S(1)}, f32[256]{0:T(256)S(1)}, u32[]{:S(2)}, u32[]{:S(2)}) collective-permute-start(f32[256]{0:T(256)S(1)} %get-tuple-element.23), channel_id=1, source_target_pairs={{0,3},{1,2},{2,5},{3,4},{4,7},{5,6},{6,9},{7,8},{8,11},{9,10},{10,... | collective-permute-start | bytes 3080 | tf_op jit(solution)/shard_map/ppermute | solution.py:134
  253.3 6.7 %collective-permute-start.11 = (f32[256]{0:T(256)S(1)}, f32[256]{0:T(256)S(1)}, u32[]{:S(2)}, u32[]{:S(2)}) collective-permute-start(f32[256]{0:T(256)S(1)} %get-tuple-element.24), channel_id=1, source_target_pairs={{0,2},{1,3},{2,4},{3,5},{4,6},{5,7},{6,8},{7,9},{8,10},{9,11},{10,... | collective-permute-start | bytes 3080 | tf_op jit(solution)/shard_map/ppermute | solution.py:133

commit v7 on v5

--- a/solution.py
+++ b/solution.py
@@ -120,11 +120,13 @@
     b2_same = lax.ppermute(lax.dynamic_slice_in_dim(band2_next, start_col, column_width, 1), cs, col_shift(1, False))
     b2_cross = lax.ppermute(lax.dynamic_slice_in_dim(band2_next, other_col, column_width, 1), cs, col_shift(1, True))
     band2 = b2_same + b2_cross
-    lagged = jnp.stack([band0, band1, band2])
 
     total_cells = cells_dev * n_space
-    kernel = jnp.exp(-lagged / (LAG * total_cells * spread))
-    part_degree = jnp.sum(kernel, axis=(0, 2))
+    denominator = LAG * total_cells * spread
+    kernel_early = jnp.exp(-jnp.stack([band0, band1]) / denominator)
+    kernel_late = jnp.exp(-band2 / denominator)
+    kernel = jnp.concatenate([kernel_early, kernel_late[None]], axis=0)
+    part_degree = jnp.sum(kernel_early, axis=(0, 2)) + jnp.sum(kernel_late, axis=1)
     degree = part_degree + lax.ppermute(part_degree, "space", swap)
     degree_list = [lax.dynamic_slice_in_dim(degree, start_col, column_width, 0)]
     for offset in range(1, BANDS):

time: 264 us -> 262 us (level)
  the two profiles are of different devices: /device:TPU:98 before, /device:TPU:100 now
where the time goes in v7:
time: 262 us; the launch traced here: 259 us
  waiting for transfers between devices  141 us (54%)
  starting transfers between devices  50.6 us (19%)
  other arithmetic  29.7 us (11%)
  matrix products  24.7 us (9%)
  local copies, waits for them, and re-layouts  11.8 us (5%)
    ppermute x1, waiting for transfers between devices, per_device(): tail_prev = lax.ppermute(tail, 'col', up)  36 us
    ppermute x1, waiting for transfers between devices, per_device(): hist_prev = lax.ppermute(hist_send, 'col', up)  32.7 us
    ppermute x1, waiting for transfers between devices, per_device(): head_prev = lax.ppermute(head, 'col', up)  32.6 us
    ppermute x2, waiting for transfers between devices, space_sum(): return mine + lax.ppermute(theirs, 'space', swap)  32 us
    dot_general x4, matrix products, gram(): lax.dot_general(rows, cols, (((1,), (1,)), ((), ())), preferred_element_t...  19.2 us
    add x20, other arithmetic, combine_lags(): return earlier[-keep:, -keep:] + later[:keep, :keep]  14 us
    ppermute x1, starting transfers between devices, per_device(): lax.ppermute(lax.dynamic_slice_in_dim(band2_next, other_col, column_width...  12.9 us
    ppermute x2, starting transfers between devices, per_device(): lax.ppermute(lax.dynamic_slice_in_dim(part_degree, start_col, column_widt...  12.8 us
  transfers between devices with their start and end apart: 15, of which 7 were waited for; matrix products, arithmetic and copies ran while one was open for 24% of the time, Pallas kernels for 0%

profile of v7, /device:TPU:100, one launch (start us, length us, event | category | flops | bytes accessed | tf_op | source)
XLA Modules:
  0.0 258.7 jit_solution(6975153471921946717)
XLA Ops:
  0.0 3.3 %slice.186 = bf16[239,4096]{1,0:T(8,128)(2,1)} slice(bf16[512,4096]{1,0:T(8,128)(2,1)} %param.3), slice={[273:512], [0:4096]} | slice | bytes 3915776 | tf_op jit(solution)/shard_map/slice | solution.py:67
  3.3 1.6 collective-permute-start.1
  4.9 2.0 collective-permute-start
  6.9 2.6 collective-permute-start.7
  9.4 1.9 collective-permute-start.6
  11.4 3.3 %slice.207 = bf16[273,4096]{1,0:T(8,128)(2,1)} slice(bf16[512,4096]{1,0:T(8,128)(2,1)} %param.3), slice={[0:273], [0:4096]} | slice | bytes 4472832 | tf_op jit(solution)/shard_map/slice | solution.py:68
  15.4 36.0 %collective-permute-done.1 = bf16[239,4096]{1,0:T(8,128)(2,1)S(1)} collective-permute-done((bf16[239,4096]{1,0:T(8,128)(2,1)}, bf16[239,4096]{1,0:T(8,128)(2,1)S(1)}, u32[]{:S(2)}, u32[]{:S(2)}) %collective-permute-start.1) | collective-permute-done | bytes 1957920 | tf_op jit(solution)/shard_map/ppermute | solution.py:75
  51.6 3.1 %multiply_reduce_fusion.1 = f32[751]{0:T(1024)S(1)} fusion(bf16[4096]{0:T(1024)(128)(2,1)S(1)} %convert_element_type.18, bf16[512,4096]{1,0:T(8,128)(2,1)S(1)} %copy-done, bf16[239,4096]{1,0:T(8,128)(2,1)S(1)} %broadcast_select_fusion.1), kind=kLoop, calls=%fused_computation.1 | loop fusion | flops 24608016 | bytes 6163388 | tf_op jit(solution)/shard_map/reduce_sum | solution.py:35
  54.7 5.5 %multiply_subtract_fusion = f32[751,751]{1,0:T(8,128)S(1)} fusion(f32[751]{0:T(1024)S(1)} %multiply_reduce_fusion.1, bf16[512,4096]{1,0:T(8,128)(2,1)S(1)} %copy-done, bf16[239,4096]{1,0:T(8,128)(2,1)S(1)} %broadcast_select_fusion.1, bf16[4096]{0:T(1024)(128)(2,1)S(1)} %convert_element_type.18), kind=kOutput, calls=%fused_computation.17 | convolution fusion | flops 4640445440 | bytes 8419392 | tf_op jit(solution)/shard_map/dot_general | solution.py:39
  60.2 0.9 slice_add_fusion.5
  61.0 0.8 slice_add_fusion.4
  61.9 0.8 slice_add_fusion.8
  62.7 0.7 slice_add_fusion.11
  63.4 0.6 slice_add_fusion.14
  65.0 0.6 slice_add_fusion.17
  66.7 0.8 collective-permute-start.2
  68.1 32.6 %collective-permute-done.4 = bf16[273,4096]{1,0:T(8,128)(2,1)} collective-permute-done((bf16[273,4096]{1,0:T(8,128)(2,1)}, bf16[273,4096]{1,0:T(8,128)(2,1)}, u32[]{:S(2)}, u32[]{:S(2)}) %collective-permute-start.4) | collective-permute-done | bytes 2236448 | tf_op jit(solution)/shard_map/ppermute | solution.py:77
  100.7 3.1 %multiply_reduce_fusion.2 = f32[512]{0:T(512)S(1)} fusion(bf16[4096]{0:T(1024)(128)(2,1)S(1)} %convert_element_type.18, bf16[239,4096]{1,0:T(8,128)(2,1)S(1)} %collective-permute-done.1, bf16[273,4096]{1,0:T(8,128)(2,1)} %collective-permute-done.4), kind=kLoop, calls=%fused_computation.2 | loop fusion | flops 16776704 | bytes 4204544 | tf_op jit(solution)/shard_map/reduce_sum | solution.py:35
  103.8 5.0 %fusion.15 = f32[751,512]{1,0:T(8,128)S(1)} fusion(bf16[239,4096]{1,0:T(8,128)(2,1)S(1)} %collective-permute-done.1, bf16[273,4096]{1,0:T(8,128)(2,1)} %collective-permute-done.4, bf16[4096]{0:T(1024)(128)(2,1)S(1)} %convert_element_type.18, bf16[512,4096]{1,0:T(8,128)(2,1)S(1)} %copy-done, bf16[239,4096]{1,0:T(8,128)(2,1)S(1)} %broadcast_select_fusion.1), kind=kOutput, calls=%fused_computation.59 | convolution fusion | flops 3180961792 | bytes 11892736 | tf_op jit(solution)/shard_map/dot_general | solution.py:47
  108.9 32.7 %collective-permute-done.3 = bf16[239,4096]{1,0:T(8,128)(2,1)S(1)} collective-permute-done((bf16[239,4096]{1,0:T(8,128)(2,1)S(1)}, bf16[239,4096]{1,0:T(8,128)(2,1)S(1)}, u32[]{:S(2)}, u32[]{:S(2)}) %collective-permute-start.3) | collective-permute-done | bytes 1957920 | tf_op jit(solution)/shard_map/ppermute | solution.py:84
  141.6 0.6 multiply_reduce_fusion.3
  142.3 1.9 fusion.5
  144.2 4.7 %multiply_reduce_fusion = f32[751]{0:T(1024)S(1)} fusion(bf16[4096]{0:T(1024)(128)(2,1)S(1)} %convert_element_type.18, bf16[512,4096]{1,0:T(8,128)(2,1)} %collective-permute-done.7, bf16[239,4096]{1,0:T(8,128)(2,1)S(1)} %broadcast_select_fusion), kind=kLoop, calls=%fused_computation | loop fusion | flops 24608016 | bytes 6163388 | tf_op jit(solution)/shard_map/reduce_sum | solution.py:35
  148.8 6.0 %fusion.3 = f32[751,239]{1,0:T(8,128)S(1)} fusion(bf16[239,4096]{1,0:T(8,128)(2,1)S(1)} %collective-permute-done.3, bf16[4096]{0:T(1024)(128)(2,1)S(1)} %convert_element_type.18, bf16[512,4096]{1,0:T(8,128)(2,1)} %collective-permute-done.7, bf16[239,4096]{1,0:T(8,128)(2,1)S(1)} %broadcast_select_fusion), kind=kOutput, calls=%fused_computation.34 | convolution fusion | flops 1489809408 | bytes 8836228 | tf_op jit(solution)/shard_map/dot_general | solution.py:47
  154.9 6.3 %fusion.14 = f32[751,512]{1,0:T(8,128)S(1)} fusion(bf16[512,4096]{1,0:T(8,128)(2,1)} %collective-permute-done.7, bf16[239,4096]{1,0:T(8,128)(2,1)S(1)} %broadcast_select_fusion, bf16[4096]{0:T(1024)(128)(2,1)S(1)} %convert_element_type.18, bf16[239,4096]{1,0:T(8,128)(2,1)S(1)} %collective-permute-done.1, bf16[273,4096]{1,0:T(8,128)(2,1)} %collective-permute-done.4), kind=kOutput, calls=%fused_computation.58 | convolution fusion | flops 3180961792 | bytes 11892736 | tf_op jit(solution)/shard_map/dot_general | solution.py:47
  161.2 1.4 fusion
  162.6 1.3 slice_add_fusion.1
  163.9 0.8 slice_add_fusion.2
  164.7 0.8 slice_add_fusion.7
  165.6 0.7 slice_add_fusion.10
  166.2 0.6 slice_add_fusion.13
  166.9 0.6 slice_add_fusion.16
  169.1 0.9 slice_add_fusion
  170.1 0.8 slice_add_fusion.6
  171.0 0.7 slice_add_fusion.9
  171.6 0.6 slice_add_fusion.12
  172.3 0.6 slice_add_fusion.15
  174.9 0.6 collective-permute-start.5
  176.1 12.9 %collective-permute-start.9 = (f32[512,256]{1,0:T(8,128)S(1)}, f32[512,256]{1,0:T(8,128)S(1)}, u32[]{:S(2)}, u32[]{:S(2)}) collective-permute-start(f32[512,256]{1,0:T(8,128)S(1)} %get-tuple-element.21), channel_id=1, source_target_pairs={{0,3},{1,2},{2,5},{3,4},{4,7},{5,6},{6,9},{7,8},{8,11},{9,10},{10,... | collective-permute-start | bytes 1572872 | tf_op jit(solution)/shard_map/ppermute | solution.py:121
  189.0 10.3 %collective-permute-done.2 = f32[512,256]{1,0:T(8,128)S(1)} collective-permute-done((f32[512,256]{1,0:T(8,128)S(1)}, f32[512,256]{1,0:T(8,128)S(1)}, u32[]{:S(2)}, u32[]{:S(2)}) %collective-permute-start.2) | collective-permute-done | bytes 524320 | tf_op jit(solution)/shard_map/ppermute | solution.py:104
  199.4 21.7 %collective-permute-done.5 = f32[512,256]{1,0:T(8,128)S(1)} collective-permute-done((f32[512,256]{1,0:T(8,128)S(1)}, f32[512,256]{1,0:T(8,128)S(1)}, u32[]{:S(2)}, u32[]{:S(2)}) %collective-permute-start.5) | collective-permute-done | bytes 524320 | tf_op jit(solution)/shard_map/ppermute | solution.py:104
  221.7 4.0 %collective-permute-start.10 = (f32[512]{0:T(512)S(1)}, f32[512]{0:T(512)S(1)}, u32[]{:S(2)}, u32[]{:S(2)}) collective-permute-start(f32[512]{0:T(512)S(1)} %add.203), channel_id=1, source_target_pairs={{0,1},{1,0},{2,3},{3,2},{4,5},{5,4},{6,7},{7,6},{8,9},{9,8},{10,11... | collective-permute-start | bytes 6152 | tf_op jit(solution)/shard_map/ppermute | solution.py:130
  225.8 2.5 collective-permute-start.11
  228.3 11.2 %collective-permute-start.12 = (f32[256]{0:T(256)S(1)}, f32[256]{0:T(256)S(1)}, u32[]{:S(2)}, u32[]{:S(2)}) collective-permute-start(f32[256]{0:T(256)S(1)} %get-tuple-element.25), channel_id=1, source_target_pairs={{0,3},{1,2},{2,5},{3,4},{4,7},{5,6},{6,9},{7,8},{8,11},{9,10},{10,... | collective-permute-start | bytes 3080 | tf_op jit(solution)/shard_map/ppermute | solution.py:134
  239.5 10.2 %collective-permute-start.13 = (f32[256]{0:T(256)S(1)}, f32[256]{0:T(256)S(1)}, u32[]{:S(2)}, u32[]{:S(2)}) collective-permute-start(f32[256]{0:T(256)S(1)} %get-tuple-element.26), channel_id=1, source_target_pairs={{0,4},{1,5},{2,6},{3,7},{4,8},{5,9},{6,10},{7,11},{8,12},{9,13},{1... | collective-permute-start | bytes 3080 | tf_op jit(solution)/shard_map/ppermute | solution.py:133
  249.8 1.3 collective-permute-done.13
  251.1 5.9 %collective-permute-done.14 = f32[256]{0:T(256)S(1)} collective-permute-done((f32[256]{0:T(256)S(1)}, f32[256]{0:T(256)S(1)}, u32[]{:S(2)}, u32[]{:S(2)}) %collective-permute-start.14) | collective-permute-done | bytes 1056 | tf_op jit(solution)/shard_map/ppermute | solution.py:134
  257.1 1.4 fusion.2
  (49 shorter events, 7.8 us)
Async XLA Ops:
  3.3 11.4 %copy-start.1 = (s32[4096]{0:T(1024)S(1)}, s32[4096]{0:T(1024)}, u32[]{:S(2)}) copy-start(s32[4096]{0:T(1024)} %param.4) | copy-start | bytes 49156
  3.3 48.0 %collective-permute-start.1 = (bf16[239,4096]{1,0:T(8,128)(2,1)}, bf16[239,4096]{1,0:T(8,128)(2,1)S(1)}, u32[]{:S(2)}, u32[]{:S(2)}) collective-permute-start(bf16[239,4096]{1,0:T(8,128)(2,1)} %slice.186), channel_id=1, source_target_pairs={{0,2},{2,4},{4,6},{6,8},{8,10},{10,12},{12,14},{14,0},{1,3},{3,5},... | collective-permute-start | bytes 5873672 | tf_op jit(solution)/shard_map/ppermute | solution.py:75
  4.9 46.4 %collective-permute-start = (bf16[239,4096]{1,0:T(8,128)(2,1)}, bf16[239,4096]{1,0:T(8,128)(2,1)}, u32[]{:S(2)}, u32[]{:S(2)}) collective-permute-start(bf16[239,4096]{1,0:T(8,128)(2,1)} %slice.186), channel_id=1, source_target_pairs={{14,16},{30,32},{46,48},{62,64},{78,80},{94,96},{110,112},{15,17},... | collective-permute-start | bytes 5873672 | tf_op jit(solution)/shard_map/ppermute | solution.py:76
  6.9 137.3 %collective-permute-start.7 = (bf16[512,4096]{1,0:T(8,128)(2,1)}, bf16[512,4096]{1,0:T(8,128)(2,1)}, u32[]{:S(2)}, u32[]{:S(2)}) collective-permute-start(bf16[512,4096]{1,0:T(8,128)(2,1)} %param.3), channel_id=1, source_target_pairs={{0,14},{2,0},{4,2},{6,4},{8,6},{10,8},{12,10},{14,12},{1,15},{3,1}... | collective-permute-start | bytes 12582920 | tf_op jit(solution)/shard_map/ppermute | solution.py:78
  9.4 58.2 %collective-permute-start.6 = (bf16[239,4096]{1,0:T(8,128)(2,1)}, bf16[239,4096]{1,0:T(8,128)(2,1)}, u32[]{:S(2)}, u32[]{:S(2)}) collective-permute-start(bf16[239,4096]{1,0:T(8,128)(2,1)} %slice.186), channel_id=1, source_target_pairs={{14,30},{30,46},{46,62},{62,78},{78,94},{94,110},{110,126},{15,31}... | collective-permute-start | bytes 5873672 | tf_op jit(solution)/shard_map/ppermute | solution.py:79
  14.7 86.0 %collective-permute-start.4 = (bf16[273,4096]{1,0:T(8,128)(2,1)}, bf16[273,4096]{1,0:T(8,128)(2,1)}, u32[]{:S(2)}, u32[]{:S(2)}) collective-permute-start(bf16[273,4096]{1,0:T(8,128)(2,1)} %slice.207), channel_id=1, source_target_pairs={{0,2},{2,4},{4,6},{6,8},{8,10},{10,12},{12,14},{14,0},{1,3},{3,5},... | collective-permute-start | bytes 6709256 | tf_op jit(solution)/shard_map/ppermute | solution.py:77
  15.4 36.2 %copy-start = (bf16[512,4096]{1,0:T(8,128)(2,1)S(1)}, bf16[512,4096]{1,0:T(8,128)(2,1)}, u32[]{:S(2)}) copy-start(bf16[512,4096]{1,0:T(8,128)(2,1)} %param.3) | copy-start | bytes 12582916
  66.6 75.0 %collective-permute-start.3 = (bf16[239,4096]{1,0:T(8,128)(2,1)S(1)}, bf16[239,4096]{1,0:T(8,128)(2,1)S(1)}, u32[]{:S(2)}, u32[]{:S(2)}) collective-permute-start(bf16[239,4096]{1,0:T(8,128)(2,1)S(1)} %broadcast_select_fusion.1), channel_id=1, source_target_pairs={{0,2},{2,4},{4,6},{6,8},{8,10},{10,12},{12,14},{14,0},{1,3},{3,5},... | collective-permute-start | bytes 5873672 | tf_op jit(solution)/shard_map/ppermute | solution.py:84
  66.7 132.6 %collective-permute-start.2 = (f32[512,256]{1,0:T(8,128)S(1)}, f32[512,256]{1,0:T(8,128)S(1)}, u32[]{:S(2)}, u32[]{:S(2)}) collective-permute-start(f32[512,256]{1,0:T(8,128)S(1)} %constant_dynamic-slice_fusion.3), channel_id=1, source_target_pairs={{0,1},{1,0},{2,3},{3,2},{4,5},{5,4},{6,7},{7,6},{8,9},{9,8},{10,11... | collective-permute-start | bytes 1572872 | tf_op jit(solution)/shard_map/ppermute | solution.py:104
  174.9 46.2 %collective-permute-start.5 = (f32[512,256]{1,0:T(8,128)S(1)}, f32[512,256]{1,0:T(8,128)S(1)}, u32[]{:S(2)}, u32[]{:S(2)}) collective-permute-start(f32[512,256]{1,0:T(8,128)S(1)} %constant_dynamic-slice_fusion.2), channel_id=1, source_target_pairs={{0,1},{1,0},{2,3},{3,2},{4,5},{5,4},{6,7},{7,6},{8,9},{9,8},{10,11... | collective-permute-start | bytes 1572872 | tf_op jit(solution)/shard_map/ppermute | solution.py:104
  176.0 45.4 %collective-permute-start.8 = (f32[512,256]{1,0:T(8,128)S(1)}, f32[512,256]{1,0:T(8,128)S(1)}, u32[]{:S(2)}, u32[]{:S(2)}) collective-permute-start(f32[512,256]{1,0:T(8,128)S(1)} %get-tuple-element.22), channel_id=1, source_target_pairs={{0,2},{1,3},{2,4},{3,5},{4,6},{5,7},{6,8},{7,9},{8,10},{9,11},{10,... | collective-permute-start | bytes 1572872 | tf_op jit(solution)/shard_map/ppermute | solution.py:120
  176.1 45.4 %collective-permute-start.9 = (f32[512,256]{1,0:T(8,128)S(1)}, f32[512,256]{1,0:T(8,128)S(1)}, u32[]{:S(2)}, u32[]{:S(2)}) collective-permute-start(f32[512,256]{1,0:T(8,128)S(1)} %get-tuple-element.21), channel_id=1, source_target_pairs={{0,3},{1,2},{2,5},{3,4},{4,7},{5,6},{6,9},{7,8},{8,11},{9,10},{10,... | collective-permute-start | bytes 1572872 | tf_op jit(solution)/shard_map/ppermute | solution.py:121
  221.7 35.3 %collective-permute-start.10 = (f32[512]{0:T(512)S(1)}, f32[512]{0:T(512)S(1)}, u32[]{:S(2)}, u32[]{:S(2)}) collective-permute-start(f32[512]{0:T(512)S(1)} %add.203), channel_id=1, source_target_pairs={{0,1},{1,0},{2,3},{3,2},{4,5},{5,4},{6,7},{7,6},{8,9},{9,8},{10,11... | collective-permute-start | bytes 6152 | tf_op jit(solution)/shard_map/ppermute | solution.py:130
  225.8 24.0 %collective-permute-start.11 = (f32[256]{0:T(256)S(1)}, f32[256]{0:T(256)S(1)}, u32[]{:S(2)}, u32[]{:S(2)}) collective-permute-start(f32[256]{0:T(256)S(1)} %get-tuple-element.26), channel_id=1, source_target_pairs={{0,2},{1,3},{2,4},{3,5},{4,6},{5,7},{6,8},{7,9},{8,10},{9,11},{10,... | collective-permute-start | bytes 3080 | tf_op jit(solution)/shard_map/ppermute | solution.py:133
  228.3 21.5 %collective-permute-start.12 = (f32[256]{0:T(256)S(1)}, f32[256]{0:T(256)S(1)}, u32[]{:S(2)}, u32[]{:S(2)}) collective-permute-start(f32[256]{0:T(256)S(1)} %get-tuple-element.25), channel_id=1, source_target_pairs={{0,3},{1,2},{2,5},{3,4},{4,7},{5,6},{6,9},{7,8},{8,11},{9,10},{10,... | collective-permute-start | bytes 3080 | tf_op jit(solution)/shard_map/ppermute | solution.py:134
  239.5 11.5 %collective-permute-start.13 = (f32[256]{0:T(256)S(1)}, f32[256]{0:T(256)S(1)}, u32[]{:S(2)}, u32[]{:S(2)}) collective-permute-start(f32[256]{0:T(256)S(1)} %get-tuple-element.26), channel_id=1, source_target_pairs={{0,4},{1,5},{2,6},{3,7},{4,8},{5,9},{6,10},{7,11},{8,12},{9,13},{1... | collective-permute-start | bytes 3080 | tf_op jit(solution)/shard_map/ppermute | solution.py:133
  249.8 7.2 %collective-permute-start.14 = (f32[256]{0:T(256)S(1)}, f32[256]{0:T(256)S(1)}, u32[]{:S(2)}, u32[]{:S(2)}) collective-permute-start(f32[256]{0:T(256)S(1)} %get-tuple-element.25), channel_id=1, source_target_pairs={{0,5},{1,4},{2,7},{3,6},{4,9},{5,8},{6,11},{7,10},{8,13},{9,12},{1... | collective-permute-start | bytes 3080 | tf_op jit(solution)/shard_map/ppermute | solution.py:134

commit v8 on v7

--- a/solution.py
+++ b/solution.py
@@ -49,11 +49,39 @@
     )
 
 
+def lag_sum_rect(distance, window):
+    rows, cols = distance.shape
+    summed = None
+    summed_w = 0
+    doubled = distance
+    width = 1
+    remaining = window
+    while remaining:
+        if remaining % 2 == 1:
+            if summed is None:
+                summed, summed_w = doubled, width
+            else:
+                r = rows - summed_w - width + 1
+                c = cols - summed_w - width + 1
+                summed = summed[width : width + r, width : width + c] + doubled[:r, :c]
+                summed_w += width
+        remaining = remaining // 2
+        if remaining:
+            r = rows - 2 * width + 1
+            c = cols - 2 * width + 1
+            doubled = doubled[width : width + r, width : width + c] + doubled[:r, :c]
+            width *= 2
+    return summed
+
+
 def lagged_split(rows, late_cols, early_gram, early_sq):
-    gram_tile = jnp.concatenate([gram(rows, late_cols), early_gram], axis=1)
-    col_sq = jnp.concatenate([square_norms(late_cols), early_sq])
-    distance = square_norms(rows)[:, None] + col_sq[None, :] - 2.0 * gram_tile
-    return lag_sum(distance, LAG)
+    row_sq = square_norms(rows)[:, None]
+    early_dist = row_sq + early_sq[None, :] - 2.0 * early_gram
+    late_dist = row_sq + square_norms(late_cols)[None, :] - 2.0 * gram(rows, late_cols)
+    n_late = late_cols.shape[0]
+    right = lag_sum_rect(early_dist, LAG)
+    left = lag_sum_rect(jnp.concatenate([late_dist, early_dist[:, : LAG - 1]], axis=1), LAG)
+    return jnp.concatenate([left[:, :n_late], right], axis=1)
 
 
 def per_device(snapshots, ocean_mask, spread):

time: 262 us -> 262 us (level)
  the two profiles are of different devices: /device:TPU:100 before, /device:TPU:98 now
where the time goes in v8:
time: 262 us; the launch traced here: 258 us
  waiting for transfers between devices  137 us (52%)
  starting transfers between devices  49 us (19%)
  other arithmetic  32.2 us (12%)
  matrix products  24.3 us (9%)
  local copies, waits for them, and re-layouts  14.7 us (6%)
    ppermute x1, waiting for transfers between devices, per_device(): tail_prev = lax.ppermute(tail, 'col', up)  36 us
    ppermute x2, waiting for transfers between devices, space_sum(): return mine + lax.ppermute(theirs, 'space', swap)  33.2 us
    ppermute x1, waiting for transfers between devices, per_device(): head_prev = lax.ppermute(head, 'col', up)  32.8 us
    ppermute x1, waiting for transfers between devices, per_device(): hist_prev = lax.ppermute(hist_send, 'col', up)  27.5 us
    dot_general x4, matrix products, gram(): lax.dot_general(rows, cols, (((1,), (1,)), ((), ())), preferred_element_t...  18.8 us
    ppermute x1, starting transfers between devices, per_device(): lax.ppermute(lax.dynamic_slice_in_dim(band2_next, other_col, column_width...  12.9 us
    add x24, other arithmetic, lag_sum_rect(): doubled = doubled[width:width + r, width:width + c] + doubled[:r, :c]  12.1 us
    reduce_sum x4, other arithmetic, square_norms(): return jnp.sum(jnp.square(values.astype(jnp.float32)), axis=1)  11.9 us
  transfers between devices with their start and end apart: 15, of which 7 were waited for; matrix products, arithmetic and copies ran while one was open for 25% of the time, Pallas kernels for 0%

profile of v8, /device:TPU:98, one launch (start us, length us, event | category | flops | bytes accessed | tf_op | source)
XLA Modules:
  0.0 258.3 jit_solution(3735256573675819797)
XLA Ops:
  0.0 3.3 %slice.312 = bf16[239,4096]{1,0:T(8,128)(2,1)} slice(bf16[512,4096]{1,0:T(8,128)(2,1)} %param.3), slice={[273:512], [0:4096]} | slice | bytes 3915776 | tf_op jit(solution)/shard_map/slice | solution.py:95
  3.3 1.6 collective-permute-start.1
  4.9 1.9 collective-permute-start
  6.9 2.6 collective-permute-start.7
  9.4 1.9 collective-permute-start.6
  11.4 3.3 %slice.333 = bf16[273,4096]{1,0:T(8,128)(2,1)} slice(bf16[512,4096]{1,0:T(8,128)(2,1)} %param.3), slice={[0:273], [0:4096]} | slice | bytes 4472832 | tf_op jit(solution)/shard_map/slice | solution.py:96
  15.4 36.0 %collective-permute-done.1 = bf16[239,4096]{1,0:T(8,128)(2,1)S(1)} collective-permute-done((bf16[239,4096]{1,0:T(8,128)(2,1)}, bf16[239,4096]{1,0:T(8,128)(2,1)S(1)}, u32[]{:S(2)}, u32[]{:S(2)}) %collective-permute-start.1) | collective-permute-done | bytes 1957920 | tf_op jit(solution)/shard_map/ppermute | solution.py:103
  51.6 3.1 %multiply_reduce_fusion.1 = f32[751]{0:T(1024)S(1)} fusion(bf16[4096]{0:T(1024)(128)(2,1)S(1)} %convert_element_type.18, bf16[512,4096]{1,0:T(8,128)(2,1)S(1)} %copy-done, bf16[239,4096]{1,0:T(8,128)(2,1)S(1)} %broadcast_select_fusion.1), kind=kLoop, calls=%fused_computation.1 | loop fusion | flops 24608016 | bytes 6163388 | tf_op jit(solution)/shard_map/reduce_sum | solution.py:35
  54.7 5.5 %multiply_subtract_fusion = f32[751,751]{0,1:T(8,128)S(1)} fusion(f32[751]{0:T(1024)S(1)} %multiply_reduce_fusion.1, bf16[512,4096]{1,0:T(8,128)(2,1)S(1)} %copy-done, bf16[239,4096]{1,0:T(8,128)(2,1)S(1)} %broadcast_select_fusion.1, bf16[4096]{0:T(1024)(128)(2,1)S(1)} %convert_element_type.18), kind=kOutput, calls=%fused_computation.9 | convolution fusion | flops 4640445440 | bytes 8419392 | tf_op jit(solution)/shard_map/dot_general | solution.py:39
  60.2 0.9 slice_add_fusion.1
  61.1 0.8 slice_add_fusion
  61.9 0.8 slice_add_fusion.2
  62.8 0.7 slice_add_fusion.3
  63.4 0.6 slice_add_fusion.4
  65.1 0.6 slice_add_fusion.5
  66.8 0.6 collective-permute-start.2
  67.4 0.5 broadcast_select_fusion
  68.0 32.8 %collective-permute-done.4 = bf16[273,4096]{1,0:T(8,128)(2,1)} collective-permute-done((bf16[273,4096]{1,0:T(8,128)(2,1)}, bf16[273,4096]{1,0:T(8,128)(2,1)}, u32[]{:S(2)}, u32[]{:S(2)}) %collective-permute-start.4) | collective-permute-done | bytes 2236448 | tf_op jit(solution)/shard_map/ppermute | solution.py:105
  100.7 3.5 %multiply_reduce_fusion.2 = f32[512]{0:T(512)S(1)} fusion(bf16[4096]{0:T(1024)(128)(2,1)S(1)} %convert_element_type.18, bf16[239,4096]{1,0:T(8,128)(2,1)S(1)} %collective-permute-done.1, bf16[273,4096]{1,0:T(8,128)(2,1)} %collective-permute-done.4), kind=kLoop, calls=%fused_computation.2 | loop fusion | flops 16776704 | bytes 4204544 | tf_op jit(solution)/shard_map/reduce_sum | solution.py:35
  104.2 5.5 %multiply_subtract_fusion.2 = f32[751,512]{0,1:T(8,128)S(1)} fusion(f32[512]{0:T(512)S(1)} %multiply_reduce_fusion.2, f32[751]{0:T(1024)S(1)} %multiply_reduce_fusion.1, bf16[239,4096]{1,0:T(8,128)(2,1)S(1)} %collective-permute-done.1, bf16[273,4096]{1,0:T(8,128)(2,1)} %collective-permute-done.4, bf16[4096]{0:T(1024)(128)(2,1)S(1)} %convert_element_type.18, ...), kind=kOutput, calls=%fused_computation.25 | convolution fusion | flops 3182115328 | bytes 11897788 | tf_op jit(solution)/shard_map/dot_general | solution.py:47
  109.8 0.6 slice_add_fusion.11
  110.3 0.6 slice_add_fusion.10
  110.9 0.6 slice_add_fusion.9
  114.1 27.5 %collective-permute-done.3 = bf16[239,4096]{1,0:T(8,128)(2,1)S(1)} collective-permute-done((bf16[239,4096]{1,0:T(8,128)(2,1)S(1)}, bf16[239,4096]{1,0:T(8,128)(2,1)S(1)}, u32[]{:S(2)}, u32[]{:S(2)}) %collective-permute-start.3) | collective-permute-done | bytes 1957920 | tf_op jit(solution)/shard_map/ppermute | solution.py:112
  141.6 0.6 multiply_reduce_fusion.3
  142.2 2.2 add_subtract_fusion.1
  145.4 0.5 slice_add_fusion.19
  146.0 0.6 slice_add_fusion.21
  148.9 0.6 collective-permute-start.5
  149.5 4.6 %multiply_reduce_fusion = f32[751]{0:T(1024)S(1)} fusion(bf16[4096]{0:T(1024)(128)(2,1)S(1)} %convert_element_type.18, bf16[512,4096]{1,0:T(8,128)(2,1)} %collective-permute-done.7, bf16[239,4096]{1,0:T(8,128)(2,1)S(1)} %broadcast_select_fusion), kind=kLoop, calls=%fused_computation | loop fusion | flops 24608016 | bytes 6163388 | tf_op jit(solution)/shard_map/reduce_sum | solution.py:35
  154.2 6.7 %multiply_subtract_fusion.1 = f32[751,512]{0,1:T(8,128)S(1)} fusion(f32[751]{0:T(1024)S(1)} %multiply_reduce_fusion, f32[512]{0:T(512)S(1)} %multiply_reduce_fusion.2, bf16[512,4096]{1,0:T(8,128)(2,1)} %collective-permute-done.7, bf16[239,4096]{1,0:T(8,128)(2,1)S(1)} %broadcast_select_fusion, bf16[4096]{0:T(1024)(128)(2,1)S(1)} %convert_element_type.18, ...), kind=kOutput, calls=%fused_computation.24 | convolution fusion | flops 3182115328 | bytes 11897788 | tf_op jit(solution)/shard_map/dot_general | solution.py:47
  160.9 0.6 slice_add_fusion.8
  161.5 0.6 copy-done.1
  162.1 0.6 slice_add_fusion.7
  162.6 0.6 slice_add_fusion.6
  165.7 4.3 %add_subtract_fusion = f32[751,239]{0,1:T(8,128)S(1)} fusion(f32[751]{0:T(1024)S(1)} %multiply_reduce_fusion, bf16[239,4096]{1,0:T(8,128)(2,1)S(1)} %collective-permute-done.3, bf16[4096]{0:T(1024)(128)(2,1)S(1)} %convert_element_type.18, f32[239]{0:T(256)S(1)} %multiply_reduce_fusion.3, bf16[512,4096]{1,0:T(8,128)(2,1)} %collective-permute-done.7, ...), kind=kOutput, calls=%fused_computation.69 | convolution fusion | flops 1490347776 | bytes 8840188 | tf_op jit(solution)/shard_map/dot_general | solution.py:47
  172.4 0.6 slice_add_fusion.26
  174.4 0.7 fusion.20
  175.2 12.9 %collective-permute-start.9 = (f32[512,256]{0,1:T(8,128)S(1)}, f32[512,256]{0,1:T(8,128)S(1)}, u32[]{:S(2)}, u32[]{:S(2)}) collective-permute-start(f32[512,256]{0,1:T(8,128)S(1)} %get-tuple-element.23), channel_id=1, source_target_pairs={{0,3},{1,2},{2,5},{3,4},{4,7},{5,6},{6,9},{7,8},{8,11},{9,10},{10,... | collective-permute-start | bytes 1572872 | tf_op jit(solution)/shard_map/ppermute | solution.py:149
  188.1 12.7 %collective-permute-done.2 = f32[512,256]{0,1:T(8,128)S(1)} collective-permute-done((f32[512,256]{0,1:T(8,128)S(1)}, f32[512,256]{0,1:T(8,128)S(1)}, u32[]{:S(2)}, u32[]{:S(2)}) %collective-permute-start.2) | collective-permute-done | bytes 524320 | tf_op jit(solution)/shard_map/ppermute | solution.py:132
  200.8 20.6 %collective-permute-done.5 = f32[512,256]{0,1:T(8,128)S(1)} collective-permute-done((f32[512,256]{0,1:T(8,128)S(1)}, f32[512,256]{0,1:T(8,128)S(1)}, u32[]{:S(2)}, u32[]{:S(2)}) %collective-permute-start.5) | collective-permute-done | bytes 524320 | tf_op jit(solution)/shard_map/ppermute | solution.py:132
  222.1 4.2 %collective-permute-start.10 = (f32[512]{0:T(512)S(1)}, f32[512]{0:T(512)S(1)}, u32[]{:S(2)}, u32[]{:S(2)}) collective-permute-start(f32[512]{0:T(512)S(1)} %add.315), channel_id=1, source_target_pairs={{0,1},{1,0},{2,3},{3,2},{4,5},{5,4},{6,7},{7,6},{8,9},{9,8},{10,11... | collective-permute-start | bytes 6152 | tf_op jit(solution)/shard_map/ppermute | solution.py:158
  226.4 1.0 collective-permute-start.11
  227.3 11.2 %collective-permute-start.12 = (f32[256]{0:T(256)S(1)}, f32[256]{0:T(256)S(1)}, u32[]{:S(2)}, u32[]{:S(2)}) collective-permute-start(f32[256]{0:T(256)S(1)} %get-tuple-element.27), channel_id=1, source_target_pairs={{0,3},{1,2},{2,5},{3,4},{4,7},{5,6},{6,9},{7,8},{8,11},{9,10},{10,... | collective-permute-start | bytes 3080 | tf_op jit(solution)/shard_map/ppermute | solution.py:162
  238.6 10.3 %collective-permute-start.13 = (f32[256]{0:T(256)S(1)}, f32[256]{0:T(256)S(1)}, u32[]{:S(2)}, u32[]{:S(2)}) collective-permute-start(f32[256]{0:T(256)S(1)} %get-tuple-element.28), channel_id=1, source_target_pairs={{0,4},{1,5},{2,6},{3,7},{4,8},{5,9},{6,10},{7,11},{8,12},{9,13},{1... | collective-permute-start | bytes 3080 | tf_op jit(solution)/shard_map/ppermute | solution.py:161
  248.9 1.3 collective-permute-done.13
  250.2 5.9 %collective-permute-done.14 = f32[256]{0:T(256)S(1)} collective-permute-done((f32[256]{0:T(256)S(1)}, f32[256]{0:T(256)S(1)}, u32[]{:S(2)}, u32[]{:S(2)}) %collective-permute-start.14) | collective-permute-done | bytes 1056 | tf_op jit(solution)/shard_map/ppermute | solution.py:162
  256.4 1.6 copy.9
  (79 shorter events, 15.7 us)
Async XLA Ops:
  3.3 11.3 %copy-start.3 = (s32[4096]{0:T(1024)S(1)}, s32[4096]{0:T(1024)}, u32[]{:S(2)}) copy-start(s32[4096]{0:T(1024)} %param.4) | copy-start | bytes 49156
  3.3 48.0 %collective-permute-start.1 = (bf16[239,4096]{1,0:T(8,128)(2,1)}, bf16[239,4096]{1,0:T(8,128)(2,1)S(1)}, u32[]{:S(2)}, u32[]{:S(2)}) collective-permute-start(bf16[239,4096]{1,0:T(8,128)(2,1)} %slice.312), channel_id=1, source_target_pairs={{0,2},{2,4},{4,6},{6,8},{8,10},{10,12},{12,14},{14,0},{1,3},{3,5},... | collective-permute-start | bytes 5873672 | tf_op jit(solution)/shard_map/ppermute | solution.py:103
  4.9 46.4 %collective-permute-start = (bf16[239,4096]{1,0:T(8,128)(2,1)}, bf16[239,4096]{1,0:T(8,128)(2,1)}, u32[]{:S(2)}, u32[]{:S(2)}) collective-permute-start(bf16[239,4096]{1,0:T(8,128)(2,1)} %slice.312), channel_id=1, source_target_pairs={{14,16},{30,32},{46,48},{62,64},{78,80},{94,96},{110,112},{15,17},... | collective-permute-start | bytes 5873672 | tf_op jit(solution)/shard_map/ppermute | solution.py:104
  6.9 142.7 %collective-permute-start.7 = (bf16[512,4096]{1,0:T(8,128)(2,1)}, bf16[512,4096]{1,0:T(8,128)(2,1)}, u32[]{:S(2)}, u32[]{:S(2)}) collective-permute-start(bf16[512,4096]{1,0:T(8,128)(2,1)} %param.3), channel_id=1, source_target_pairs={{0,14},{2,0},{4,2},{6,4},{8,6},{10,8},{12,10},{14,12},{1,15},{3,1}... | collective-permute-start | bytes 12582920 | tf_op jit(solution)/shard_map/ppermute | solution.py:106
  9.4 58.0 %collective-permute-start.6 = (bf16[239,4096]{1,0:T(8,128)(2,1)}, bf16[239,4096]{1,0:T(8,128)(2,1)}, u32[]{:S(2)}, u32[]{:S(2)}) collective-permute-start(bf16[239,4096]{1,0:T(8,128)(2,1)} %slice.312), channel_id=1, source_target_pairs={{14,30},{30,46},{46,62},{62,78},{78,94},{94,110},{110,126},{15,31}... | collective-permute-start | bytes 5873672 | tf_op jit(solution)/shard_map/ppermute | solution.py:107
  14.7 86.0 %collective-permute-start.4 = (bf16[273,4096]{1,0:T(8,128)(2,1)}, bf16[273,4096]{1,0:T(8,128)(2,1)}, u32[]{:S(2)}, u32[]{:S(2)}) collective-permute-start(bf16[273,4096]{1,0:T(8,128)(2,1)} %slice.333), channel_id=1, source_target_pairs={{0,2},{2,4},{4,6},{6,8},{8,10},{10,12},{12,14},{14,0},{1,3},{3,5},... | collective-permute-start | bytes 6709256 | tf_op jit(solution)/shard_map/ppermute | solution.py:105
  15.4 36.2 %copy-start = (bf16[512,4096]{1,0:T(8,128)(2,1)S(1)}, bf16[512,4096]{1,0:T(8,128)(2,1)}, u32[]{:S(2)}) copy-start(bf16[512,4096]{1,0:T(8,128)(2,1)} %param.3) | copy-start | bytes 12582916
  66.7 75.0 %collective-permute-start.3 = (bf16[239,4096]{1,0:T(8,128)(2,1)S(1)}, bf16[239,4096]{1,0:T(8,128)(2,1)S(1)}, u32[]{:S(2)}, u32[]{:S(2)}) collective-permute-start(bf16[239,4096]{1,0:T(8,128)(2,1)S(1)} %broadcast_select_fusion.1), channel_id=1, source_target_pairs={{0,2},{2,4},{4,6},{6,8},{8,10},{10,12},{12,14},{14,0},{1,3},{3,5},... | collective-permute-start | bytes 5873672 | tf_op jit(solution)/shard_map/ppermute | solution.py:112
  66.8 133.9 %collective-permute-start.2 = (f32[512,256]{0,1:T(8,128)S(1)}, f32[512,256]{0,1:T(8,128)S(1)}, u32[]{:S(2)}, u32[]{:S(2)}) collective-permute-start(f32[512,256]{0,1:T(8,128)S(1)} %constant_dynamic-slice_fusion), channel_id=1, source_target_pairs={{0,1},{1,0},{2,3},{3,2},{4,5},{5,4},{6,7},{7,6},{8,9},{9,8},{10,11... | collective-permute-start | bytes 1572872 | tf_op jit(solution)/shard_map/ppermute | solution.py:132
  109.7 1.1 copy-start.2
  142.2 2.2 slice-start.1
  148.9 72.5 %collective-permute-start.5 = (f32[512,256]{0,1:T(8,128)S(1)}, f32[512,256]{0,1:T(8,128)S(1)}, u32[]{:S(2)}, u32[]{:S(2)}) collective-permute-start(f32[512,256]{0,1:T(8,128)S(1)} %fusion.22), channel_id=1, source_target_pairs={{0,1},{1,0},{2,3},{3,2},{4,5},{5,4},{6,7},{7,6},{8,9},{9,8},{10,11... | collective-permute-start | bytes 1572872 | tf_op jit(solution)/shard_map/ppermute | solution.py:132
  160.9 1.1 copy-start.1
  165.7 4.4 %slice-start = ((f32[751,512]{0,1:T(8,128)}), f32[751,239]{0,1:T(8,128)S(1)}, s32[]{:S(2)}) async-start(f32[751,512]{0,1:T(8,128)} %copy-done.1), calls=%async_computation | async-start | bytes 1474560 | tf_op jit(solution)/shard_map/slice | solution.py:83
  175.1 46.8 %collective-permute-start.8 = (f32[512,256]{0,1:T(8,128)S(1)}, f32[512,256]{0,1:T(8,128)S(1)}, u32[]{:S(2)}, u32[]{:S(2)}) collective-permute-start(f32[512,256]{0,1:T(8,128)S(1)} %get-tuple-element.24), channel_id=1, source_target_pairs={{0,2},{1,3},{2,4},{3,5},{4,6},{5,7},{6,8},{7,9},{8,10},{9,11},{10,... | collective-permute-start | bytes 1572872 | tf_op jit(solution)/shard_map/ppermute | solution.py:148
  175.2 46.8 %collective-permute-start.9 = (f32[512,256]{0,1:T(8,128)S(1)}, f32[512,256]{0,1:T(8,128)S(1)}, u32[]{:S(2)}, u32[]{:S(2)}) collective-permute-start(f32[512,256]{0,1:T(8,128)S(1)} %get-tuple-element.23), channel_id=1, source_target_pairs={{0,3},{1,2},{2,5},{3,4},{4,7},{5,6},{6,9},{7,8},{8,11},{9,10},{10,... | collective-permute-start | bytes 1572872 | tf_op jit(solution)/shard_map/ppermute | solution.py:149
  222.1 34.0 %collective-permute-start.10 = (f32[512]{0:T(512)S(1)}, f32[512]{0:T(512)S(1)}, u32[]{:S(2)}, u32[]{:S(2)}) collective-permute-start(f32[512]{0:T(512)S(1)} %add.315), channel_id=1, source_target_pairs={{0,1},{1,0},{2,3},{3,2},{4,5},{5,4},{6,7},{7,6},{8,9},{9,8},{10,11... | collective-permute-start | bytes 6152 | tf_op jit(solution)/shard_map/ppermute | solution.py:158
  226.4 22.5 %collective-permute-start.11 = (f32[256]{0:T(256)S(1)}, f32[256]{0:T(256)S(1)}, u32[]{:S(2)}, u32[]{:S(2)}) collective-permute-start(f32[256]{0:T(256)S(1)} %get-tuple-element.28), channel_id=1, source_target_pairs={{0,2},{1,3},{2,4},{3,5},{4,6},{5,7},{6,8},{7,9},{8,10},{9,11},{10,... | collective-permute-start | bytes 3080 | tf_op jit(solution)/shard_map/ppermute | solution.py:161
  227.3 21.5 %collective-permute-start.12 = (f32[256]{0:T(256)S(1)}, f32[256]{0:T(256)S(1)}, u32[]{:S(2)}, u32[]{:S(2)}) collective-permute-start(f32[256]{0:T(256)S(1)} %get-tuple-element.27), channel_id=1, source_target_pairs={{0,3},{1,2},{2,5},{3,4},{4,7},{5,6},{6,9},{7,8},{8,11},{9,10},{10,... | collective-permute-start | bytes 3080 | tf_op jit(solution)/shard_map/ppermute | solution.py:162
  238.6 11.6 %collective-permute-start.13 = (f32[256]{0:T(256)S(1)}, f32[256]{0:T(256)S(1)}, u32[]{:S(2)}, u32[]{:S(2)}) collective-permute-start(f32[256]{0:T(256)S(1)} %get-tuple-element.28), channel_id=1, source_target_pairs={{0,4},{1,5},{2,6},{3,7},{4,8},{5,9},{6,10},{7,11},{8,12},{9,13},{1... | collective-permute-start | bytes 3080 | tf_op jit(solution)/shard_map/ppermute | solution.py:161
  248.8 7.2 %collective-permute-start.14 = (f32[256]{0:T(256)S(1)}, f32[256]{0:T(256)S(1)}, u32[]{:S(2)}, u32[]{:S(2)}) collective-permute-start(f32[256]{0:T(256)S(1)} %get-tuple-element.27), channel_id=1, source_target_pairs={{0,5},{1,4},{2,7},{3,6},{4,9},{5,8},{6,11},{7,10},{8,13},{9,12},{1... | collective-permute-start | bytes 3080 | tf_op jit(solution)/shard_map/ppermute | solution.py:162

commit v9 on v8

--- a/solution.py
+++ b/solution.py
@@ -103,7 +103,11 @@
     tail_prev = lax.ppermute(tail, "col", up)
     tail_to_first = lax.ppermute(tail, flat, to_slot0)
     head_prev = lax.ppermute(head, "col", up)
-    block_next = lax.ppermute(snapshots, "col", down)
+    half_rows = block_rows // 2
+    block_next = jnp.concatenate([
+        lax.ppermute(snapshots[:half_rows], "col", down),
+        lax.ppermute(snapshots[half_rows:], "col", down),
+    ], axis=0)
     tail_to_last = lax.ppermute(tail, flat, to_slot7)
     own_hist = jnp.where(slot == 0, tail_to_first, tail_prev)
     own_rows = jnp.concatenate([own_hist, snapshots], axis=0) * mask

time: 262 us -> 251 us (0.958)
  the two profiles are of different devices: /device:TPU:98 before, /device:TPU:100 now
where the time goes in v9:
time: 251 us; the launch traced here: 247 us
  waiting for transfers between devices  104 us (41%)
  starting transfers between devices  65.2 us (26%)
  other arithmetic  34.5 us (14%)
  matrix products  24 us (10%)
  local copies, waits for them, and re-layouts  18.7 us (7%)
    ppermute x1, waiting for transfers between devices, per_device(): lax.ppermute(snapshots[half_rows:], 'col', down)  37.7 us
    ppermute x1, waiting for transfers between devices, per_device(): tail_prev = lax.ppermute(tail, 'col', up)  31.9 us
    ppermute x2, waiting for transfers between devices, space_sum(): return mine + lax.ppermute(theirs, 'space', swap)  22.4 us
    ppermute x1, starting transfers between devices, per_device(): lax.ppermute(lax.dynamic_slice_in_dim(band2_next, start_col, column_width...  19.7 us
    dot_general x4, matrix products, gram(): lax.dot_general(rows, cols, (((1,), (1,)), ((), ())), preferred_element_t...  18.5 us
    ppermute x2, starting transfers between devices, per_device(): lax.ppermute(lax.dynamic_slice_in_dim(part_degree, start_col, column_widt...  16.2 us
    ppermute x2, starting transfers between devices, per_device(): lax.ppermute(lax.dynamic_slice_in_dim(part_degree, other_col, column_widt...  12.6 us
    add x24, other arithmetic, lag_sum_rect(): doubled = doubled[width:width + r, width:width + c] + doubled[:r, :c]  12 us
  transfers between devices with their start and end apart: 16, of which 7 were waited for; matrix products, arithmetic and copies ran while one was open for 29% of the time, Pallas kernels for 0%

profile of v9, /device:TPU:100, one launch (start us, length us, event | category | flops | bytes accessed | tf_op | source)
XLA Modules:
  0.0 247.3 jit_solution(3807963667588626514)
XLA Ops:
  0.0 3.3 %slice.318 = bf16[239,4096]{1,0:T(8,128)(2,1)} slice(bf16[512,4096]{1,0:T(8,128)(2,1)} %param.3), slice={[273:512], [0:4096]} | slice | bytes 3915776 | tf_op jit(solution)/shard_map/slice | solution.py:95
  3.3 1.6 collective-permute-start.1
  4.9 1.9 collective-permute-start
  6.8 2.0 collective-permute-start.6
  8.8 3.3 %slice.339 = bf16[273,4096]{1,0:T(8,128)(2,1)} slice(bf16[512,4096]{1,0:T(8,128)(2,1)} %param.3), slice={[0:273], [0:4096]} | slice | bytes 4472832 | tf_op jit(solution)/shard_map/slice | solution.py:96
  12.0 1.6 collective-permute-start.4
  13.6 2.5 %fusion.39 = (bf16[256,4096]{1,0:T(8,128)(2,1)}, bf16[256,4096]{1,0:T(8,128)(2,1)}) fusion(bf16[512,4096]{1,0:T(8,128)(2,1)S(1)} %copy-done), kind=kLoop, calls=%fused_computation.104 | loop fusion | bytes 8388608 | tf_op jit(solution)/shard_map/slice | solution.py:108
  16.2 2.6 %collective-permute-start.7 = (bf16[256,4096]{1,0:T(8,128)(2,1)}, bf16[256,4096]{1,0:T(8,128)(2,1)}, u32[]{:S(2)}, u32[]{:S(2)}) collective-permute-start(bf16[256,4096]{1,0:T(8,128)(2,1)} %get-tuple-element.13), channel_id=1, source_target_pairs={{0,14},{2,0},{4,2},{6,4},{8,6},{10,8},{12,10},{14,12},{1,15},{3,1}... | collective-permute-start | bytes 6291464 | tf_op jit(solution)/shard_map/ppermute | solution.py:108
  19.4 31.9 %collective-permute-done.1 = bf16[239,4096]{1,0:T(8,128)(2,1)S(1)} collective-permute-done((bf16[239,4096]{1,0:T(8,128)(2,1)}, bf16[239,4096]{1,0:T(8,128)(2,1)S(1)}, u32[]{:S(2)}, u32[]{:S(2)}) %collective-permute-start.1) | collective-permute-done | bytes 1957920 | tf_op jit(solution)/shard_map/ppermute | solution.py:103
  51.3 0.7 collective-permute-start.8
  52.3 1.2 copy-done.1
  53.5 3.1 %multiply_reduce_fusion.1 = f32[751]{0:T(1024)S(1)} fusion(bf16[4096]{0:T(1024)(128)(2,1)S(1)} %convert_element_type.18, bf16[512,4096]{1,0:T(8,128)(2,1)S(1)} %copy-done.1, bf16[239,4096]{1,0:T(8,128)(2,1)S(1)} %broadcast_select_fusion.1), kind=kLoop, calls=%fused_computation.1 | loop fusion | flops 24608016 | bytes 6163388 | tf_op jit(solution)/shard_map/reduce_sum | solution.py:35
  56.6 5.5 %multiply_subtract_fusion = f32[751,751]{0,1:T(8,128)S(1)} fusion(f32[751]{0:T(1024)S(1)} %multiply_reduce_fusion.1, bf16[512,4096]{1,0:T(8,128)(2,1)S(1)} %copy-done.1, bf16[239,4096]{1,0:T(8,128)(2,1)S(1)} %broadcast_select_fusion.1, bf16[4096]{0:T(1024)(128)(2,1)S(1)} %convert_element_type.18), kind=kOutput, calls=%fused_computation.10 | convolution fusion | flops 4640445440 | bytes 8419392 | tf_op jit(solution)/shard_map/dot_general | solution.py:39
  62.1 0.9 slice_add_fusion.1
  63.0 0.8 slice_add_fusion
  63.8 0.8 slice_add_fusion.2
  64.7 0.7 slice_add_fusion.3
  65.8 0.6 slice_add_fusion.4
  66.9 0.6 slice_add_fusion.5
  68.7 0.9 constant_dynamic-slice_fusion
  70.6 37.7 %collective-permute-done.8 = bf16[256,4096]{1,0:T(8,128)(2,1)} collective-permute-done((bf16[256,4096]{1,0:T(8,128)(2,1)}, bf16[256,4096]{1,0:T(8,128)(2,1)}, u32[]{:S(2)}, u32[]{:S(2)}) %collective-permute-start.8) | collective-permute-done | bytes 2097184 | tf_op jit(solution)/shard_map/ppermute | solution.py:109
  108.3 2.5 %pad_maximum_fusion = bf16[512,4096]{1,0:T(8,128)(2,1)S(1)} fusion(bf16[256,4096]{1,0:T(8,128)(2,1)} %collective-permute-done.8, bf16[256,4096]{1,0:T(8,128)(2,1)} %collective-permute-done.7), kind=kLoop, calls=%fused_computation.6 | loop fusion | flops 8388608 | bytes 8388608 | tf_op jit(solution)/shard_map/concatenate | solution.py:107
  110.8 2.9 %multiply_reduce_fusion = f32[751]{0:T(1024)S(1)} fusion(bf16[4096]{0:T(1024)(128)(2,1)S(1)} %convert_element_type.18, bf16[512,4096]{1,0:T(8,128)(2,1)S(1)} %pad_maximum_fusion, bf16[239,4096]{1,0:T(8,128)(2,1)S(1)} %broadcast_select_fusion), kind=kLoop, calls=%fused_computation | loop fusion | flops 24608016 | bytes 6163388 | tf_op jit(solution)/shard_map/reduce_sum | solution.py:35
  113.7 3.5 %multiply_reduce_fusion.2 = f32[512]{0:T(512)S(1)} fusion(bf16[4096]{0:T(1024)(128)(2,1)S(1)} %convert_element_type.18, bf16[239,4096]{1,0:T(8,128)(2,1)S(1)} %collective-permute-done.1, bf16[273,4096]{1,0:T(8,128)(2,1)} %collective-permute-done.4), kind=kLoop, calls=%fused_computation.2 | loop fusion | flops 16776704 | bytes 4204544 | tf_op jit(solution)/shard_map/reduce_sum | solution.py:35
  117.3 5.5 %multiply_subtract_fusion.2 = f32[751,512]{0,1:T(8,128)S(1)} fusion(f32[512]{0:T(512)S(1)} %multiply_reduce_fusion.2, f32[751]{0:T(1024)S(1)} %multiply_reduce_fusion.1, bf16[239,4096]{1,0:T(8,128)(2,1)S(1)} %collective-permute-done.1, bf16[273,4096]{1,0:T(8,128)(2,1)} %collective-permute-done.4, bf16[4096]{0:T(1024)(128)(2,1)S(1)} %convert_element_type.18, ...), kind=kOutput, calls=%fused_computation.26 | convolution fusion | flops 3182115328 | bytes 11897788 | tf_op jit(solution)/shard_map/dot_general | solution.py:47
  122.8 0.6 slice_add_fusion.11
  125.4 5.5 %multiply_subtract_fusion.1 = f32[751,512]{0,1:T(8,128)S(1)} fusion(f32[751]{0:T(1024)S(1)} %multiply_reduce_fusion, f32[512]{0:T(512)S(1)} %multiply_reduce_fusion.2, bf16[512,4096]{1,0:T(8,128)(2,1)S(1)} %pad_maximum_fusion, bf16[239,4096]{1,0:T(8,128)(2,1)S(1)} %broadcast_select_fusion, bf16[4096]{0:T(1024)(128)(2,1)S(1)} %convert_element_type.18, ...), kind=kOutput, calls=%fused_computation.25 | convolution fusion | flops 3182115328 | bytes 11897788 | tf_op jit(solution)/shard_map/dot_general | solution.py:47
  131.0 0.6 slice_add_fusion.8
  132.1 0.6 slice_add_fusion.6
  133.1 0.6 slice_add_fusion.23
  137.2 4.4 %collective-permute-done.3 = bf16[239,4096]{1,0:T(8,128)(2,1)} collective-permute-done((bf16[239,4096]{1,0:T(8,128)(2,1)S(1)}, bf16[239,4096]{1,0:T(8,128)(2,1)}, u32[]{:S(2)}, u32[]{:S(2)}) %collective-permute-start.3) | collective-permute-done | bytes 1957920 | tf_op jit(solution)/shard_map/ppermute | solution.py:116
  141.7 2.1 multiply_reduce_fusion.3
  143.8 3.7 %add_subtract_fusion.1 = f32[751,239]{0,1:T(8,128)S(1)} fusion(bf16[239,4096]{1,0:T(8,128)(2,1)} %collective-permute-done.3, bf16[4096]{0:T(1024)(128)(2,1)S(1)} %convert_element_type.18, f32[239]{0:T(256)S(1)} %multiply_reduce_fusion.3, f32[751]{0:T(1024)S(1)} %multiply_reduce_fusion.1, bf16[512,4096]{1,0:T(8,128)(2,1)S(1)} %copy-done.1, ...), kind=kOutput, calls=%fused_computation.71 | convolution fusion | flops 1490347776 | bytes 8840188 | tf_op jit(solution)/shard_map/dot_general | solution.py:47
  151.4 3.7 %add_subtract_fusion = f32[751,239]{0,1:T(8,128)S(1)} fusion(f32[751]{0:T(1024)S(1)} %multiply_reduce_fusion, bf16[239,4096]{1,0:T(8,128)(2,1)} %collective-permute-done.3, bf16[4096]{0:T(1024)(128)(2,1)S(1)} %convert_element_type.18, f32[239]{0:T(256)S(1)} %multiply_reduce_fusion.3, bf16[512,4096]{1,0:T(8,128)(2,1)S(1)} %pad_maximum_fusion, ...), kind=kOutput, calls=%fused_computation.70 | convolution fusion | flops 1490347776 | bytes 8840188 | tf_op jit(solution)/shard_map/dot_general | solution.py:47
  155.6 0.7 slice_add_fusion.16
  159.6 0.6 collective-permute-start.5
  160.4 0.7 fusion.20
  161.1 1.9 collective-permute-start.10
  163.0 19.7 %collective-permute-start.9 = (f32[512,256]{0,1:T(8,128)S(1)}, f32[512,256]{0,1:T(8,128)S(1)}, u32[]{:S(2)}, u32[]{:S(2)}) collective-permute-start(f32[512,256]{0,1:T(8,128)S(1)} %get-tuple-element.26), channel_id=1, source_target_pairs={{0,2},{1,3},{2,4},{3,5},{4,6},{5,7},{6,8},{7,9},{8,10},{9,11},{10,... | collective-permute-start | bytes 1572872 | tf_op jit(solution)/shard_map/ppermute | solution.py:152
  182.7 11.4 %collective-permute-done.2 = f32[512,256]{0,1:T(8,128)S(1)} collective-permute-done((f32[512,256]{0,1:T(8,128)}, f32[512,256]{0,1:T(8,128)S(1)}, u32[]{:S(2)}, u32[]{:S(2)}) %collective-permute-start.2) | collective-permute-done | bytes 524320 | tf_op jit(solution)/shard_map/ppermute | solution.py:136
  194.1 11.1 %collective-permute-done.5 = f32[512,256]{0,1:T(8,128)S(1)} collective-permute-done((f32[512,256]{0,1:T(8,128)S(1)}, f32[512,256]{0,1:T(8,128)S(1)}, u32[]{:S(2)}, u32[]{:S(2)}) %collective-permute-start.5) | collective-permute-done | bytes 524320 | tf_op jit(solution)/shard_map/ppermute | solution.py:136
  205.9 3.1 %collective-permute-start.11 = (f32[512]{0:T(512)S(1)}, f32[512]{0:T(512)S(1)}, u32[]{:S(2)}, u32[]{:S(2)}) collective-permute-start(f32[512]{0:T(512)S(1)} %add.315), channel_id=1, source_target_pairs={{0,1},{1,0},{2,3},{3,2},{4,5},{5,4},{6,7},{7,6},{8,9},{9,8},{10,11... | collective-permute-start | bytes 6152 | tf_op jit(solution)/shard_map/ppermute | solution.py:162
  209.0 4.2 %collective-permute-start.12 = (f32[256]{0:T(256)S(1)}, f32[256]{0:T(256)S(1)}, u32[]{:S(2)}, u32[]{:S(2)}) collective-permute-start(f32[256]{0:T(256)S(1)} %get-tuple-element.30), channel_id=1, source_target_pairs={{0,2},{1,3},{2,4},{3,5},{4,6},{5,7},{6,8},{7,9},{8,10},{9,11},{10,... | collective-permute-start | bytes 3080 | tf_op jit(solution)/shard_map/ppermute | solution.py:165
  213.2 12.6 %collective-permute-start.13 = (f32[256]{0:T(256)S(1)}, f32[256]{0:T(256)S(1)}, u32[]{:S(2)}, u32[]{:S(2)}) collective-permute-start(f32[256]{0:T(256)S(1)} %get-tuple-element.29), channel_id=1, source_target_pairs={{0,3},{1,2},{2,5},{3,4},{4,7},{5,6},{6,9},{7,8},{8,11},{9,10},{10,... | collective-permute-start | bytes 3080 | tf_op jit(solution)/shard_map/ppermute | solution.py:166
  225.9 12.0 %collective-permute-start.14 = (f32[256]{0:T(256)S(1)}, f32[256]{0:T(256)S(1)}, u32[]{:S(2)}, u32[]{:S(2)}) collective-permute-start(f32[256]{0:T(256)S(1)} %get-tuple-element.30), channel_id=1, source_target_pairs={{0,4},{1,5},{2,6},{3,7},{4,8},{5,9},{6,10},{7,11},{8,12},{9,13},{1... | collective-permute-start | bytes 3080 | tf_op jit(solution)/shard_map/ppermute | solution.py:165
  237.9 1.3 collective-permute-done.14
  239.2 5.9 %collective-permute-done.15 = f32[256]{0:T(256)S(1)} collective-permute-done((f32[256]{0:T(256)S(1)}, f32[256]{0:T(256)S(1)}, u32[]{:S(2)}, u32[]{:S(2)}) %collective-permute-start.15) | collective-permute-done | bytes 1056 | tf_op jit(solution)/shard_map/ppermute | solution.py:166
  245.5 1.6 copy.9
  (85 shorter events, 18.8 us)
Async XLA Ops:
  3.3 10.3 %copy-start = (bf16[512,4096]{1,0:T(8,128)(2,1)S(1)}, bf16[512,4096]{1,0:T(8,128)(2,1)}, u32[]{:S(2)}) copy-start(bf16[512,4096]{1,0:T(8,128)(2,1)} %param.3) | copy-start | bytes 12582916
  3.3 48.0 %collective-permute-start.1 = (bf16[239,4096]{1,0:T(8,128)(2,1)}, bf16[239,4096]{1,0:T(8,128)(2,1)S(1)}, u32[]{:S(2)}, u32[]{:S(2)}) collective-permute-start(bf16[239,4096]{1,0:T(8,128)(2,1)} %slice.318), channel_id=1, source_target_pairs={{0,2},{2,4},{4,6},{6,8},{8,10},{10,12},{12,14},{14,0},{1,3},{3,5},... | collective-permute-start | bytes 5873672 | tf_op jit(solution)/shard_map/ppermute | solution.py:103
  4.9 47.2 %collective-permute-start = (bf16[239,4096]{1,0:T(8,128)(2,1)}, bf16[239,4096]{1,0:T(8,128)(2,1)}, u32[]{:S(2)}, u32[]{:S(2)}) collective-permute-start(bf16[239,4096]{1,0:T(8,128)(2,1)} %slice.318), channel_id=1, source_target_pairs={{14,16},{30,32},{46,48},{62,64},{78,80},{94,96},{110,112},{15,17},... | collective-permute-start | bytes 5873672 | tf_op jit(solution)/shard_map/ppermute | solution.py:104
  6.8 62.8 %collective-permute-start.6 = (bf16[239,4096]{1,0:T(8,128)(2,1)}, bf16[239,4096]{1,0:T(8,128)(2,1)}, u32[]{:S(2)}, u32[]{:S(2)}) collective-permute-start(bf16[239,4096]{1,0:T(8,128)(2,1)} %slice.318), channel_id=1, source_target_pairs={{14,30},{30,46},{46,62},{62,78},{78,94},{94,110},{110,126},{15,31}... | collective-permute-start | bytes 5873672 | tf_op jit(solution)/shard_map/ppermute | solution.py:111
  12.0 6.7 %copy-start.4 = (s32[4096]{0:T(1024)S(1)}, s32[4096]{0:T(1024)}, u32[]{:S(2)}) copy-start(s32[4096]{0:T(1024)} %param.4) | copy-start | bytes 49156
  12.0 101.7 %collective-permute-start.4 = (bf16[273,4096]{1,0:T(8,128)(2,1)}, bf16[273,4096]{1,0:T(8,128)(2,1)}, u32[]{:S(2)}, u32[]{:S(2)}) collective-permute-start(bf16[273,4096]{1,0:T(8,128)(2,1)} %slice.339), channel_id=1, source_target_pairs={{0,2},{2,4},{4,6},{6,8},{8,10},{10,12},{12,14},{14,0},{1,3},{3,5},... | collective-permute-start | bytes 6709256 | tf_op jit(solution)/shard_map/ppermute | solution.py:105
  16.2 54.5 %collective-permute-start.7 = (bf16[256,4096]{1,0:T(8,128)(2,1)}, bf16[256,4096]{1,0:T(8,128)(2,1)}, u32[]{:S(2)}, u32[]{:S(2)}) collective-permute-start(bf16[256,4096]{1,0:T(8,128)(2,1)} %get-tuple-element.13), channel_id=1, source_target_pairs={{0,14},{2,0},{4,2},{6,4},{8,6},{10,8},{12,10},{14,12},{1,15},{3,1}... | collective-permute-start | bytes 6291464 | tf_op jit(solution)/shard_map/ppermute | solution.py:108
  51.3 2.2 copy-start.1
  51.3 57.0 %collective-permute-start.8 = (bf16[256,4096]{1,0:T(8,128)(2,1)}, bf16[256,4096]{1,0:T(8,128)(2,1)}, u32[]{:S(2)}, u32[]{:S(2)}) collective-permute-start(bf16[256,4096]{1,0:T(8,128)(2,1)} %get-tuple-element.14), channel_id=1, source_target_pairs={{0,14},{2,0},{4,2},{6,4},{8,6},{10,8},{12,10},{14,12},{1,15},{3,1}... | collective-permute-start | bytes 6291464 | tf_op jit(solution)/shard_map/ppermute | solution.py:109
  68.5 73.1 %collective-permute-start.3 = (bf16[239,4096]{1,0:T(8,128)(2,1)S(1)}, bf16[239,4096]{1,0:T(8,128)(2,1)}, u32[]{:S(2)}, u32[]{:S(2)}) collective-permute-start(bf16[239,4096]{1,0:T(8,128)(2,1)S(1)} %broadcast_select_fusion.1), channel_id=1, source_target_pairs={{0,2},{2,4},{4,6},{6,8},{8,10},{10,12},{12,14},{14,0},{1,3},{3,5},... | collective-permute-start | bytes 5873672 | tf_op jit(solution)/shard_map/ppermute | solution.py:116
  69.5 124.5 %collective-permute-start.2 = (f32[512,256]{0,1:T(8,128)}, f32[512,256]{0,1:T(8,128)S(1)}, u32[]{:S(2)}, u32[]{:S(2)}) collective-permute-start(f32[512,256]{0,1:T(8,128)} %constant_dynamic-slice_fusion), channel_id=1, source_target_pairs={{0,1},{1,0},{2,3},{3,2},{4,5},{5,4},{6,7},{7,6},{8,9},{9,8},{10,11... | collective-permute-start | bytes 1572872 | tf_op jit(solution)/shard_map/ppermute | solution.py:136
  122.8 11.0 %copy-start.2 = (f32[751,512]{0,1:T(8,128)}, f32[751,512]{0,1:T(8,128)S(1)}, u32[]{:S(2)}) copy-start(f32[751,512]{0,1:T(8,128)S(1)} %multiply_subtract_fusion.2) | copy-start | bytes 4614148
  130.9 3.5 %copy-start.3 = (f32[751,512]{0,1:T(8,128)}, f32[751,512]{0,1:T(8,128)S(1)}, u32[]{:S(2)}) copy-start(f32[751,512]{0,1:T(8,128)S(1)} %multiply_subtract_fusion.1) | copy-start | bytes 4614148
  143.8 3.8 %slice-start = ((f32[751,512]{0,1:T(8,128)}), f32[751,239]{0,1:T(8,128)S(1)}, s32[]{:S(2)}) async-start(f32[751,512]{0,1:T(8,128)} %copy-done.2), calls=%async_computation | async-start | bytes 1474560 | tf_op jit(solution)/shard_map/slice | solution.py:83
  151.4 3.8 %slice-start.1 = ((f32[751,512]{0,1:T(8,128)}), f32[751,239]{0,1:T(8,128)S(1)}, s32[]{:S(2)}) async-start(f32[751,512]{0,1:T(8,128)} %copy-done.3), calls=%async_computation.1 | async-start | bytes 1474560 | tf_op jit(solution)/shard_map/slice | solution.py:83
  159.6 45.6 %collective-permute-start.5 = (f32[512,256]{0,1:T(8,128)S(1)}, f32[512,256]{0,1:T(8,128)S(1)}, u32[]{:S(2)}, u32[]{:S(2)}) collective-permute-start(f32[512,256]{0,1:T(8,128)S(1)} %fusion.22), channel_id=1, source_target_pairs={{0,1},{1,0},{2,3},{3,2},{4,5},{5,4},{6,7},{7,6},{8,9},{9,8},{10,11... | collective-permute-start | bytes 1572872 | tf_op jit(solution)/shard_map/ppermute | solution.py:136
  161.1 44.6 %collective-permute-start.10 = (f32[512,256]{0,1:T(8,128)S(1)}, f32[512,256]{0,1:T(8,128)S(1)}, u32[]{:S(2)}, u32[]{:S(2)}) collective-permute-start(f32[512,256]{0,1:T(8,128)S(1)} %get-tuple-element.25), channel_id=1, source_target_pairs={{0,3},{1,2},{2,5},{3,4},{4,7},{5,6},{6,9},{7,8},{8,11},{9,10},{10,... | collective-permute-start | bytes 1572872 | tf_op jit(solution)/shard_map/ppermute | solution.py:153
  163.0 42.8 %collective-permute-start.9 = (f32[512,256]{0,1:T(8,128)S(1)}, f32[512,256]{0,1:T(8,128)S(1)}, u32[]{:S(2)}, u32[]{:S(2)}) collective-permute-start(f32[512,256]{0,1:T(8,128)S(1)} %get-tuple-element.26), channel_id=1, source_target_pairs={{0,2},{1,3},{2,4},{3,5},{4,6},{5,7},{6,8},{7,9},{8,10},{9,11},{10,... | collective-permute-start | bytes 1572872 | tf_op jit(solution)/shard_map/ppermute | solution.py:152
  205.9 39.2 %collective-permute-start.11 = (f32[512]{0:T(512)S(1)}, f32[512]{0:T(512)S(1)}, u32[]{:S(2)}, u32[]{:S(2)}) collective-permute-start(f32[512]{0:T(512)S(1)} %add.315), channel_id=1, source_target_pairs={{0,1},{1,0},{2,3},{3,2},{4,5},{5,4},{6,7},{7,6},{8,9},{9,8},{10,11... | collective-permute-start | bytes 6152 | tf_op jit(solution)/shard_map/ppermute | solution.py:162
  209.0 28.9 %collective-permute-start.12 = (f32[256]{0:T(256)S(1)}, f32[256]{0:T(256)S(1)}, u32[]{:S(2)}, u32[]{:S(2)}) collective-permute-start(f32[256]{0:T(256)S(1)} %get-tuple-element.30), channel_id=1, source_target_pairs={{0,2},{1,3},{2,4},{3,5},{4,6},{5,7},{6,8},{7,9},{8,10},{9,11},{10,... | collective-permute-start | bytes 3080 | tf_op jit(solution)/shard_map/ppermute | solution.py:165
  213.2 24.7 %collective-permute-start.13 = (f32[256]{0:T(256)S(1)}, f32[256]{0:T(256)S(1)}, u32[]{:S(2)}, u32[]{:S(2)}) collective-permute-start(f32[256]{0:T(256)S(1)} %get-tuple-element.29), channel_id=1, source_target_pairs={{0,3},{1,2},{2,5},{3,4},{4,7},{5,6},{6,9},{7,8},{8,11},{9,10},{10,... | collective-permute-start | bytes 3080 | tf_op jit(solution)/shard_map/ppermute | solution.py:166
  225.9 13.3 %collective-permute-start.14 = (f32[256]{0:T(256)S(1)}, f32[256]{0:T(256)S(1)}, u32[]{:S(2)}, u32[]{:S(2)}) collective-permute-start(f32[256]{0:T(256)S(1)} %get-tuple-element.30), channel_id=1, source_target_pairs={{0,4},{1,5},{2,6},{3,7},{4,8},{5,9},{6,10},{7,11},{8,12},{9,13},{1... | collective-permute-start | bytes 3080 | tf_op jit(solution)/shard_map/ppermute | solution.py:165
  237.9 7.2 %collective-permute-start.15 = (f32[256]{0:T(256)S(1)}, f32[256]{0:T(256)S(1)}, u32[]{:S(2)}, u32[]{:S(2)}) collective-permute-start(f32[256]{0:T(256)S(1)} %get-tuple-element.29), channel_id=1, source_target_pairs={{0,5},{1,4},{2,7},{3,6},{4,9},{5,8},{6,11},{7,10},{8,13},{9,12},{1... | collective-permute-start | bytes 3080 | tf_op jit(solution)/shard_map/ppermute | solution.py:166

commit v10 on v9

--- a/solution.py
+++ b/solution.py
@@ -137,8 +137,10 @@
 
     band0 = space_sum(band0_part)
     prev_late = hist_prev * mask
-    band1 = space_sum(lagged_split(own_rows, prev_late, early1, early_sq))
-    band2_next = lagged_split(next_rows, prev_late, early2, early_sq)
+    band1_part = lagged_split(own_rows, prev_late, early1, early_sq)
+    band1 = space_sum(band1_part)
+    prev_late_b2, _ = lax.optimization_barrier((prev_late, band1_part))
+    band2_next = lagged_split(next_rows, prev_late_b2, early2, early_sq)
 
     cs = ("col", "space")
 

time: 251 us -> 249 us (level)
  the two profiles are of different devices: /device:TPU:100 before, /device:TPU:98 now
where the time goes in v10:
time: 249 us; the launch traced here: 245 us
  waiting for transfers between devices  106 us (43%)
  starting transfers between devices  62.7 us (25%)
  other arithmetic  35.2 us (14%)
  matrix products  20.9 us (8%)
  local copies, waits for them, and re-layouts  18.6 us (7%)
    ppermute x1, waiting for transfers between devices, per_device(): lax.ppermute(snapshots[half_rows:], 'col', down)  37.7 us
    ppermute x1, waiting for transfers between devices, per_device(): tail_prev = lax.ppermute(tail, 'col', up)  31.9 us
    ppermute x2, waiting for transfers between devices, space_sum(): return mine + lax.ppermute(theirs, 'space', swap)  24.9 us
    ppermute x1, starting transfers between devices, per_device(): lax.ppermute(lax.dynamic_slice_in_dim(band2_next, start_col, column_width...  19.7 us
    dot_general x4, matrix products, gram(): lax.dot_general(rows, cols, (((1,), (1,)), ((), ())), preferred_element_t...  15.3 us
    ppermute x2, starting transfers between devices, per_device(): lax.ppermute(lax.dynamic_slice_in_dim(part_degree, start_col, column_widt...  13.8 us
    ppermute x2, starting transfers between devices, per_device(): lax.ppermute(lax.dynamic_slice_in_dim(part_degree, other_col, column_widt...  12.6 us
    reduce_sum x5, other arithmetic, square_norms(): return jnp.sum(jnp.square(values.astype(jnp.float32)), axis=1)  12.3 us
  transfers between devices with their start and end apart: 16, of which 7 were waited for; matrix products, arithmetic and copies ran while one was open for 28% of the time, Pallas kernels for 0%

profile of v10, /device:TPU:98, one launch (start us, length us, event | category | flops | bytes accessed | tf_op | source)
XLA Modules:
  0.0 244.8 jit_solution(7606894634752060237)
XLA Ops:
  0.0 3.3 %slice.318 = bf16[239,4096]{1,0:T(8,128)(2,1)} slice(bf16[512,4096]{1,0:T(8,128)(2,1)} %param.3), slice={[273:512], [0:4096]} | slice | bytes 3915776 | tf_op jit(solution)/shard_map/slice | solution.py:95
  3.3 1.6 collective-permute-start.1
  4.9 2.0 collective-permute-start
  6.8 1.9 collective-permute-start.6
  8.7 3.3 %slice.339 = bf16[273,4096]{1,0:T(8,128)(2,1)} slice(bf16[512,4096]{1,0:T(8,128)(2,1)} %param.3), slice={[0:273], [0:4096]} | slice | bytes 4472832 | tf_op jit(solution)/shard_map/slice | solution.py:96
  12.0 1.6 collective-permute-start.4
  13.6 2.5 %fusion.23 = (bf16[256,4096]{1,0:T(8,128)(2,1)}, bf16[256,4096]{1,0:T(8,128)(2,1)}) fusion(bf16[512,4096]{1,0:T(8,128)(2,1)S(1)} %copy-done), kind=kLoop, calls=%fused_computation.101 | loop fusion | bytes 8388608 | tf_op jit(solution)/shard_map/slice | solution.py:108
  16.1 2.6 %collective-permute-start.7 = (bf16[256,4096]{1,0:T(8,128)(2,1)}, bf16[256,4096]{1,0:T(8,128)(2,1)}, u32[]{:S(2)}, u32[]{:S(2)}) collective-permute-start(bf16[256,4096]{1,0:T(8,128)(2,1)} %get-tuple-element.17), channel_id=1, source_target_pairs={{0,14},{2,0},{4,2},{6,4},{8,6},{10,8},{12,10},{14,12},{1,15},{3,1}... | collective-permute-start | bytes 6291464 | tf_op jit(solution)/shard_map/ppermute | solution.py:108
  19.4 31.9 %collective-permute-done.1 = bf16[239,4096]{1,0:T(8,128)(2,1)S(1)} collective-permute-done((bf16[239,4096]{1,0:T(8,128)(2,1)}, bf16[239,4096]{1,0:T(8,128)(2,1)S(1)}, u32[]{:S(2)}, u32[]{:S(2)}) %collective-permute-start.1) | collective-permute-done | bytes 1957920 | tf_op jit(solution)/shard_map/ppermute | solution.py:103
  51.3 0.7 collective-permute-start.8
  52.2 1.2 copy-done.1
  53.5 3.1 %multiply_reduce_fusion.1 = f32[751]{0:T(1024)S(1)} fusion(bf16[4096]{0:T(1024)(128)(2,1)S(1)} %convert_element_type.20, bf16[512,4096]{1,0:T(8,128)(2,1)S(1)} %copy-done.1, bf16[239,4096]{1,0:T(8,128)(2,1)S(1)} %broadcast_select_fusion.1), kind=kLoop, calls=%fused_computation.1 | loop fusion | flops 24608016 | bytes 6163388 | tf_op jit(solution)/shard_map/reduce_sum | solution.py:35
  56.6 5.5 %multiply_subtract_fusion = f32[751,751]{0,1:T(8,128)S(1)} fusion(f32[751]{0:T(1024)S(1)} %multiply_reduce_fusion.1, bf16[512,4096]{1,0:T(8,128)(2,1)S(1)} %copy-done.1, bf16[239,4096]{1,0:T(8,128)(2,1)S(1)} %broadcast_select_fusion.1, bf16[4096]{0:T(1024)(128)(2,1)S(1)} %convert_element_type.20), kind=kOutput, calls=%fused_computation.11 | convolution fusion | flops 4640445440 | bytes 8419392 | tf_op jit(solution)/shard_map/dot_general | solution.py:39
  62.1 0.9 slice_add_fusion.1
  63.0 0.8 slice_add_fusion
  63.8 0.8 slice_add_fusion.2
  64.7 0.7 slice_add_fusion.3
  65.8 0.6 slice_add_fusion.4
  66.9 0.6 slice_add_fusion.5
  68.7 0.8 constant_dynamic-slice_fusion
  70.6 37.7 %collective-permute-done.8 = bf16[256,4096]{1,0:T(8,128)(2,1)} collective-permute-done((bf16[256,4096]{1,0:T(8,128)(2,1)}, bf16[256,4096]{1,0:T(8,128)(2,1)}, u32[]{:S(2)}, u32[]{:S(2)}) %collective-permute-start.8) | collective-permute-done | bytes 2097184 | tf_op jit(solution)/shard_map/ppermute | solution.py:109
  108.3 2.5 %pad_maximum_fusion = bf16[512,4096]{1,0:T(8,128)(2,1)S(1)} fusion(bf16[256,4096]{1,0:T(8,128)(2,1)} %collective-permute-done.8, bf16[256,4096]{1,0:T(8,128)(2,1)} %collective-permute-done.7), kind=kLoop, calls=%fused_computation.6 | loop fusion | flops 8388608 | bytes 8388608 | tf_op jit(solution)/shard_map/concatenate | solution.py:107
  110.8 2.9 %multiply_reduce_fusion = f32[751]{0:T(1024)S(1)} fusion(bf16[4096]{0:T(1024)(128)(2,1)S(1)} %convert_element_type.20, bf16[512,4096]{1,0:T(8,128)(2,1)S(1)} %pad_maximum_fusion, bf16[239,4096]{1,0:T(8,128)(2,1)S(1)} %broadcast_select_fusion), kind=kLoop, calls=%fused_computation | loop fusion | flops 24608016 | bytes 6163388 | tf_op jit(solution)/shard_map/reduce_sum | solution.py:35
  113.7 3.5 %multiply_reduce_fusion.2 = f32[512]{0:T(512)S(1)} fusion(bf16[4096]{0:T(1024)(128)(2,1)S(1)} %convert_element_type.20, bf16[239,4096]{1,0:T(8,128)(2,1)S(1)} %collective-permute-done.1, bf16[273,4096]{1,0:T(8,128)(2,1)} %collective-permute-done.4), kind=kLoop, calls=%fused_computation.2 | loop fusion | flops 16776704 | bytes 4204544 | tf_op jit(solution)/shard_map/reduce_sum | solution.py:35
  117.2 5.5 %multiply_subtract_fusion.2 = f32[751,512]{0,1:T(8,128)S(1)} fusion(f32[512]{0:T(512)S(1)} %multiply_reduce_fusion.2, f32[751]{0:T(1024)S(1)} %multiply_reduce_fusion.1, bf16[239,4096]{1,0:T(8,128)(2,1)S(1)} %collective-permute-done.1, bf16[273,4096]{1,0:T(8,128)(2,1)} %collective-permute-done.4, bf16[4096]{0:T(1024)(128)(2,1)S(1)} %convert_element_type.20, ...), kind=kOutput, calls=%fused_computation.27 | convolution fusion | flops 3182115328 | bytes 11897788 | tf_op jit(solution)/shard_map/dot_general | solution.py:47
  122.8 0.6 slice_add_fusion.11
  125.4 5.5 %multiply_subtract_fusion.1 = f32[751,512]{0,1:T(8,128)S(1)} fusion(f32[751]{0:T(1024)S(1)} %multiply_reduce_fusion, f32[512]{0:T(512)S(1)} %multiply_reduce_fusion.2, bf16[512,4096]{1,0:T(8,128)(2,1)S(1)} %pad_maximum_fusion, bf16[239,4096]{1,0:T(8,128)(2,1)S(1)} %broadcast_select_fusion, bf16[4096]{0:T(1024)(128)(2,1)S(1)} %convert_element_type.20, ...), kind=kOutput, calls=%fused_computation.26 | convolution fusion | flops 3182115328 | bytes 11897788 | tf_op jit(solution)/shard_map/dot_general | solution.py:47
  130.9 0.6 slice_add_fusion.8
  132.1 0.6 slice_add_fusion.6
  133.1 0.6 slice_add_fusion.23
  137.2 4.4 %collective-permute-done.3 = bf16[239,4096]{1,0:T(8,128)(2,1)} collective-permute-done((bf16[239,4096]{1,0:T(8,128)(2,1)S(1)}, bf16[239,4096]{1,0:T(8,128)(2,1)}, u32[]{:S(2)}, u32[]{:S(2)}) %collective-permute-start.3) | collective-permute-done | bytes 1957920 | tf_op jit(solution)/shard_map/ppermute | solution.py:116
  141.6 2.3 multiply_reduce_fusion.4
  144.0 2.2 add_subtract_fusion.1
  150.5 2.2 add_subtract_fusion
  152.7 0.7 fusion.1
  157.1 0.6 collective-permute-start.5
  158.0 0.7 fusion.8
  158.6 1.9 collective-permute-start.10
  160.5 19.7 %collective-permute-start.9 = (f32[512,256]{0,1:T(8,128)S(1)}, f32[512,256]{0,1:T(8,128)S(1)}, u32[]{:S(2)}, u32[]{:S(2)}) collective-permute-start(f32[512,256]{0,1:T(8,128)S(1)} %get-tuple-element.30), channel_id=1, source_target_pairs={{0,2},{1,3},{2,4},{3,5},{4,6},{5,7},{6,8},{7,9},{8,10},{9,11},{10,... | collective-permute-start | bytes 1572872 | tf_op jit(solution)/shard_map/ppermute | solution.py:154
  180.2 13.9 %collective-permute-done.2 = f32[512,256]{0,1:T(8,128)S(1)} collective-permute-done((f32[512,256]{0,1:T(8,128)}, f32[512,256]{0,1:T(8,128)S(1)}, u32[]{:S(2)}, u32[]{:S(2)}) %collective-permute-start.2) | collective-permute-done | bytes 524320 | tf_op jit(solution)/shard_map/ppermute | solution.py:136
  194.1 11.1 %collective-permute-done.5 = f32[512,256]{0,1:T(8,128)S(1)} collective-permute-done((f32[512,256]{0,1:T(8,128)S(1)}, f32[512,256]{0,1:T(8,128)S(1)}, u32[]{:S(2)}, u32[]{:S(2)}) %collective-permute-start.5) | collective-permute-done | bytes 524320 | tf_op jit(solution)/shard_map/ppermute | solution.py:136
  205.9 3.1 %collective-permute-start.11 = (f32[512]{0:T(512)S(1)}, f32[512]{0:T(512)S(1)}, u32[]{:S(2)}, u32[]{:S(2)}) collective-permute-start(f32[512]{0:T(512)S(1)} %add.318), channel_id=1, source_target_pairs={{0,1},{1,0},{2,3},{3,2},{4,5},{5,4},{6,7},{7,6},{8,9},{9,8},{10,11... | collective-permute-start | bytes 6152 | tf_op jit(solution)/shard_map/ppermute | solution.py:164
  209.0 1.8 collective-permute-start.12
  210.8 12.6 %collective-permute-start.13 = (f32[256]{0:T(256)S(1)}, f32[256]{0:T(256)S(1)}, u32[]{:S(2)}, u32[]{:S(2)}) collective-permute-start(f32[256]{0:T(256)S(1)} %get-tuple-element.33), channel_id=1, source_target_pairs={{0,3},{1,2},{2,5},{3,4},{4,7},{5,6},{6,9},{7,8},{8,11},{9,10},{10,... | collective-permute-start | bytes 3080 | tf_op jit(solution)/shard_map/ppermute | solution.py:168
  223.4 12.0 %collective-permute-start.14 = (f32[256]{0:T(256)S(1)}, f32[256]{0:T(256)S(1)}, u32[]{:S(2)}, u32[]{:S(2)}) collective-permute-start(f32[256]{0:T(256)S(1)} %get-tuple-element.34), channel_id=1, source_target_pairs={{0,4},{1,5},{2,6},{3,7},{4,8},{5,9},{6,10},{7,11},{8,12},{9,13},{1... | collective-permute-start | bytes 3080 | tf_op jit(solution)/shard_map/ppermute | solution.py:167
  235.4 1.3 collective-permute-done.14
  236.7 5.9 %collective-permute-done.15 = f32[256]{0:T(256)S(1)} collective-permute-done((f32[256]{0:T(256)S(1)}, f32[256]{0:T(256)S(1)}, u32[]{:S(2)}, u32[]{:S(2)}) %collective-permute-start.15) | collective-permute-done | bytes 1056 | tf_op jit(solution)/shard_map/ppermute | solution.py:168
  243.0 1.6 copy.9
  (86 shorter events, 19.3 us)
Async XLA Ops:
  3.3 10.3 %copy-start = (bf16[512,4096]{1,0:T(8,128)(2,1)S(1)}, bf16[512,4096]{1,0:T(8,128)(2,1)}, u32[]{:S(2)}) copy-start(bf16[512,4096]{1,0:T(8,128)(2,1)} %param.3) | copy-start | bytes 12582916
  3.3 48.0 %collective-permute-start.1 = (bf16[239,4096]{1,0:T(8,128)(2,1)}, bf16[239,4096]{1,0:T(8,128)(2,1)S(1)}, u32[]{:S(2)}, u32[]{:S(2)}) collective-permute-start(bf16[239,4096]{1,0:T(8,128)(2,1)} %slice.318), channel_id=1, source_target_pairs={{0,2},{2,4},{4,6},{6,8},{8,10},{10,12},{12,14},{14,0},{1,3},{3,5},... | collective-permute-start | bytes 5873672 | tf_op jit(solution)/shard_map/ppermute | solution.py:103
  4.9 47.2 %collective-permute-start = (bf16[239,4096]{1,0:T(8,128)(2,1)}, bf16[239,4096]{1,0:T(8,128)(2,1)}, u32[]{:S(2)}, u32[]{:S(2)}) collective-permute-start(bf16[239,4096]{1,0:T(8,128)(2,1)} %slice.318), channel_id=1, source_target_pairs={{14,16},{30,32},{46,48},{62,64},{78,80},{94,96},{110,112},{15,17},... | collective-permute-start | bytes 5873672 | tf_op jit(solution)/shard_map/ppermute | solution.py:104
  6.8 62.7 %collective-permute-start.6 = (bf16[239,4096]{1,0:T(8,128)(2,1)}, bf16[239,4096]{1,0:T(8,128)(2,1)}, u32[]{:S(2)}, u32[]{:S(2)}) collective-permute-start(bf16[239,4096]{1,0:T(8,128)(2,1)} %slice.318), channel_id=1, source_target_pairs={{14,30},{30,46},{46,62},{62,78},{78,94},{94,110},{110,126},{15,31}... | collective-permute-start | bytes 5873672 | tf_op jit(solution)/shard_map/ppermute | solution.py:111
  12.0 6.7 %copy-start.4 = (s32[4096]{0:T(1024)S(1)}, s32[4096]{0:T(1024)}, u32[]{:S(2)}) copy-start(s32[4096]{0:T(1024)} %param.4) | copy-start | bytes 49156
  12.0 101.7 %collective-permute-start.4 = (bf16[273,4096]{1,0:T(8,128)(2,1)}, bf16[273,4096]{1,0:T(8,128)(2,1)}, u32[]{:S(2)}, u32[]{:S(2)}) collective-permute-start(bf16[273,4096]{1,0:T(8,128)(2,1)} %slice.339), channel_id=1, source_target_pairs={{0,2},{2,4},{4,6},{6,8},{8,10},{10,12},{12,14},{14,0},{1,3},{3,5},... | collective-permute-start | bytes 6709256 | tf_op jit(solution)/shard_map/ppermute | solution.py:105
  16.1 54.5 %collective-permute-start.7 = (bf16[256,4096]{1,0:T(8,128)(2,1)}, bf16[256,4096]{1,0:T(8,128)(2,1)}, u32[]{:S(2)}, u32[]{:S(2)}) collective-permute-start(bf16[256,4096]{1,0:T(8,128)(2,1)} %get-tuple-element.17), channel_id=1, source_target_pairs={{0,14},{2,0},{4,2},{6,4},{8,6},{10,8},{12,10},{14,12},{1,15},{3,1}... | collective-permute-start | bytes 6291464 | tf_op jit(solution)/shard_map/ppermute | solution.py:108
  51.3 2.2 copy-start.1
  51.3 57.0 %collective-permute-start.8 = (bf16[256,4096]{1,0:T(8,128)(2,1)}, bf16[256,4096]{1,0:T(8,128)(2,1)}, u32[]{:S(2)}, u32[]{:S(2)}) collective-permute-start(bf16[256,4096]{1,0:T(8,128)(2,1)} %get-tuple-element.18), channel_id=1, source_target_pairs={{0,14},{2,0},{4,2},{6,4},{8,6},{10,8},{12,10},{14,12},{1,15},{3,1}... | collective-permute-start | bytes 6291464 | tf_op jit(solution)/shard_map/ppermute | solution.py:109
  68.5 73.1 %collective-permute-start.3 = (bf16[239,4096]{1,0:T(8,128)(2,1)S(1)}, bf16[239,4096]{1,0:T(8,128)(2,1)}, u32[]{:S(2)}, u32[]{:S(2)}) collective-permute-start(bf16[239,4096]{1,0:T(8,128)(2,1)S(1)} %broadcast_select_fusion.1), channel_id=1, source_target_pairs={{0,2},{2,4},{4,6},{6,8},{8,10},{10,12},{12,14},{14,0},{1,3},{3,5},... | collective-permute-start | bytes 5873672 | tf_op jit(solution)/shard_map/ppermute | solution.py:116
  69.5 124.5 %collective-permute-start.2 = (f32[512,256]{0,1:T(8,128)}, f32[512,256]{0,1:T(8,128)S(1)}, u32[]{:S(2)}, u32[]{:S(2)}) collective-permute-start(f32[512,256]{0,1:T(8,128)} %constant_dynamic-slice_fusion), channel_id=1, source_target_pairs={{0,1},{1,0},{2,3},{3,2},{4,5},{5,4},{6,7},{7,6},{8,9},{9,8},{10,11... | collective-permute-start | bytes 1572872 | tf_op jit(solution)/shard_map/ppermute | solution.py:136
  122.8 11.0 %copy-start.2 = (f32[751,512]{0,1:T(8,128)}, f32[751,512]{0,1:T(8,128)S(1)}, u32[]{:S(2)}) copy-start(f32[751,512]{0,1:T(8,128)S(1)} %multiply_subtract_fusion.2) | copy-start | bytes 4614148
  130.9 3.5 %copy-start.3 = (f32[751,512]{0,1:T(8,128)}, f32[751,512]{0,1:T(8,128)S(1)}, u32[]{:S(2)}) copy-start(f32[751,512]{0,1:T(8,128)S(1)} %multiply_subtract_fusion.1) | copy-start | bytes 4614148
  144.0 2.2 slice-start
  150.5 2.2 slice-start.1
  157.1 48.1 %collective-permute-start.5 = (f32[512,256]{0,1:T(8,128)S(1)}, f32[512,256]{0,1:T(8,128)S(1)}, u32[]{:S(2)}, u32[]{:S(2)}) collective-permute-start(f32[512,256]{0,1:T(8,128)S(1)} %fusion.13), channel_id=1, source_target_pairs={{0,1},{1,0},{2,3},{3,2},{4,5},{5,4},{6,7},{7,6},{8,9},{9,8},{10,11... | collective-permute-start | bytes 1572872 | tf_op jit(solution)/shard_map/ppermute | solution.py:136
  158.6 47.1 %collective-permute-start.10 = (f32[512,256]{0,1:T(8,128)S(1)}, f32[512,256]{0,1:T(8,128)S(1)}, u32[]{:S(2)}, u32[]{:S(2)}) collective-permute-start(f32[512,256]{0,1:T(8,128)S(1)} %get-tuple-element.29), channel_id=1, source_target_pairs={{0,3},{1,2},{2,5},{3,4},{4,7},{5,6},{6,9},{7,8},{8,11},{9,10},{10,... | collective-permute-start | bytes 1572872 | tf_op jit(solution)/shard_map/ppermute | solution.py:155
  160.5 45.2 %collective-permute-start.9 = (f32[512,256]{0,1:T(8,128)S(1)}, f32[512,256]{0,1:T(8,128)S(1)}, u32[]{:S(2)}, u32[]{:S(2)}) collective-permute-start(f32[512,256]{0,1:T(8,128)S(1)} %get-tuple-element.30), channel_id=1, source_target_pairs={{0,2},{1,3},{2,4},{3,5},{4,6},{5,7},{6,8},{7,9},{8,10},{9,11},{10,... | collective-permute-start | bytes 1572872 | tf_op jit(solution)/shard_map/ppermute | solution.py:154
  205.9 36.7 %collective-permute-start.11 = (f32[512]{0:T(512)S(1)}, f32[512]{0:T(512)S(1)}, u32[]{:S(2)}, u32[]{:S(2)}) collective-permute-start(f32[512]{0:T(512)S(1)} %add.318), channel_id=1, source_target_pairs={{0,1},{1,0},{2,3},{3,2},{4,5},{5,4},{6,7},{7,6},{8,9},{9,8},{10,11... | collective-permute-start | bytes 6152 | tf_op jit(solution)/shard_map/ppermute | solution.py:164
  209.0 26.4 %collective-permute-start.12 = (f32[256]{0:T(256)S(1)}, f32[256]{0:T(256)S(1)}, u32[]{:S(2)}, u32[]{:S(2)}) collective-permute-start(f32[256]{0:T(256)S(1)} %get-tuple-element.34), channel_id=1, source_target_pairs={{0,2},{1,3},{2,4},{3,5},{4,6},{5,7},{6,8},{7,9},{8,10},{9,11},{10,... | collective-permute-start | bytes 3080 | tf_op jit(solution)/shard_map/ppermute | solution.py:167
  210.8 24.7 %collective-permute-start.13 = (f32[256]{0:T(256)S(1)}, f32[256]{0:T(256)S(1)}, u32[]{:S(2)}, u32[]{:S(2)}) collective-permute-start(f32[256]{0:T(256)S(1)} %get-tuple-element.33), channel_id=1, source_target_pairs={{0,3},{1,2},{2,5},{3,4},{4,7},{5,6},{6,9},{7,8},{8,11},{9,10},{10,... | collective-permute-start | bytes 3080 | tf_op jit(solution)/shard_map/ppermute | solution.py:168
  223.4 13.3 %collective-permute-start.14 = (f32[256]{0:T(256)S(1)}, f32[256]{0:T(256)S(1)}, u32[]{:S(2)}, u32[]{:S(2)}) collective-permute-start(f32[256]{0:T(256)S(1)} %get-tuple-element.34), channel_id=1, source_target_pairs={{0,4},{1,5},{2,6},{3,7},{4,8},{5,9},{6,10},{7,11},{8,12},{9,13},{1... | collective-permute-start | bytes 3080 | tf_op jit(solution)/shard_map/ppermute | solution.py:167
  235.4 7.2 %collective-permute-start.15 = (f32[256]{0:T(256)S(1)}, f32[256]{0:T(256)S(1)}, u32[]{:S(2)}, u32[]{:S(2)}) collective-permute-start(f32[256]{0:T(256)S(1)} %get-tuple-element.33), channel_id=1, source_target_pairs={{0,5},{1,4},{2,7},{3,6},{4,9},{5,8},{6,11},{7,10},{8,13},{9,12},{1... | collective-permute-start | bytes 3080 | tf_op jit(solution)/shard_map/ppermute | solution.py:168

commit v11 on v10

--- a/solution.py
+++ b/solution.py
@@ -162,11 +162,10 @@
     kernel = jnp.concatenate([kernel_early, kernel_late[None]], axis=0)
     part_degree = jnp.sum(kernel_early, axis=(0, 2)) + jnp.sum(kernel_late, axis=1)
     degree = part_degree + lax.ppermute(part_degree, "space", swap)
-    degree_list = [lax.dynamic_slice_in_dim(degree, start_col, column_width, 0)]
+    degree_half = lax.dynamic_slice_in_dim(degree, start_col, column_width, 0)
+    degree_list = [degree_half]
     for offset in range(1, BANDS):
-        d_same = lax.ppermute(lax.dynamic_slice_in_dim(part_degree, start_col, column_width, 0), cs, col_shift(offset, False))
-        d_cross = lax.ppermute(lax.dynamic_slice_in_dim(part_degree, other_col, column_width, 0), cs, col_shift(offset, True))
-        degree_list.append(d_same + d_cross)
+        degree_list.append(lax.ppermute(degree_half, "col", ring("col", offset)))
     column_degrees = jnp.stack(degree_list)
     factor = float(BANDS * block_rows)
     return factor * kernel / jnp.sqrt(degree[None, :, None] * column_degrees[:, None, :])

time: 249 us -> 245 us (0.984)
  the two profiles are of different devices: /device:TPU:98 before, /device:TPU:4 now
where the time goes in v11:
time: 245 us; the launch traced here: 241 us
  waiting for transfers between devices  141 us (58%)
  other arithmetic  36.9 us (15%)
  starting transfers between devices  23.2 us (9%)
  matrix products  20.9 us (9%)
  local copies, waits for them, and re-layouts  18.2 us (7%)
    ppermute x1, waiting for transfers between devices, per_device(): tail_prev = lax.ppermute(tail, 'col', up)  51.3 us
    ppermute x1, waiting for transfers between devices, per_device(): head_prev = lax.ppermute(head, 'col', up)  23.4 us
    ppermute x1, waiting for transfers between devices, per_device(): lax.ppermute(snapshots[half_rows:], 'col', down)  23.2 us
    ppermute x2, waiting for transfers between devices, space_sum(): return mine + lax.ppermute(theirs, 'space', swap)  15.8 us
    dot_general x4, matrix products, gram(): lax.dot_general(rows, cols, (((1,), (1,)), ((), ())), preferred_element_t...  15.3 us
    ppermute x1, waiting for transfers between devices, per_device(): hist_prev = lax.ppermute(hist_send, 'col', up)  13.2 us
    reduce_sum x5, other arithmetic, square_norms(): return jnp.sum(jnp.square(values.astype(jnp.float32)), axis=1)  12.3 us
    add x24, other arithmetic, lag_sum_rect(): doubled = doubled[width:width + r, width:width + c] + doubled[:r, :c]  12 us
  transfers between devices with their start and end apart: 14, of which 10 were waited for; matrix products, arithmetic and copies ran while one was open for 29% of the time, Pallas kernels for 0%

profile of v11, /device:TPU:4, one launch (start us, length us, event | category | flops | bytes accessed | tf_op | source)
XLA Modules:
  0.0 240.9 jit_solution(14732624898378293359)
XLA Ops:
  0.0 3.3 %slice.318 = bf16[239,4096]{1,0:T(8,128)(2,1)} slice(bf16[512,4096]{1,0:T(8,128)(2,1)} %param.3), slice={[273:512], [0:4096]} | slice | bytes 3915776 | tf_op jit(solution)/shard_map/slice | solution.py:95
  3.3 1.6 collective-permute-start.1
  4.8 1.3 collective-permute-start
  6.1 1.9 collective-permute-start.6
  8.1 3.3 %slice.339 = bf16[273,4096]{1,0:T(8,128)(2,1)} slice(bf16[512,4096]{1,0:T(8,128)(2,1)} %param.3), slice={[0:273], [0:4096]} | slice | bytes 4472832 | tf_op jit(solution)/shard_map/slice | solution.py:96
  11.3 2.2 collective-permute-start.4
  13.6 2.5 %fusion.23 = (bf16[256,4096]{1,0:T(8,128)(2,1)}, bf16[256,4096]{1,0:T(8,128)(2,1)}) fusion(bf16[512,4096]{1,0:T(8,128)(2,1)S(1)} %copy-done), kind=kLoop, calls=%fused_computation.101 | loop fusion | bytes 8388608 | tf_op jit(solution)/shard_map/slice | solution.py:108
  16.1 4.5 %collective-permute-start.7 = (bf16[256,4096]{1,0:T(8,128)(2,1)}, bf16[256,4096]{1,0:T(8,128)(2,1)}, u32[]{:S(2)}, u32[]{:S(2)}) collective-permute-start(bf16[256,4096]{1,0:T(8,128)(2,1)} %get-tuple-element.17), channel_id=1, source_target_pairs={{0,14},{2,0},{4,2},{6,4},{8,6},{10,8},{12,10},{14,12},{1,15},{3,1}... | collective-permute-start | bytes 6291464 | tf_op jit(solution)/shard_map/ppermute | solution.py:108
  21.3 51.3 %collective-permute-done.1 = bf16[239,4096]{1,0:T(8,128)(2,1)S(1)} collective-permute-done((bf16[239,4096]{1,0:T(8,128)(2,1)}, bf16[239,4096]{1,0:T(8,128)(2,1)S(1)}, u32[]{:S(2)}, u32[]{:S(2)}) %collective-permute-start.1) | collective-permute-done | bytes 1957920 | tf_op jit(solution)/shard_map/ppermute | solution.py:103
  72.6 1.9 broadcast_select_fusion.1
  74.5 0.9 copy-done.1
  75.3 3.1 %multiply_reduce_fusion.1 = f32[751]{0:T(1024)S(1)} fusion(bf16[4096]{0:T(1024)(128)(2,1)S(1)} %convert_element_type.20, bf16[512,4096]{1,0:T(8,128)(2,1)S(1)} %copy-done.1, bf16[239,4096]{1,0:T(8,128)(2,1)S(1)} %broadcast_select_fusion.1), kind=kLoop, calls=%fused_computation.1 | loop fusion | flops 24608016 | bytes 6163388 | tf_op jit(solution)/shard_map/reduce_sum | solution.py:35
  78.4 5.5 %multiply_subtract_fusion = f32[751,751]{0,1:T(8,128)S(1)} fusion(f32[751]{0:T(1024)S(1)} %multiply_reduce_fusion.1, bf16[512,4096]{1,0:T(8,128)(2,1)S(1)} %copy-done.1, bf16[239,4096]{1,0:T(8,128)(2,1)S(1)} %broadcast_select_fusion.1, bf16[4096]{0:T(1024)(128)(2,1)S(1)} %convert_element_type.20), kind=kOutput, calls=%fused_computation.11 | convolution fusion | flops 4640445440 | bytes 8419392 | tf_op jit(solution)/shard_map/dot_general | solution.py:39
  84.0 0.9 slice_add_fusion.1
  84.8 0.8 slice_add_fusion
  85.7 0.8 slice_add_fusion.2
  86.5 0.7 slice_add_fusion.3
  87.7 0.6 slice_add_fusion.4
  88.8 0.6 slice_add_fusion.5
  90.5 0.8 constant_dynamic-slice_fusion
  91.3 3.7 %collective-permute-start.2 = (f32[512,256]{0,1:T(8,128)}, f32[512,256]{0,1:T(8,128)S(1)}, u32[]{:S(2)}, u32[]{:S(2)}) collective-permute-start(f32[512,256]{0,1:T(8,128)} %constant_dynamic-slice_fusion), channel_id=1, source_target_pairs={{0,1},{1,0},{2,3},{3,2},{4,5},{5,4},{6,7},{7,6},{8,9},{9,8},{10,11... | collective-permute-start | bytes 1572872 | tf_op jit(solution)/shard_map/ppermute | solution.py:136
  95.6 23.2 %collective-permute-done.8 = bf16[256,4096]{1,0:T(8,128)(2,1)} collective-permute-done((bf16[256,4096]{1,0:T(8,128)(2,1)}, bf16[256,4096]{1,0:T(8,128)(2,1)}, u32[]{:S(2)}, u32[]{:S(2)}) %collective-permute-start.8) | collective-permute-done | bytes 2097184 | tf_op jit(solution)/shard_map/ppermute | solution.py:109
  118.8 2.5 %pad_maximum_fusion = bf16[512,4096]{1,0:T(8,128)(2,1)S(1)} fusion(bf16[256,4096]{1,0:T(8,128)(2,1)} %collective-permute-done.8, bf16[256,4096]{1,0:T(8,128)(2,1)} %collective-permute-done.7), kind=kLoop, calls=%fused_computation.6 | loop fusion | flops 8388608 | bytes 8388608 | tf_op jit(solution)/shard_map/concatenate | solution.py:107
  121.3 2.9 %multiply_reduce_fusion = f32[751]{0:T(1024)S(1)} fusion(bf16[4096]{0:T(1024)(128)(2,1)S(1)} %convert_element_type.20, bf16[512,4096]{1,0:T(8,128)(2,1)S(1)} %pad_maximum_fusion, bf16[239,4096]{1,0:T(8,128)(2,1)S(1)} %broadcast_select_fusion), kind=kLoop, calls=%fused_computation | loop fusion | flops 24608016 | bytes 6163388 | tf_op jit(solution)/shard_map/reduce_sum | solution.py:35
  124.3 23.4 %collective-permute-done.4 = bf16[273,4096]{1,0:T(8,128)(2,1)} collective-permute-done((bf16[273,4096]{1,0:T(8,128)(2,1)}, bf16[273,4096]{1,0:T(8,128)(2,1)}, u32[]{:S(2)}, u32[]{:S(2)}) %collective-permute-start.4) | collective-permute-done | bytes 2236448 | tf_op jit(solution)/shard_map/ppermute | solution.py:105
  147.7 3.5 %multiply_reduce_fusion.2 = f32[512]{0:T(512)S(1)} fusion(bf16[4096]{0:T(1024)(128)(2,1)S(1)} %convert_element_type.20, bf16[239,4096]{1,0:T(8,128)(2,1)S(1)} %collective-permute-done.1, bf16[273,4096]{1,0:T(8,128)(2,1)} %collective-permute-done.4), kind=kLoop, calls=%fused_computation.2 | loop fusion | flops 16776704 | bytes 4204544 | tf_op jit(solution)/shard_map/reduce_sum | solution.py:35
  151.2 5.5 %multiply_subtract_fusion.2 = f32[751,512]{0,1:T(8,128)S(1)} fusion(f32[512]{0:T(512)S(1)} %multiply_reduce_fusion.2, f32[751]{0:T(1024)S(1)} %multiply_reduce_fusion.1, bf16[239,4096]{1,0:T(8,128)(2,1)S(1)} %collective-permute-done.1, bf16[273,4096]{1,0:T(8,128)(2,1)} %collective-permute-done.4, bf16[4096]{0:T(1024)(128)(2,1)S(1)} %convert_element_type.20, ...), kind=kOutput, calls=%fused_computation.27 | convolution fusion | flops 3182115328 | bytes 11897788 | tf_op jit(solution)/shard_map/dot_general | solution.py:47
  156.7 0.6 slice_add_fusion.11
  157.3 0.6 slice_add_fusion.10
  157.8 0.6 slice_add_fusion.9
  159.3 5.5 %multiply_subtract_fusion.1 = f32[751,512]{0,1:T(8,128)S(1)} fusion(f32[751]{0:T(1024)S(1)} %multiply_reduce_fusion, f32[512]{0:T(512)S(1)} %multiply_reduce_fusion.2, bf16[512,4096]{1,0:T(8,128)(2,1)S(1)} %pad_maximum_fusion, bf16[239,4096]{1,0:T(8,128)(2,1)S(1)} %broadcast_select_fusion, bf16[4096]{0:T(1024)(128)(2,1)S(1)} %convert_element_type.20, ...), kind=kOutput, calls=%fused_computation.26 | convolution fusion | flops 3182115328 | bytes 11897788 | tf_op jit(solution)/shard_map/dot_general | solution.py:47
  164.8 0.6 slice_add_fusion.8
  166.0 0.6 slice_add_fusion.6
  167.0 0.6 slice_add_fusion.23
  171.1 13.2 %collective-permute-done.3 = bf16[239,4096]{1,0:T(8,128)(2,1)} collective-permute-done((bf16[239,4096]{1,0:T(8,128)(2,1)S(1)}, bf16[239,4096]{1,0:T(8,128)(2,1)}, u32[]{:S(2)}, u32[]{:S(2)}) %collective-permute-start.3) | collective-permute-done | bytes 1957920 | tf_op jit(solution)/shard_map/ppermute | solution.py:116
  184.3 2.3 multiply_reduce_fusion.4
  186.6 2.2 add_subtract_fusion.1
  193.1 2.2 add_subtract_fusion
  195.3 0.7 fusion.1
  199.8 3.7 %collective-permute-start.5 = (f32[512,256]{0,1:T(8,128)S(1)}, f32[512,256]{0,1:T(8,128)S(1)}, u32[]{:S(2)}, u32[]{:S(2)}) collective-permute-start(f32[512,256]{0,1:T(8,128)S(1)} %fusion.13), channel_id=1, source_target_pairs={{0,1},{1,0},{2,3},{3,2},{4,5},{5,4},{6,7},{7,6},{8,9},{9,8},{10,11... | collective-permute-start | bytes 1572872 | tf_op jit(solution)/shard_map/ppermute | solution.py:136
  203.6 0.6 fusion.8
  204.6 15.8 %collective-permute-done.5 = f32[512,256]{0,1:T(8,128)S(1)} collective-permute-done((f32[512,256]{0,1:T(8,128)S(1)}, f32[512,256]{0,1:T(8,128)S(1)}, u32[]{:S(2)}, u32[]{:S(2)}) %collective-permute-start.5) | collective-permute-done | bytes 524320 | tf_op jit(solution)/shard_map/ppermute | solution.py:136
  220.9 2.3 collective-permute-done.10
  223.2 3.8 %collective-permute-done.9 = f32[512,256]{0,1:T(8,128)S(1)} collective-permute-done((f32[512,256]{0,1:T(8,128)S(1)}, f32[512,256]{0,1:T(8,128)S(1)}, u32[]{:S(2)}, u32[]{:S(2)}) %collective-permute-start.9) | collective-permute-done | bytes 524320 | tf_op jit(solution)/shard_map/ppermute | solution.py:154
  227.2 3.9 %collective-permute-start.11 = (f32[512]{0:T(512)S(1)}, f32[512]{0:T(512)S(1)}, u32[]{:S(2)}, u32[]{:S(2)}) collective-permute-start(f32[512]{0:T(512)S(1)} %add.308), channel_id=1, source_target_pairs={{0,1},{1,0},{2,3},{3,2},{4,5},{5,4},{6,7},{7,6},{8,9},{9,8},{10,11... | collective-permute-start | bytes 6152 | tf_op jit(solution)/shard_map/ppermute | solution.py:164
  231.1 1.6 collective-permute-done.11
  232.8 5.6 %collective-permute-done.12 = f32[256]{0:T(256)S(1)} collective-permute-done((f32[256]{0:T(256)S(1)}, f32[256]{0:T(256)S(1)}, u32[]{:S(2)}, u32[]{:S(2)}) %collective-permute-start.12) | collective-permute-done | bytes 1056 | tf_op jit(solution)/shard_map/ppermute | solution.py:168
  239.1 1.6 copy.9
  (79 shorter events, 17.9 us)
Async XLA Ops:
  3.3 10.3 %copy-start = (bf16[512,4096]{1,0:T(8,128)(2,1)S(1)}, bf16[512,4096]{1,0:T(8,128)(2,1)}, u32[]{:S(2)}) copy-start(bf16[512,4096]{1,0:T(8,128)(2,1)} %param.3) | copy-start | bytes 12582916
  3.3 69.3 %collective-permute-start.1 = (bf16[239,4096]{1,0:T(8,128)(2,1)}, bf16[239,4096]{1,0:T(8,128)(2,1)S(1)}, u32[]{:S(2)}, u32[]{:S(2)}) collective-permute-start(bf16[239,4096]{1,0:T(8,128)(2,1)} %slice.318), channel_id=1, source_target_pairs={{0,2},{2,4},{4,6},{6,8},{8,10},{10,12},{12,14},{14,0},{1,3},{3,5},... | collective-permute-start | bytes 5873672 | tf_op jit(solution)/shard_map/ppermute | solution.py:103
  4.8 67.7 %collective-permute-start = (bf16[239,4096]{1,0:T(8,128)(2,1)}, bf16[239,4096]{1,0:T(8,128)(2,1)}, u32[]{:S(2)}, u32[]{:S(2)}) collective-permute-start(bf16[239,4096]{1,0:T(8,128)(2,1)} %slice.318), channel_id=1, source_target_pairs={{14,16},{30,32},{46,48},{62,64},{78,80},{94,96},{110,112},{15,17},... | collective-permute-start | bytes 5873672 | tf_op jit(solution)/shard_map/ppermute | solution.py:104
  6.1 85.2 %collective-permute-start.6 = (bf16[239,4096]{1,0:T(8,128)(2,1)}, bf16[239,4096]{1,0:T(8,128)(2,1)}, u32[]{:S(2)}, u32[]{:S(2)}) collective-permute-start(bf16[239,4096]{1,0:T(8,128)(2,1)} %slice.318), channel_id=1, source_target_pairs={{14,30},{30,46},{46,62},{62,78},{78,94},{94,110},{110,126},{15,31}... | collective-permute-start | bytes 5873672 | tf_op jit(solution)/shard_map/ppermute | solution.py:111
  11.3 9.3 %copy-start.4 = (s32[4096]{0:T(1024)S(1)}, s32[4096]{0:T(1024)}, u32[]{:S(2)}) copy-start(s32[4096]{0:T(1024)} %param.4) | copy-start | bytes 49156
  11.3 136.3 %collective-permute-start.4 = (bf16[273,4096]{1,0:T(8,128)(2,1)}, bf16[273,4096]{1,0:T(8,128)(2,1)}, u32[]{:S(2)}, u32[]{:S(2)}) collective-permute-start(bf16[273,4096]{1,0:T(8,128)(2,1)} %slice.339), channel_id=1, source_target_pairs={{0,2},{2,4},{4,6},{6,8},{8,10},{10,12},{12,14},{14,0},{1,3},{3,5},... | collective-permute-start | bytes 6709256 | tf_op jit(solution)/shard_map/ppermute | solution.py:105
  16.1 79.5 %collective-permute-start.7 = (bf16[256,4096]{1,0:T(8,128)(2,1)}, bf16[256,4096]{1,0:T(8,128)(2,1)}, u32[]{:S(2)}, u32[]{:S(2)}) collective-permute-start(bf16[256,4096]{1,0:T(8,128)(2,1)} %get-tuple-element.17), channel_id=1, source_target_pairs={{0,14},{2,0},{4,2},{6,4},{8,6},{10,8},{12,10},{14,12},{1,15},{3,1}... | collective-permute-start | bytes 6291464 | tf_op jit(solution)/shard_map/ppermute | solution.py:108
  72.6 2.8 %copy-start.1 = (bf16[512,4096]{1,0:T(8,128)(2,1)S(1)}, bf16[512,4096]{1,0:T(8,128)(2,1)}, u32[]{:S(2)}) copy-start(bf16[512,4096]{1,0:T(8,128)(2,1)} %param.3) | copy-start | bytes 12582916
  72.6 46.3 %collective-permute-start.8 = (bf16[256,4096]{1,0:T(8,128)(2,1)}, bf16[256,4096]{1,0:T(8,128)(2,1)}, u32[]{:S(2)}, u32[]{:S(2)}) collective-permute-start(bf16[256,4096]{1,0:T(8,128)(2,1)} %get-tuple-element.18), channel_id=1, source_target_pairs={{0,14},{2,0},{4,2},{6,4},{8,6},{10,8},{12,10},{14,12},{1,15},{3,1}... | collective-permute-start | bytes 6291464 | tf_op jit(solution)/shard_map/ppermute | solution.py:109
  90.4 93.9 %collective-permute-start.3 = (bf16[239,4096]{1,0:T(8,128)(2,1)S(1)}, bf16[239,4096]{1,0:T(8,128)(2,1)}, u32[]{:S(2)}, u32[]{:S(2)}) collective-permute-start(bf16[239,4096]{1,0:T(8,128)(2,1)S(1)} %broadcast_select_fusion.1), channel_id=1, source_target_pairs={{0,2},{2,4},{4,6},{6,8},{8,10},{10,12},{12,14},{14,0},{1,3},{3,5},... | collective-permute-start | bytes 5873672 | tf_op jit(solution)/shard_map/ppermute | solution.py:116
  91.3 113.1 %collective-permute-start.2 = (f32[512,256]{0,1:T(8,128)}, f32[512,256]{0,1:T(8,128)S(1)}, u32[]{:S(2)}, u32[]{:S(2)}) collective-permute-start(f32[512,256]{0,1:T(8,128)} %constant_dynamic-slice_fusion), channel_id=1, source_target_pairs={{0,1},{1,0},{2,3},{3,2},{4,5},{5,4},{6,7},{7,6},{8,9},{9,8},{10,11... | collective-permute-start | bytes 1572872 | tf_op jit(solution)/shard_map/ppermute | solution.py:136
  156.7 11.0 %copy-start.2 = (f32[751,512]{0,1:T(8,128)}, f32[751,512]{0,1:T(8,128)S(1)}, u32[]{:S(2)}) copy-start(f32[751,512]{0,1:T(8,128)S(1)} %multiply_subtract_fusion.2) | copy-start | bytes 4614148
  164.8 3.5 %copy-start.3 = (f32[751,512]{0,1:T(8,128)}, f32[751,512]{0,1:T(8,128)S(1)}, u32[]{:S(2)}) copy-start(f32[751,512]{0,1:T(8,128)S(1)} %multiply_subtract_fusion.1) | copy-start | bytes 4614148
  186.6 2.2 slice-start
  193.1 2.2 slice-start.1
  199.8 20.6 %collective-permute-start.5 = (f32[512,256]{0,1:T(8,128)S(1)}, f32[512,256]{0,1:T(8,128)S(1)}, u32[]{:S(2)}, u32[]{:S(2)}) collective-permute-start(f32[512,256]{0,1:T(8,128)S(1)} %fusion.13), channel_id=1, source_target_pairs={{0,1},{1,0},{2,3},{3,2},{4,5},{5,4},{6,7},{7,6},{8,9},{9,8},{10,11... | collective-permute-start | bytes 1572872 | tf_op jit(solution)/shard_map/ppermute | solution.py:136
  204.3 18.9 %collective-permute-start.10 = (f32[512,256]{0,1:T(8,128)S(1)}, f32[512,256]{0,1:T(8,128)S(1)}, u32[]{:S(2)}, u32[]{:S(2)}) collective-permute-start(f32[512,256]{0,1:T(8,128)S(1)} %get-tuple-element.29), channel_id=1, source_target_pairs={{0,3},{1,2},{2,5},{3,4},{4,7},{5,6},{6,9},{7,8},{8,11},{9,10},{10,... | collective-permute-start | bytes 1572872 | tf_op jit(solution)/shard_map/ppermute | solution.py:155
  204.4 22.7 %collective-permute-start.9 = (f32[512,256]{0,1:T(8,128)S(1)}, f32[512,256]{0,1:T(8,128)S(1)}, u32[]{:S(2)}, u32[]{:S(2)}) collective-permute-start(f32[512,256]{0,1:T(8,128)S(1)} %get-tuple-element.30), channel_id=1, source_target_pairs={{0,2},{1,3},{2,4},{3,5},{4,6},{5,7},{6,8},{7,9},{8,10},{9,11},{10,... | collective-permute-start | bytes 1572872 | tf_op jit(solution)/shard_map/ppermute | solution.py:154
  227.2 5.5 %collective-permute-start.11 = (f32[512]{0:T(512)S(1)}, f32[512]{0:T(512)S(1)}, u32[]{:S(2)}, u32[]{:S(2)}) collective-permute-start(f32[512]{0:T(512)S(1)} %add.308), channel_id=1, source_target_pairs={{0,1},{1,0},{2,3},{3,2},{4,5},{5,4},{6,7},{7,6},{8,9},{9,8},{10,11... | collective-permute-start | bytes 6152 | tf_op jit(solution)/shard_map/ppermute | solution.py:164
  232.7 5.7 %collective-permute-start.12 = (f32[256]{0:T(256)S(1)}, f32[256]{0:T(256)S(1)}, u32[]{:S(2)}, u32[]{:S(2)}) collective-permute-start(f32[256]{0:T(256)S(1)} %dynamic_slice.27), channel_id=1, source_target_pairs={{0,2},{2,4},{4,6},{6,8},{8,10},{10,12},{12,14},{14,0},{1,3},{3,5},... | collective-permute-start | bytes 3080 | tf_op jit(solution)/shard_map/ppermute | solution.py:168
  232.7 6.0 %collective-permute-start.13 = (f32[256]{0:T(256)S(1)}, f32[256]{0:T(256)S(1)}, u32[]{:S(2)}, u32[]{:S(2)}) collective-permute-start(f32[256]{0:T(256)S(1)} %dynamic_slice.27), channel_id=1, source_target_pairs={{0,4},{2,6},{4,8},{6,10},{8,12},{10,14},{12,0},{14,2},{1,5},{3,7},... | collective-permute-start | bytes 3080 | tf_op jit(solution)/shard_map/ppermute | solution.py:168

commit v12 on v11

--- a/solution.py
+++ b/solution.py
@@ -104,16 +104,14 @@
     tail_to_first = lax.ppermute(tail, flat, to_slot0)
     head_prev = lax.ppermute(head, "col", up)
     half_rows = block_rows // 2
-    block_next = jnp.concatenate([
-        lax.ppermute(snapshots[:half_rows], "col", down),
-        lax.ppermute(snapshots[half_rows:], "col", down),
-    ], axis=0)
+    next_first = lax.ppermute(snapshots[:half_rows], "col", down)
     tail_to_last = lax.ppermute(tail, flat, to_slot7)
     own_hist = jnp.where(slot == 0, tail_to_first, tail_prev)
     own_rows = jnp.concatenate([own_hist, snapshots], axis=0) * mask
     band0_part = lagged_partial(own_rows, own_rows)
-    hist_send, band0_part = lax.optimization_barrier((own_hist, band0_part))
-    hist_prev = lax.ppermute(hist_send, "col", up)
+    hist_prev = lax.ppermute(own_hist, "col", up)
+    second_send, band0_part = lax.optimization_barrier((snapshots[half_rows:], band0_part))
+    block_next = jnp.concatenate([next_first, lax.ppermute(second_send, "col", down)], axis=0)
     hist_next = jnp.where(slot == n_col - 1, tail_to_last, tail)
     block_next, _ = lax.optimization_barrier((block_next, band0_part))
 

time: 245 us -> 254 us (1.037)
  starting transfers between devices: 23.2 us -> 63.6 us
  waiting for transfers between devices: 141 us -> 110 us
    ppermute x3, starting transfers between devices: 4.62 us -> 44.2 us  [the longest x1 39.6 us: per_device(): lax.ppermute(second_send, 'col', down)]
    ppermute x3, waiting for transfers between devices: 36.4 us -> 8.14 us  [the longest x1 8.13 us: per_device(): hist_prev = lax.ppermute(own_hist, 'col', up)]
    ppermute x2, waiting for transfers between devices: 15.8 us -> 0.01 us  [space_sum(): return mine + lax.ppermute(theirs, 'space', swap)]
    ppermute x1, waiting for transfers between devices: 2.31 us -> 11.8 us  [per_device(): lax.ppermute(lax.dynamic_slice_in_dim(band2_next, other_col, column_width...]
    ppermute x1, waiting for transfers between devices: 23.4 us -> 29.2 us  [per_device(): head_prev = lax.ppermute(head, 'col', up)]
  transfers between devices with their start and end apart: 14 -> 14, of which waited for: 10 -> 7; matrix products, arithmetic and copies ran while one was open for 29% -> 27% of each run, Pallas kernels for 0% -> 0%
where the time goes in v12:
time: 254 us; the launch traced here: 250 us
  waiting for transfers between devices  110 us (43%)
  starting transfers between devices  63.6 us (25%)
  other arithmetic  36.7 us (14%)
  matrix products  20.8 us (8%)
  local copies, waits for them, and re-layouts  17.2 us (7%)
    ppermute x1, waiting for transfers between devices, per_device(): tail_prev = lax.ppermute(tail, 'col', up)  51.3 us
    ppermute x1, starting transfers between devices, per_device(): lax.ppermute(second_send, 'col', down)  39.6 us
    ppermute x1, waiting for transfers between devices, per_device(): head_prev = lax.ppermute(head, 'col', up)  29.2 us
    dot_general x4, matrix products, gram(): lax.dot_general(rows, cols, (((1,), (1,)), ((), ())), preferred_element_t...  15.3 us
    reduce_sum x5, other arithmetic, square_norms(): return jnp.sum(jnp.square(values.astype(jnp.float32)), axis=1)  12.3 us
    add x24, other arithmetic, lag_sum_rect(): doubled = doubled[width:width + r, width:width + c] + doubled[:r, :c]  12 us
    ppermute x1, waiting for transfers between devices, per_device(): lax.ppermute(lax.dynamic_slice_in_dim(band2_next, other_col, column_width...  11.8 us
    ppermute x1, waiting for transfers between devices, per_device(): hist_prev = lax.ppermute(own_hist, 'col', up)  8.13 us
  transfers between devices with their start and end apart: 14, of which 7 were waited for; matrix products, arithmetic and copies ran while one was open for 27% of the time, Pallas kernels for 0%

profile of v12, /device:TPU:4, one launch (start us, length us, event | category | flops | bytes accessed | tf_op | source)
XLA Modules:
  0.0 250.0 jit_solution(12310465466823991621)
XLA Ops:
  0.0 3.3 %slice.319 = bf16[239,4096]{1,0:T(8,128)(2,1)} slice(bf16[512,4096]{1,0:T(8,128)(2,1)} %param.3), slice={[273:512], [0:4096]} | slice | bytes 3915776 | tf_op jit(solution)/shard_map/slice | solution.py:95
  3.3 1.6 collective-permute-start.1
  4.9 1.3 collective-permute-start
  6.2 2.0 collective-permute-start.6
  8.1 3.3 %slice.340 = bf16[273,4096]{1,0:T(8,128)(2,1)} slice(bf16[512,4096]{1,0:T(8,128)(2,1)} %param.3), slice={[0:273], [0:4096]} | slice | bytes 4472832 | tf_op jit(solution)/shard_map/slice | solution.py:96
  11.4 2.2 collective-permute-start.4
  13.6 2.6 %fusion.23 = (bf16[256,4096]{1,0:T(8,128)(2,1)}, bf16[256,4096]{1,0:T(8,128)(2,1)}) fusion(bf16[512,4096]{1,0:T(8,128)(2,1)S(1)} %copy-done), kind=kLoop, calls=%fused_computation.101 | loop fusion | bytes 8388608 | tf_op jit(solution)/shard_map/slice | solution.py:107
  16.2 4.5 %collective-permute-start.7 = (bf16[256,4096]{1,0:T(8,128)(2,1)}, bf16[256,4096]{1,0:T(8,128)(2,1)}, u32[]{:S(2)}, u32[]{:S(2)}) collective-permute-start(bf16[256,4096]{1,0:T(8,128)(2,1)} %get-tuple-element.17), channel_id=1, source_target_pairs={{0,14},{2,0},{4,2},{6,4},{8,6},{10,8},{12,10},{14,12},{1,15},{3,1}... | collective-permute-start | bytes 6291464 | tf_op jit(solution)/shard_map/ppermute | solution.py:107
  21.4 51.3 %collective-permute-done.1 = bf16[239,4096]{1,0:T(8,128)(2,1)S(1)} collective-permute-done((bf16[239,4096]{1,0:T(8,128)(2,1)}, bf16[239,4096]{1,0:T(8,128)(2,1)S(1)}, u32[]{:S(2)}, u32[]{:S(2)}) %collective-permute-start.1) | collective-permute-done | bytes 1957920 | tf_op jit(solution)/shard_map/ppermute | solution.py:103
  72.7 1.8 broadcast_select_fusion.1
  74.6 3.1 %multiply_reduce_fusion.1 = f32[751]{0:T(1024)S(1)} fusion(bf16[4096]{0:T(1024)(128)(2,1)S(1)} %convert_element_type.20, bf16[512,4096]{1,0:T(8,128)(2,1)S(1)} %copy-done.1, bf16[239,4096]{1,0:T(8,128)(2,1)S(1)} %broadcast_select_fusion.1), kind=kLoop, calls=%fused_computation.1 | loop fusion | flops 24608016 | bytes 6163388 | tf_op jit(solution)/shard_map/reduce_sum | solution.py:35
  77.7 5.5 %multiply_subtract_fusion = f32[751,751]{0,1:T(8,128)S(1)} fusion(f32[751]{0:T(1024)S(1)} %multiply_reduce_fusion.1, bf16[512,4096]{1,0:T(8,128)(2,1)S(1)} %copy-done.1, bf16[239,4096]{1,0:T(8,128)(2,1)S(1)} %broadcast_select_fusion.1, bf16[4096]{0:T(1024)(128)(2,1)S(1)} %convert_element_type.20), kind=kOutput, calls=%fused_computation.11 | convolution fusion | flops 4640445440 | bytes 8419392 | tf_op jit(solution)/shard_map/dot_general | solution.py:39
  83.2 0.9 slice_add_fusion.1
  84.1 0.8 slice_add_fusion
  84.9 0.8 slice_add_fusion.2
  85.8 0.7 slice_add_fusion.3
  86.4 0.6 slice_add_fusion.4
  88.0 0.6 slice_add_fusion.5
  89.7 3.7 %collective-permute-start.2 = (f32[512,256]{0,1:T(8,128)S(1)}, f32[512,256]{0,1:T(8,128)S(1)}, u32[]{:S(2)}, u32[]{:S(2)}) collective-permute-start(f32[512,256]{0,1:T(8,128)S(1)} %constant_dynamic-slice_fusion), channel_id=1, source_target_pairs={{0,1},{1,0},{2,3},{3,2},{4,5},{5,4},{6,7},{7,6},{8,9},{9,8},{10,11... | collective-permute-start | bytes 1572872 | tf_op jit(solution)/shard_map/ppermute | solution.py:134
  93.4 39.6 %collective-permute-start.8 = (bf16[256,4096]{1,0:T(8,128)(2,1)S(1)}, bf16[256,4096]{1,0:T(8,128)(2,1)}, u32[]{:S(2)}, u32[]{:S(2)}) collective-permute-start(bf16[256,4096]{1,0:T(8,128)(2,1)S(1)} %copy-done.4), channel_id=1, source_target_pairs={{0,14},{2,0},{4,2},{6,4},{8,6},{10,8},{12,10},{14,12},{1,15},{3,1}... | collective-permute-start | bytes 6291464 | tf_op jit(solution)/shard_map/ppermute | solution.py:114
  133.0 0.5 broadcast_select_fusion
  133.5 29.2 %collective-permute-done.4 = bf16[273,4096]{1,0:T(8,128)(2,1)} collective-permute-done((bf16[273,4096]{1,0:T(8,128)(2,1)}, bf16[273,4096]{1,0:T(8,128)(2,1)}, u32[]{:S(2)}, u32[]{:S(2)}) %collective-permute-start.4) | collective-permute-done | bytes 2236448 | tf_op jit(solution)/shard_map/ppermute | solution.py:105
  162.8 3.5 %multiply_reduce_fusion.2 = f32[512]{0:T(512)S(1)} fusion(bf16[4096]{0:T(1024)(128)(2,1)S(1)} %convert_element_type.20, bf16[239,4096]{1,0:T(8,128)(2,1)S(1)} %collective-permute-done.1, bf16[273,4096]{1,0:T(8,128)(2,1)} %collective-permute-done.4), kind=kLoop, calls=%fused_computation.2 | loop fusion | flops 16776704 | bytes 4204544 | tf_op jit(solution)/shard_map/reduce_sum | solution.py:35
  166.3 5.5 %multiply_subtract_fusion.2 = f32[751,512]{0,1:T(8,128)S(1)} fusion(f32[512]{0:T(512)S(1)} %multiply_reduce_fusion.2, f32[751]{0:T(1024)S(1)} %multiply_reduce_fusion.1, bf16[239,4096]{1,0:T(8,128)(2,1)S(1)} %collective-permute-done.1, bf16[273,4096]{1,0:T(8,128)(2,1)} %collective-permute-done.4, bf16[4096]{0:T(1024)(128)(2,1)S(1)} %convert_element_type.20, ...), kind=kOutput, calls=%fused_computation.27 | convolution fusion | flops 3182115328 | bytes 11897788 | tf_op jit(solution)/shard_map/dot_general | solution.py:47
  171.8 0.6 slice_add_fusion.11
  172.4 0.6 slice_add_fusion.10
  173.0 0.6 slice_add_fusion.9
  176.2 8.1 %collective-permute-done.3 = bf16[239,4096]{1,0:T(8,128)(2,1)} collective-permute-done((bf16[239,4096]{1,0:T(8,128)(2,1)S(1)}, bf16[239,4096]{1,0:T(8,128)(2,1)}, u32[]{:S(2)}, u32[]{:S(2)}) %collective-permute-start.3) | collective-permute-done | bytes 1957920 | tf_op jit(solution)/shard_map/ppermute | solution.py:112
  184.3 2.3 multiply_reduce_fusion.4
  186.7 2.2 add_subtract_fusion.1
  190.4 0.6 slice_add_fusion.21
  193.3 3.7 %collective-permute-start.5 = (f32[512,256]{0,1:T(8,128)S(1)}, f32[512,256]{0,1:T(8,128)S(1)}, u32[]{:S(2)}, u32[]{:S(2)}) collective-permute-start(f32[512,256]{0,1:T(8,128)S(1)} %fusion.13), channel_id=1, source_target_pairs={{0,1},{1,0},{2,3},{3,2},{4,5},{5,4},{6,7},{7,6},{8,9},{9,8},{10,11... | collective-permute-start | bytes 1572872 | tf_op jit(solution)/shard_map/ppermute | solution.py:134
  197.5 2.5 pad_maximum_fusion
  200.0 2.9 %multiply_reduce_fusion = f32[751]{0:T(1024)S(1)} fusion(bf16[4096]{0:T(1024)(128)(2,1)S(1)} %convert_element_type.20, bf16[512,4096]{1,0:T(8,128)(2,1)S(1)} %pad_maximum_fusion, bf16[239,4096]{1,0:T(8,128)(2,1)S(1)} %broadcast_select_fusion), kind=kLoop, calls=%fused_computation | loop fusion | flops 24608016 | bytes 6163388 | tf_op jit(solution)/shard_map/reduce_sum | solution.py:35
  202.9 5.5 %multiply_subtract_fusion.1 = f32[751,512]{0,1:T(8,128)S(1)} fusion(f32[751]{0:T(1024)S(1)} %multiply_reduce_fusion, f32[512]{0:T(512)S(1)} %multiply_reduce_fusion.2, bf16[512,4096]{1,0:T(8,128)(2,1)S(1)} %pad_maximum_fusion, bf16[239,4096]{1,0:T(8,128)(2,1)S(1)} %broadcast_select_fusion, bf16[4096]{0:T(1024)(128)(2,1)S(1)} %convert_element_type.20, ...), kind=kOutput, calls=%fused_computation.26 | convolution fusion | flops 3182115328 | bytes 11897788 | tf_op jit(solution)/shard_map/dot_general | solution.py:47
  208.4 0.6 slice_add_fusion.8
  209.0 0.6 copy-done.2
  209.5 0.6 slice_add_fusion.7
  210.1 0.6 slice_add_fusion.6
  213.1 2.1 add_subtract_fusion
  217.7 0.6 slice_add_fusion.26
  219.7 0.7 fusion.8
  221.1 11.8 %collective-permute-done.10 = f32[512,256]{0,1:T(8,128)S(1)} collective-permute-done((f32[512,256]{0,1:T(8,128)S(1)}, f32[512,256]{0,1:T(8,128)S(1)}, u32[]{:S(2)}, u32[]{:S(2)}) %collective-permute-start.10) | collective-permute-done | bytes 524320 | tf_op jit(solution)/shard_map/ppermute | solution.py:153
  232.9 2.3 collective-permute-done.9
  235.4 4.8 %collective-permute-start.11 = (f32[512]{0:T(512)S(1)}, f32[512]{0:T(512)S(1)}, u32[]{:S(2)}, u32[]{:S(2)}) collective-permute-start(f32[512]{0:T(512)S(1)} %add.308), channel_id=1, source_target_pairs={{0,1},{1,0},{2,3},{3,2},{4,5},{5,4},{6,7},{7,6},{8,9},{9,8},{10,11... | collective-permute-start | bytes 6152 | tf_op jit(solution)/shard_map/ppermute | solution.py:162
  240.2 1.6 collective-permute-done.11
  242.0 5.9 %collective-permute-done.13 = f32[256]{0:T(256)S(1)} collective-permute-done((f32[256]{0:T(256)S(1)}, f32[256]{0:T(256)S(1)}, u32[]{:S(2)}, u32[]{:S(2)}) %collective-permute-start.13) | collective-permute-done | bytes 1056 | tf_op jit(solution)/shard_map/ppermute | solution.py:166
  248.2 1.6 copy.9
  (81 shorter events, 16.5 us)
Async XLA Ops:
  3.3 10.3 %copy-start = (bf16[512,4096]{1,0:T(8,128)(2,1)S(1)}, bf16[512,4096]{1,0:T(8,128)(2,1)}, u32[]{:S(2)}) copy-start(bf16[512,4096]{1,0:T(8,128)(2,1)} %param.3) | copy-start | bytes 12582916
  3.3 69.4 %collective-permute-start.1 = (bf16[239,4096]{1,0:T(8,128)(2,1)}, bf16[239,4096]{1,0:T(8,128)(2,1)S(1)}, u32[]{:S(2)}, u32[]{:S(2)}) collective-permute-start(bf16[239,4096]{1,0:T(8,128)(2,1)} %slice.319), channel_id=1, source_target_pairs={{0,2},{2,4},{4,6},{6,8},{8,10},{10,12},{12,14},{14,0},{1,3},{3,5},... | collective-permute-start | bytes 5873672 | tf_op jit(solution)/shard_map/ppermute | solution.py:103
  4.9 67.8 %collective-permute-start = (bf16[239,4096]{1,0:T(8,128)(2,1)}, bf16[239,4096]{1,0:T(8,128)(2,1)}, u32[]{:S(2)}, u32[]{:S(2)}) collective-permute-start(bf16[239,4096]{1,0:T(8,128)(2,1)} %slice.319), channel_id=1, source_target_pairs={{14,16},{30,32},{46,48},{62,64},{78,80},{94,96},{110,112},{15,17},... | collective-permute-start | bytes 5873672 | tf_op jit(solution)/shard_map/ppermute | solution.py:104
  6.2 87.3 %collective-permute-start.6 = (bf16[239,4096]{1,0:T(8,128)(2,1)}, bf16[239,4096]{1,0:T(8,128)(2,1)}, u32[]{:S(2)}, u32[]{:S(2)}) collective-permute-start(bf16[239,4096]{1,0:T(8,128)(2,1)} %slice.319), channel_id=1, source_target_pairs={{14,30},{30,46},{46,62},{62,78},{78,94},{94,110},{110,126},{15,31}... | collective-permute-start | bytes 5873672 | tf_op jit(solution)/shard_map/ppermute | solution.py:108
  11.4 9.9 %copy-start.5 = (s32[4096]{0:T(1024)S(1)}, s32[4096]{0:T(1024)}, u32[]{:S(2)}) copy-start(s32[4096]{0:T(1024)} %param.4) | copy-start | bytes 49156
  11.4 151.4 %collective-permute-start.4 = (bf16[273,4096]{1,0:T(8,128)(2,1)}, bf16[273,4096]{1,0:T(8,128)(2,1)}, u32[]{:S(2)}, u32[]{:S(2)}) collective-permute-start(bf16[273,4096]{1,0:T(8,128)(2,1)} %slice.340), channel_id=1, source_target_pairs={{0,2},{2,4},{4,6},{6,8},{8,10},{10,12},{12,14},{14,0},{1,3},{3,5},... | collective-permute-start | bytes 6709256 | tf_op jit(solution)/shard_map/ppermute | solution.py:105
  16.2 181.3 %collective-permute-start.7 = (bf16[256,4096]{1,0:T(8,128)(2,1)}, bf16[256,4096]{1,0:T(8,128)(2,1)}, u32[]{:S(2)}, u32[]{:S(2)}) collective-permute-start(bf16[256,4096]{1,0:T(8,128)(2,1)} %get-tuple-element.17), channel_id=1, source_target_pairs={{0,14},{2,0},{4,2},{6,4},{8,6},{10,8},{12,10},{14,12},{1,15},{3,1}... | collective-permute-start | bytes 6291464 | tf_op jit(solution)/shard_map/ppermute | solution.py:107
  21.4 53.2 %copy-start.1 = (bf16[512,4096]{1,0:T(8,128)(2,1)S(1)}, bf16[512,4096]{1,0:T(8,128)(2,1)}, u32[]{:S(2)}) copy-start(bf16[512,4096]{1,0:T(8,128)(2,1)} %param.3) | copy-start | bytes 12582916
  74.5 109.9 %collective-permute-start.3 = (bf16[239,4096]{1,0:T(8,128)(2,1)S(1)}, bf16[239,4096]{1,0:T(8,128)(2,1)}, u32[]{:S(2)}, u32[]{:S(2)}) collective-permute-start(bf16[239,4096]{1,0:T(8,128)(2,1)S(1)} %broadcast_select_fusion.1), channel_id=1, source_target_pairs={{0,2},{2,4},{4,6},{6,8},{8,10},{10,12},{12,14},{14,0},{1,3},{3,5},... | collective-permute-start | bytes 5873672 | tf_op jit(solution)/shard_map/ppermute | solution.py:112
  89.3 4.1 %copy-start.4 = (bf16[256,4096]{1,0:T(8,128)(2,1)S(1)}, bf16[256,4096]{1,0:T(8,128)(2,1)}, u32[]{:S(2)}) copy-start(bf16[256,4096]{1,0:T(8,128)(2,1)} %get-tuple-element.10) | copy-start | bytes 6291460
  89.7 130.8 %collective-permute-start.2 = (f32[512,256]{0,1:T(8,128)S(1)}, f32[512,256]{0,1:T(8,128)S(1)}, u32[]{:S(2)}, u32[]{:S(2)}) collective-permute-start(f32[512,256]{0,1:T(8,128)S(1)} %constant_dynamic-slice_fusion), channel_id=1, source_target_pairs={{0,1},{1,0},{2,3},{3,2},{4,5},{5,4},{6,7},{7,6},{8,9},{9,8},{10,11... | collective-permute-start | bytes 1572872 | tf_op jit(solution)/shard_map/ppermute | solution.py:134
  93.4 104.0 %collective-permute-start.8 = (bf16[256,4096]{1,0:T(8,128)(2,1)S(1)}, bf16[256,4096]{1,0:T(8,128)(2,1)}, u32[]{:S(2)}, u32[]{:S(2)}) collective-permute-start(bf16[256,4096]{1,0:T(8,128)(2,1)S(1)} %copy-done.4), channel_id=1, source_target_pairs={{0,14},{2,0},{4,2},{6,4},{8,6},{10,8},{12,10},{14,12},{1,15},{3,1}... | collective-permute-start | bytes 6291464 | tf_op jit(solution)/shard_map/ppermute | solution.py:114
  171.8 1.1 copy-start.3
  186.7 2.2 slice-start.1
  193.3 27.3 %collective-permute-start.5 = (f32[512,256]{0,1:T(8,128)S(1)}, f32[512,256]{0,1:T(8,128)S(1)}, u32[]{:S(2)}, u32[]{:S(2)}) collective-permute-start(f32[512,256]{0,1:T(8,128)S(1)} %fusion.13), channel_id=1, source_target_pairs={{0,1},{1,0},{2,3},{3,2},{4,5},{5,4},{6,7},{7,6},{8,9},{9,8},{10,11... | collective-permute-start | bytes 1572872 | tf_op jit(solution)/shard_map/ppermute | solution.py:134
  208.4 1.1 copy-start.2
  213.1 2.2 slice-start
  220.3 12.6 %collective-permute-start.10 = (f32[512,256]{0,1:T(8,128)S(1)}, f32[512,256]{0,1:T(8,128)S(1)}, u32[]{:S(2)}, u32[]{:S(2)}) collective-permute-start(f32[512,256]{0,1:T(8,128)S(1)} %get-tuple-element.29), channel_id=1, source_target_pairs={{0,3},{1,2},{2,5},{3,4},{4,7},{5,6},{6,9},{7,8},{8,11},{9,10},{10,... | collective-permute-start | bytes 1572872 | tf_op jit(solution)/shard_map/ppermute | solution.py:153
  220.4 14.8 %collective-permute-start.9 = (f32[512,256]{0,1:T(8,128)S(1)}, f32[512,256]{0,1:T(8,128)S(1)}, u32[]{:S(2)}, u32[]{:S(2)}) collective-permute-start(f32[512,256]{0,1:T(8,128)S(1)} %get-tuple-element.30), channel_id=1, source_target_pairs={{0,2},{1,3},{2,4},{3,5},{4,6},{5,7},{6,8},{7,9},{8,10},{9,11},{10,... | collective-permute-start | bytes 1572872 | tf_op jit(solution)/shard_map/ppermute | solution.py:152
  235.4 6.4 %collective-permute-start.11 = (f32[512]{0:T(512)S(1)}, f32[512]{0:T(512)S(1)}, u32[]{:S(2)}, u32[]{:S(2)}) collective-permute-start(f32[512]{0:T(512)S(1)} %add.308), channel_id=1, source_target_pairs={{0,1},{1,0},{2,3},{3,2},{4,5},{5,4},{6,7},{7,6},{8,9},{9,8},{10,11... | collective-permute-start | bytes 6152 | tf_op jit(solution)/shard_map/ppermute | solution.py:162
  241.9 6.0 %collective-permute-start.13 = (f32[256]{0:T(256)S(1)}, f32[256]{0:T(256)S(1)}, u32[]{:S(2)}, u32[]{:S(2)}) collective-permute-start(f32[256]{0:T(256)S(1)} %dynamic_slice.27), channel_id=1, source_target_pairs={{0,4},{2,6},{4,8},{6,10},{8,12},{10,14},{12,0},{14,2},{1,5},{3,7},... | collective-permute-start | bytes 3080 | tf_op jit(solution)/shard_map/ppermute | solution.py:166
  241.9 6.0 %collective-permute-start.12 = (f32[256]{0:T(256)S(1)}, f32[256]{0:T(256)S(1)}, u32[]{:S(2)}, u32[]{:S(2)}) collective-permute-start(f32[256]{0:T(256)S(1)} %dynamic_slice.27), channel_id=1, source_target_pairs={{0,2},{2,4},{4,6},{6,8},{8,10},{10,12},{12,14},{14,0},{1,3},{3,5},... | collective-permute-start | bytes 3080 | tf_op jit(solution)/shard_map/ppermute | solution.py:166

commit v13 on v11

--- a/solution.py
+++ b/solution.py
@@ -110,8 +110,14 @@
     ], axis=0)
     tail_to_last = lax.ppermute(tail, flat, to_slot7)
     own_hist = jnp.where(slot == 0, tail_to_first, tail_prev)
-    own_rows = jnp.concatenate([own_hist, snapshots], axis=0) * mask
-    band0_part = lagged_partial(own_rows, own_rows)
+    own_block = snapshots * mask
+    own_hist_m = own_hist * mask
+    own_rows = jnp.concatenate([own_hist_m, own_block], axis=0)
+    block_gram = gram(own_block, own_block)
+    hist_gram = gram(own_hist_m, own_rows)
+    gram0 = jnp.concatenate([hist_gram, jnp.concatenate([hist_gram[:, hist:].T, block_gram], axis=1)], axis=0)
+    row_sq0 = square_norms(own_rows)
+    band0_part = lag_sum(row_sq0[:, None] + row_sq0[None, :] - 2.0 * gram0, LAG)
     hist_send, band0_part = lax.optimization_barrier((own_hist, band0_part))
     hist_prev = lax.ppermute(hist_send, "col", up)
     hist_next = jnp.where(slot == n_col - 1, tail_to_last, tail)

time: 245 us -> 246 us (level)
  other arithmetic: 36.9 us -> 43.1 us
  waiting for transfers between devices: 141 us -> 135 us
    ppermute x1, waiting for transfers between devices: 51.3 us -> 45.4 us  [per_device(): tail_prev = lax.ppermute(tail, 'col', up)]
    mul x0 -> x2, other arithmetic: none -> 5.61 us  [the longest x1 3.14 us: per_device(): own_hist_m = own_hist * mask]
    dot_general x1 -> x0, matrix products: 5.52 us -> none  [lagged_partial(): lax.dot_general(rows, cols, (((1,), (1,)), ((), ())), preferred_element_t...]
    dot_general x4 -> x6, matrix products: 15.3 us -> 19.7 us  [gram(): lax.dot_general(rows, cols, (((1,), (1,)), ((), ())), preferred_element_t...]
  transfers between devices with their start and end apart: 14 -> 14, of which waited for: 10 -> 10; matrix products, arithmetic and copies ran while one was open for 29% -> 31% of each run, Pallas kernels for 0% -> 0%
where the time goes in v13:
time: 246 us; the launch traced here: 242 us
  waiting for transfers between devices  135 us (55%)
  other arithmetic  43.1 us (18%)
  starting transfers between devices  24.2 us (10%)
  matrix products  19.7 us (8%)
  local copies, waits for them, and re-layouts  18.5 us (8%)
    ppermute x1, waiting for transfers between devices, per_device(): tail_prev = lax.ppermute(tail, 'col', up)  45.4 us
    ppermute x1, waiting for transfers between devices, per_device(): head_prev = lax.ppermute(head, 'col', up)  22.8 us
    ppermute x1, waiting for transfers between devices, per_device(): lax.ppermute(snapshots[half_rows:], 'col', down)  22.5 us
    dot_general x6, matrix products, gram(): lax.dot_general(rows, cols, (((1,), (1,)), ((), ())), preferred_element_t...  19.7 us
    ppermute x2, waiting for transfers between devices, space_sum(): return mine + lax.ppermute(theirs, 'space', swap)  16.4 us
    ppermute x1, waiting for transfers between devices, per_device(): hist_prev = lax.ppermute(hist_send, 'col', up)  13.9 us
    add x24, other arithmetic, lag_sum_rect(): doubled = doubled[width:width + r, width:width + c] + doubled[:r, :c]  11.9 us
    reduce_sum x5, other arithmetic, square_norms(): return jnp.sum(jnp.square(values.astype(jnp.float32)), axis=1)  11.5 us
  transfers between devices with their start and end apart: 14, of which 10 were waited for; matrix products, arithmetic and copies ran while one was open for 31% of the time, Pallas kernels for 0%

profile of v13, /device:TPU:4, one launch (start us, length us, event | category | flops | bytes accessed | tf_op | source)
XLA Modules:
  0.0 241.6 jit_solution(18200718461272070051)
XLA Ops:
  0.0 3.3 %slice.321 = bf16[239,4096]{1,0:T(8,128)(2,1)} slice(bf16[512,4096]{1,0:T(8,128)(2,1)} %param.3), slice={[273:512], [0:4096]} | slice | bytes 3915776 | tf_op jit(solution)/shard_map/slice | solution.py:95
  3.3 1.6 collective-permute-start.1
  4.9 1.3 collective-permute-start
  6.2 1.9 collective-permute-start.6
  8.1 3.4 %slice.343 = bf16[273,4096]{1,0:T(8,128)(2,1)} slice(bf16[512,4096]{1,0:T(8,128)(2,1)} %param.3), slice={[0:273], [0:4096]} | slice | bytes 4472832 | tf_op jit(solution)/shard_map/slice | solution.py:96
  11.5 2.2 collective-permute-start.4
  13.7 2.5 %fusion.27 = (bf16[256,4096]{1,0:T(8,128)(2,1)}, bf16[256,4096]{1,0:T(8,128)(2,1)}) fusion(bf16[512,4096]{1,0:T(8,128)(2,1)S(1)} %copy-done), kind=kLoop, calls=%fused_computation.108 | loop fusion | bytes 8388608 | tf_op jit(solution)/shard_map/slice | solution.py:108
  16.3 4.5 %collective-permute-start.7 = (bf16[256,4096]{1,0:T(8,128)(2,1)}, bf16[256,4096]{1,0:T(8,128)(2,1)}, u32[]{:S(2)}, u32[]{:S(2)}) collective-permute-start(bf16[256,4096]{1,0:T(8,128)(2,1)} %get-tuple-element.19), channel_id=1, source_target_pairs={{0,14},{2,0},{4,2},{6,4},{8,6},{10,8},{12,10},{14,12},{1,15},{3,1}... | collective-permute-start | bytes 6291464 | tf_op jit(solution)/shard_map/ppermute | solution.py:108
  21.5 2.5 %broadcast_multiply_fusion = bf16[512,4096]{1,0:T(8,128)(2,1)S(1)} fusion(bf16[512,4096]{1,0:T(8,128)(2,1)} %param.3, bf16[4096]{0:T(1024)(128)(2,1)S(1)} %convert_element_type.19), kind=kLoop, calls=%fused_computation.17 | loop fusion | flops 2097152 | bytes 8396800 | tf_op jit(solution)/shard_map/mul | solution.py:113
  23.9 3.3 %fusion.33 = f32[512,512]{0,1:T(8,128)} fusion(bf16[512,4096]{1,0:T(8,128)(2,1)S(1)} %broadcast_multiply_fusion), kind=kOutput, calls=%fused_computation.114 | convolution fusion | flops 2147483648 | bytes 5242880 | tf_op jit(solution)/shard_map/dot_general | solution.py:47
  27.3 45.4 %collective-permute-done.1 = bf16[239,4096]{1,0:T(8,128)(2,1)S(1)} collective-permute-done((bf16[239,4096]{1,0:T(8,128)(2,1)}, bf16[239,4096]{1,0:T(8,128)(2,1)S(1)}, u32[]{:S(2)}, u32[]{:S(2)}) %collective-permute-start.1) | collective-permute-done | bytes 1957920 | tf_op jit(solution)/shard_map/ppermute | solution.py:103
  72.9 3.1 %broadcast_multiply_fusion.2 = (bf16[239,4096]{1,0:T(8,128)(2,1)S(1)}, bf16[239,4096]{1,0:T(8,128)(2,1)}) fusion(bf16[4096]{0:T(1024)(128)(2,1)S(1)} %convert_element_type.19, bf16[239,4096]{1,0:T(8,128)(2,1)} %collective-permute-done, bf16[239,4096]{1,0:T(8,128)(2,1)S(1)} %collective-permute-done.1, pred[]{:T(512)S(6)} %eq.6), kind=kLoop, calls=%fused_computation.69 | loop fusion | flops 1957888 | bytes 7839745 | tf_op jit(solution)/shard_map/mul | solution.py:114
  76.0 2.3 multiply_reduce_fusion.1
  78.3 1.8 fusion.7
  80.5 2.0 fusion
  82.6 0.8 slice_add_fusion.1
  83.5 0.8 slice_add_fusion
  84.3 0.8 slice_add_fusion.2
  85.2 0.7 slice_add_fusion.3
  86.3 0.6 slice_add_fusion.4
  87.4 0.6 slice_add_fusion.5
  89.0 1.2 copy-done.7
  90.7 3.8 %collective-permute-start.2 = (f32[512,256]{0,1:T(8,128)S(1)}, f32[512,256]{0,1:T(8,128)S(1)}, u32[]{:S(2)}, u32[]{:S(2)}) collective-permute-start(f32[512,256]{0,1:T(8,128)S(1)} %constant_dynamic-slice_fusion), channel_id=1, source_target_pairs={{0,1},{1,0},{2,3},{3,2},{4,5},{5,4},{6,7},{7,6},{8,9},{9,8},{10,11... | collective-permute-start | bytes 1572872 | tf_op jit(solution)/shard_map/ppermute | solution.py:142
  94.5 2.1 broadcast_select_fusion
  96.6 22.5 %collective-permute-done.8 = bf16[256,4096]{1,0:T(8,128)(2,1)} collective-permute-done((bf16[256,4096]{1,0:T(8,128)(2,1)}, bf16[256,4096]{1,0:T(8,128)(2,1)}, u32[]{:S(2)}, u32[]{:S(2)}) %collective-permute-start.8) | collective-permute-done | bytes 2097184 | tf_op jit(solution)/shard_map/ppermute | solution.py:109
  119.1 2.5 %pad_maximum_fusion.1 = bf16[512,4096]{1,0:T(8,128)(2,1)S(1)} fusion(bf16[256,4096]{1,0:T(8,128)(2,1)} %collective-permute-done.8, bf16[256,4096]{1,0:T(8,128)(2,1)} %collective-permute-done.7), kind=kLoop, calls=%fused_computation.6 | loop fusion | flops 8388608 | bytes 8388608 | tf_op jit(solution)/shard_map/concatenate | solution.py:107
  121.6 2.9 %multiply_reduce_fusion = f32[751]{0:T(1024)S(1)} fusion(bf16[4096]{0:T(1024)(128)(2,1)S(1)} %convert_element_type.19, bf16[512,4096]{1,0:T(8,128)(2,1)S(1)} %pad_maximum_fusion.1, bf16[239,4096]{1,0:T(8,128)(2,1)S(1)} %broadcast_select_fusion), kind=kLoop, calls=%fused_computation | loop fusion | flops 24608016 | bytes 6163388 | tf_op jit(solution)/shard_map/reduce_sum | solution.py:35
  124.5 22.8 %collective-permute-done.4 = bf16[273,4096]{1,0:T(8,128)(2,1)} collective-permute-done((bf16[273,4096]{1,0:T(8,128)(2,1)}, bf16[273,4096]{1,0:T(8,128)(2,1)}, u32[]{:S(2)}, u32[]{:S(2)}) %collective-permute-start.4) | collective-permute-done | bytes 2236448 | tf_op jit(solution)/shard_map/ppermute | solution.py:105
  147.3 3.5 %multiply_reduce_fusion.2 = f32[512]{0:T(512)S(1)} fusion(bf16[4096]{0:T(1024)(128)(2,1)S(1)} %convert_element_type.19, bf16[239,4096]{1,0:T(8,128)(2,1)S(1)} %collective-permute-done.1, bf16[273,4096]{1,0:T(8,128)(2,1)} %collective-permute-done.4), kind=kLoop, calls=%fused_computation.2 | loop fusion | flops 16776704 | bytes 4204544 | tf_op jit(solution)/shard_map/reduce_sum | solution.py:35
  150.8 5.2 %multiply_subtract_fusion.1 = f32[751,512]{0,1:T(8,128)S(1)} fusion(f32[512]{0:T(512)S(1)} %multiply_reduce_fusion.2, f32[751]{0:T(1024)S(1)} %multiply_reduce_fusion.1, bf16[512,4096]{1,0:T(8,128)(2,1)S(1)} %copy-done.2, bf16[239,4096]{1,0:T(8,128)(2,1)S(1)} %copy-done.6, bf16[239,4096]{1,0:T(8,128)(2,1)S(1)} %collective-permute-done.1, ...), kind=kOutput, calls=%fused_computation.29 | convolution fusion | flops 3175963136 | bytes 11897788 | tf_op jit(solution)/shard_map/dot_general | solution.py:47
  156.6 0.6 slice_add_fusion.10
  158.7 5.5 %multiply_subtract_fusion = f32[751,512]{0,1:T(8,128)S(1)} fusion(f32[751]{0:T(1024)S(1)} %multiply_reduce_fusion, f32[512]{0:T(512)S(1)} %multiply_reduce_fusion.2, bf16[512,4096]{1,0:T(8,128)(2,1)S(1)} %pad_maximum_fusion.1, bf16[239,4096]{1,0:T(8,128)(2,1)S(1)} %broadcast_select_fusion, bf16[4096]{0:T(1024)(128)(2,1)S(1)} %convert_element_type.19, ...), kind=kOutput, calls=%fused_computation.28 | convolution fusion | flops 3182115328 | bytes 11897788 | tf_op jit(solution)/shard_map/dot_general | solution.py:47
  164.7 0.6 slice_add_fusion.7
  165.3 0.6 slice_add_fusion.6
  170.4 13.9 %collective-permute-done.3 = bf16[239,4096]{1,0:T(8,128)(2,1)} collective-permute-done((bf16[239,4096]{1,0:T(8,128)(2,1)S(1)}, bf16[239,4096]{1,0:T(8,128)(2,1)}, u32[]{:S(2)}, u32[]{:S(2)}) %collective-permute-start.3) | collective-permute-done | bytes 1957920 | tf_op jit(solution)/shard_map/ppermute | solution.py:122
  184.3 2.3 multiply_reduce_fusion.4
  186.7 1.8 add_subtract_fusion.1
  192.8 2.0 add_subtract_fusion
  195.4 0.7 slice_add_fusion.16
  199.3 3.7 %collective-permute-start.5 = (f32[512,256]{0,1:T(8,128)S(1)}, f32[512,256]{0,1:T(8,128)S(1)}, u32[]{:S(2)}, u32[]{:S(2)}) collective-permute-start(f32[512,256]{0,1:T(8,128)S(1)} %fusion.15), channel_id=1, source_target_pairs={{0,1},{1,0},{2,3},{3,2},{4,5},{5,4},{6,7},{7,6},{8,9},{9,8},{10,11... | collective-permute-start | bytes 1572872 | tf_op jit(solution)/shard_map/ppermute | solution.py:142
  203.2 0.6 fusion.10
  204.1 16.3 %collective-permute-done.5 = f32[512,256]{0,1:T(8,128)S(1)} collective-permute-done((f32[512,256]{0,1:T(8,128)S(1)}, f32[512,256]{0,1:T(8,128)S(1)}, u32[]{:S(2)}, u32[]{:S(2)}) %collective-permute-start.5) | collective-permute-done | bytes 524320 | tf_op jit(solution)/shard_map/ppermute | solution.py:142
  221.0 2.4 %collective-permute-done.10 = f32[512,256]{0,1:T(8,128)S(1)} collective-permute-done((f32[512,256]{0,1:T(8,128)S(1)}, f32[512,256]{0,1:T(8,128)S(1)}, u32[]{:S(2)}, u32[]{:S(2)}) %collective-permute-start.10) | collective-permute-done | bytes 524320 | tf_op jit(solution)/shard_map/ppermute | solution.py:161
  223.4 3.8 %collective-permute-done.9 = f32[512,256]{0,1:T(8,128)S(1)} collective-permute-done((f32[512,256]{0,1:T(8,128)S(1)}, f32[512,256]{0,1:T(8,128)S(1)}, u32[]{:S(2)}, u32[]{:S(2)}) %collective-permute-start.9) | collective-permute-done | bytes 524320 | tf_op jit(solution)/shard_map/ppermute | solution.py:160
  227.4 4.3 %collective-permute-start.11 = (f32[512]{0:T(512)S(1)}, f32[512]{0:T(512)S(1)}, u32[]{:S(2)}, u32[]{:S(2)}) collective-permute-start(f32[512]{0:T(512)S(1)} %add.308), channel_id=1, source_target_pairs={{0,1},{1,0},{2,3},{3,2},{4,5},{5,4},{6,7},{7,6},{8,9},{9,8},{10,11... | collective-permute-start | bytes 6152 | tf_op jit(solution)/shard_map/ppermute | solution.py:170
  231.7 1.6 collective-permute-done.11
  233.5 5.6 %collective-permute-done.12 = f32[256]{0:T(256)S(1)} collective-permute-done((f32[256]{0:T(256)S(1)}, f32[256]{0:T(256)S(1)}, u32[]{:S(2)}, u32[]{:S(2)}) %collective-permute-start.12) | collective-permute-done | bytes 1056 | tf_op jit(solution)/shard_map/ppermute | solution.py:174
  239.7 1.6 copy.7
  (92 shorter events, 20.0 us)
Async XLA Ops:
  3.3 10.4 %copy-start = (bf16[512,4096]{1,0:T(8,128)(2,1)S(1)}, bf16[512,4096]{1,0:T(8,128)(2,1)}, u32[]{:S(2)}) copy-start(bf16[512,4096]{1,0:T(8,128)(2,1)} %param.3) | copy-start | bytes 12582916
  3.3 69.4 %collective-permute-start.1 = (bf16[239,4096]{1,0:T(8,128)(2,1)}, bf16[239,4096]{1,0:T(8,128)(2,1)S(1)}, u32[]{:S(2)}, u32[]{:S(2)}) collective-permute-start(bf16[239,4096]{1,0:T(8,128)(2,1)} %slice.321), channel_id=1, source_target_pairs={{0,2},{2,4},{4,6},{6,8},{8,10},{10,12},{12,14},{14,0},{1,3},{3,5},... | collective-permute-start | bytes 5873672 | tf_op jit(solution)/shard_map/ppermute | solution.py:103
  4.9 68.0 %collective-permute-start = (bf16[239,4096]{1,0:T(8,128)(2,1)}, bf16[239,4096]{1,0:T(8,128)(2,1)}, u32[]{:S(2)}, u32[]{:S(2)}) collective-permute-start(bf16[239,4096]{1,0:T(8,128)(2,1)} %slice.321), channel_id=1, source_target_pairs={{14,16},{30,32},{46,48},{62,64},{78,80},{94,96},{110,112},{15,17},... | collective-permute-start | bytes 5873672 | tf_op jit(solution)/shard_map/ppermute | solution.py:104
  6.2 84.5 %collective-permute-start.6 = (bf16[239,4096]{1,0:T(8,128)(2,1)}, bf16[239,4096]{1,0:T(8,128)(2,1)}, u32[]{:S(2)}, u32[]{:S(2)}) collective-permute-start(bf16[239,4096]{1,0:T(8,128)(2,1)} %slice.321), channel_id=1, source_target_pairs={{14,30},{30,46},{46,62},{62,78},{78,94},{94,110},{110,126},{15,31}... | collective-permute-start | bytes 5873672 | tf_op jit(solution)/shard_map/ppermute | solution.py:111
  11.5 9.3 %copy-start.8 = (s32[4096]{0:T(1024)S(1)}, s32[4096]{0:T(1024)}, u32[]{:S(2)}) copy-start(s32[4096]{0:T(1024)} %param.4) | copy-start | bytes 49156
  11.5 135.8 %collective-permute-start.4 = (bf16[273,4096]{1,0:T(8,128)(2,1)}, bf16[273,4096]{1,0:T(8,128)(2,1)}, u32[]{:S(2)}, u32[]{:S(2)}) collective-permute-start(bf16[273,4096]{1,0:T(8,128)(2,1)} %slice.343), channel_id=1, source_target_pairs={{0,2},{2,4},{4,6},{6,8},{8,10},{10,12},{12,14},{14,0},{1,3},{3,5},... | collective-permute-start | bytes 6709256 | tf_op jit(solution)/shard_map/ppermute | solution.py:105
  16.3 80.3 %collective-permute-start.7 = (bf16[256,4096]{1,0:T(8,128)(2,1)}, bf16[256,4096]{1,0:T(8,128)(2,1)}, u32[]{:S(2)}, u32[]{:S(2)}) collective-permute-start(bf16[256,4096]{1,0:T(8,128)(2,1)} %get-tuple-element.19), channel_id=1, source_target_pairs={{0,14},{2,0},{4,2},{6,4},{8,6},{10,8},{12,10},{14,12},{1,15},{3,1}... | collective-permute-start | bytes 6291464 | tf_op jit(solution)/shard_map/ppermute | solution.py:108
  23.9 54.3 %copy-start.1 = (bf16[512,4096]{1,0:T(8,128)(2,1)}, bf16[512,4096]{1,0:T(8,128)(2,1)S(1)}, u32[]{:S(2)}) copy-start(bf16[512,4096]{1,0:T(8,128)(2,1)S(1)} %broadcast_multiply_fusion) | copy-start | bytes 12582916
  72.7 46.4 %collective-permute-start.8 = (bf16[256,4096]{1,0:T(8,128)(2,1)}, bf16[256,4096]{1,0:T(8,128)(2,1)}, u32[]{:S(2)}, u32[]{:S(2)}) collective-permute-start(bf16[256,4096]{1,0:T(8,128)(2,1)} %get-tuple-element.20), channel_id=1, source_target_pairs={{0,14},{2,0},{4,2},{6,4},{8,6},{10,8},{12,10},{14,12},{1,15},{3,1}... | collective-permute-start | bytes 6291464 | tf_op jit(solution)/shard_map/ppermute | solution.py:109
  76.0 2.3 copy-start.5
  88.7 1.5 copy-start.7
  90.2 94.1 %collective-permute-start.3 = (bf16[239,4096]{1,0:T(8,128)(2,1)S(1)}, bf16[239,4096]{1,0:T(8,128)(2,1)}, u32[]{:S(2)}, u32[]{:S(2)}) collective-permute-start(bf16[239,4096]{1,0:T(8,128)(2,1)S(1)} %copy-done.7), channel_id=1, source_target_pairs={{0,2},{2,4},{4,6},{6,8},{8,10},{10,12},{12,14},{14,0},{1,3},{3,5},... | collective-permute-start | bytes 5873672 | tf_op jit(solution)/shard_map/ppermute | solution.py:122
  90.7 113.3 %collective-permute-start.2 = (f32[512,256]{0,1:T(8,128)S(1)}, f32[512,256]{0,1:T(8,128)S(1)}, u32[]{:S(2)}, u32[]{:S(2)}) collective-permute-start(f32[512,256]{0,1:T(8,128)S(1)} %constant_dynamic-slice_fusion), channel_id=1, source_target_pairs={{0,1},{1,0},{2,3},{3,2},{4,5},{5,4},{6,7},{7,6},{8,9},{9,8},{10,11... | collective-permute-start | bytes 1572872 | tf_op jit(solution)/shard_map/ppermute | solution.py:142
  121.5 29.2 %copy-start.6 = (bf16[239,4096]{1,0:T(8,128)(2,1)S(1)}, bf16[239,4096]{1,0:T(8,128)(2,1)}, u32[]{:S(2)}) copy-start(bf16[239,4096]{1,0:T(8,128)(2,1)} %copy-done.5) | copy-start | bytes 5873668
  124.5 26.3 %copy-start.2 = (bf16[512,4096]{1,0:T(8,128)(2,1)S(1)}, bf16[512,4096]{1,0:T(8,128)(2,1)}, u32[]{:S(2)}) copy-start(bf16[512,4096]{1,0:T(8,128)(2,1)} %copy-done.1) | copy-start | bytes 12582916
  156.0 10.8 %copy-start.3 = (f32[751,512]{0,1:T(8,128)}, f32[751,512]{0,1:T(8,128)S(1)}, u32[]{:S(2)}) copy-start(f32[751,512]{0,1:T(8,128)S(1)} %multiply_subtract_fusion.1) | copy-start | bytes 4614148
  164.1 3.5 %copy-start.4 = (f32[751,512]{0,1:T(8,128)}, f32[751,512]{0,1:T(8,128)S(1)}, u32[]{:S(2)}) copy-start(f32[751,512]{0,1:T(8,128)S(1)} %multiply_subtract_fusion) | copy-start | bytes 4614148
  186.7 1.8 slice-start
  192.8 2.1 slice-start.1
  199.3 21.1 %collective-permute-start.5 = (f32[512,256]{0,1:T(8,128)S(1)}, f32[512,256]{0,1:T(8,128)S(1)}, u32[]{:S(2)}, u32[]{:S(2)}) collective-permute-start(f32[512,256]{0,1:T(8,128)S(1)} %fusion.15), channel_id=1, source_target_pairs={{0,1},{1,0},{2,3},{3,2},{4,5},{5,4},{6,7},{7,6},{8,9},{9,8},{10,11... | collective-permute-start | bytes 1572872 | tf_op jit(solution)/shard_map/ppermute | solution.py:142
  203.8 19.6 %collective-permute-start.10 = (f32[512,256]{0,1:T(8,128)S(1)}, f32[512,256]{0,1:T(8,128)S(1)}, u32[]{:S(2)}, u32[]{:S(2)}) collective-permute-start(f32[512,256]{0,1:T(8,128)S(1)} %get-tuple-element.31), channel_id=1, source_target_pairs={{0,3},{1,2},{2,5},{3,4},{4,7},{5,6},{6,9},{7,8},{8,11},{9,10},{10,... | collective-permute-start | bytes 1572872 | tf_op jit(solution)/shard_map/ppermute | solution.py:161
  203.9 23.3 %collective-permute-start.9 = (f32[512,256]{0,1:T(8,128)S(1)}, f32[512,256]{0,1:T(8,128)S(1)}, u32[]{:S(2)}, u32[]{:S(2)}) collective-permute-start(f32[512,256]{0,1:T(8,128)S(1)} %get-tuple-element.32), channel_id=1, source_target_pairs={{0,2},{1,3},{2,4},{3,5},{4,6},{5,7},{6,8},{7,9},{8,10},{9,11},{10,... | collective-permute-start | bytes 1572872 | tf_op jit(solution)/shard_map/ppermute | solution.py:160
  227.4 5.9 %collective-permute-start.11 = (f32[512]{0:T(512)S(1)}, f32[512]{0:T(512)S(1)}, u32[]{:S(2)}, u32[]{:S(2)}) collective-permute-start(f32[512]{0:T(512)S(1)} %add.308), channel_id=1, source_target_pairs={{0,1},{1,0},{2,3},{3,2},{4,5},{5,4},{6,7},{7,6},{8,9},{9,8},{10,11... | collective-permute-start | bytes 6152 | tf_op jit(solution)/shard_map/ppermute | solution.py:170
  233.4 5.7 %collective-permute-start.12 = (f32[256]{0:T(256)S(1)}, f32[256]{0:T(256)S(1)}, u32[]{:S(2)}, u32[]{:S(2)}) collective-permute-start(f32[256]{0:T(256)S(1)} %dynamic_slice.27), channel_id=1, source_target_pairs={{0,2},{2,4},{4,6},{6,8},{8,10},{10,12},{12,14},{14,0},{1,3},{3,5},... | collective-permute-start | bytes 3080 | tf_op jit(solution)/shard_map/ppermute | solution.py:174
  233.4 6.0 %collective-permute-start.13 = (f32[256]{0:T(256)S(1)}, f32[256]{0:T(256)S(1)}, u32[]{:S(2)}, u32[]{:S(2)}) collective-permute-start(f32[256]{0:T(256)S(1)} %dynamic_slice.27), channel_id=1, source_target_pairs={{0,4},{2,6},{4,8},{6,10},{8,12},{10,14},{12,0},{14,2},{1,5},{3,7},... | collective-permute-start | bytes 3080 | tf_op jit(solution)/shard_map/ppermute | solution.py:174

commit v14 on v11

--- a/solution.py
+++ b/solution.py
@@ -138,22 +138,13 @@
     band0 = space_sum(band0_part)
     prev_late = hist_prev * mask
     band1_part = lagged_split(own_rows, prev_late, early1, early_sq)
-    band1 = space_sum(band1_part)
-    prev_late_b2, _ = lax.optimization_barrier((prev_late, band1_part))
-    band2_next = lagged_split(next_rows, prev_late_b2, early2, early_sq)
-
-    cs = ("col", "space")
-
-    def col_shift(offset, flip):
-        return [
-            (n_space * c + p, n_space * ((c + offset) % n_col) + (1 - p if flip else p))
-            for c in range(n_col)
-            for p in range(n_space)
-        ]
-
-    b2_same = lax.ppermute(lax.dynamic_slice_in_dim(band2_next, start_col, column_width, 1), cs, col_shift(1, False))
-    b2_cross = lax.ppermute(lax.dynamic_slice_in_dim(band2_next, other_col, column_width, 1), cs, col_shift(1, True))
-    band2 = b2_same + b2_cross
+    band2_next = lagged_split(next_rows, prev_late, early2, early_sq)
+    late_bands = jnp.stack([band1_part, band2_next])
+    mine = lax.dynamic_slice_in_dim(late_bands, start_col, column_width, 2)
+    theirs = lax.dynamic_slice_in_dim(late_bands, other_col, column_width, 2)
+    late_summed = mine + lax.ppermute(theirs, "space", swap)
+    band1 = late_summed[0]
+    band2 = lax.ppermute(late_summed[1], "col", up)
 
     total_cells = cells_dev * n_space
     denominator = LAG * total_cells * spread

time: 245 us -> 267 us (1.090)
  waiting for transfers between devices: 141 us -> 163 us
  starting transfers between devices: 23.2 us -> 18.7 us
  matrix products: 20.9 us -> 24 us
    ppermute x2, waiting for transfers between devices: 6.12 us -> 34.9 us  [the longest x1 29 us: per_device(): late_summed = mine + lax.ppermute(theirs, 'space', swap)]
    ppermute x1, waiting for transfers between devices: 23.4 us -> 37.5 us  [per_device(): head_prev = lax.ppermute(head, 'col', up)]
    ppermute x2 -> x1, waiting for transfers between devices: 15.8 us -> 3.42 us  [space_sum(): return mine + lax.ppermute(theirs, 'space', swap)]
    ppermute x2 -> x1, starting transfers between devices: 7.41 us -> 0.01 us  [space_sum(): return mine + lax.ppermute(theirs, 'space', swap)]
    ppermute x1, waiting for transfers between devices: 13.2 us -> 8.06 us  [per_device(): hist_prev = lax.ppermute(hist_send, 'col', up)]
    ppermute x2, starting transfers between devices: 0.15 us -> 3.66 us  [the longest x1 3.58 us: per_device(): late_summed = mine + lax.ppermute(theirs, 'space', swap)]
    dot_general x4, matrix products: 15.3 us -> 18.5 us  [gram(): lax.dot_general(rows, cols, (((1,), (1,)), ((), ())), preferred_element_t...]
    reduce_sum x5 -> x4, other arithmetic: 12.3 us -> 11.7 us  [square_norms(): return jnp.sum(jnp.square(values.astype(jnp.float32)), axis=1)]
  transfers between devices with their start and end apart: 14 -> 13, of which waited for: 10 -> 10; matrix products, arithmetic and copies ran while one was open for 29% -> 21% of each run, Pallas kernels for 0% -> 0%
where the time goes in v14:
time: 267 us; the launch traced here: 263 us
  waiting for transfers between devices  163 us (61%)
  other arithmetic  38.5 us (14%)
  matrix products  24 us (9%)
  starting transfers between devices  18.7 us (7%)
  local copies, waits for them, and re-layouts  18 us (7%)
    ppermute x1, waiting for transfers between devices, per_device(): tail_prev = lax.ppermute(tail, 'col', up)  50.5 us
    ppermute x1, waiting for transfers between devices, per_device(): head_prev = lax.ppermute(head, 'col', up)  37.5 us
    ppermute x1, waiting for transfers between devices, per_device(): late_summed = mine + lax.ppermute(theirs, 'space', swap)  29 us
    ppermute x1, waiting for transfers between devices, per_device(): lax.ppermute(snapshots[half_rows:], 'col', down)  20.6 us
    dot_general x4, matrix products, gram(): lax.dot_general(rows, cols, (((1,), (1,)), ((), ())), preferred_element_t...  18.5 us
    add x24, other arithmetic, lag_sum_rect(): doubled = doubled[width:width + r, width:width + c] + doubled[:r, :c]  12 us
    reduce_sum x4, other arithmetic, square_norms(): return jnp.sum(jnp.square(values.astype(jnp.float32)), axis=1)  11.7 us
    ppermute x1, waiting for transfers between devices, per_device(): hist_prev = lax.ppermute(hist_send, 'col', up)  8.06 us
  transfers between devices with their start and end apart: 13, of which 10 were waited for; matrix products, arithmetic and copies ran while one was open for 21% of the time, Pallas kernels for 0%

profile of v14, /device:TPU:4, one launch (start us, length us, event | category | flops | bytes accessed | tf_op | source)
XLA Modules:
  0.0 263.3 jit_solution(9121925565722878534)
XLA Ops:
  0.0 3.3 %slice.324 = bf16[239,4096]{1,0:T(8,128)(2,1)} slice(bf16[512,4096]{1,0:T(8,128)(2,1)} %param.3), slice={[273:512], [0:4096]} | slice | bytes 3915776 | tf_op jit(solution)/shard_map/slice | solution.py:95
  3.3 1.6 collective-permute-start.1
  4.9 1.3 collective-permute-start
  6.1 2.0 collective-permute-start.5
  8.1 4.7 %fusion.36 = (bf16[256,4096]{1,0:T(8,128)(2,1)}, bf16[256,4096]{1,0:T(8,128)(2,1)}) fusion(bf16[512,4096]{1,0:T(8,128)(2,1)} %param.3), kind=kLoop, calls=%fused_computation.100 | loop fusion | bytes 8388608 | tf_op jit(solution)/shard_map/slice | solution.py:108
  12.9 6.7 %collective-permute-start.6 = (bf16[256,4096]{1,0:T(8,128)(2,1)}, bf16[256,4096]{1,0:T(8,128)(2,1)}, u32[]{:S(2)}, u32[]{:S(2)}) collective-permute-start(bf16[256,4096]{1,0:T(8,128)(2,1)} %get-tuple-element.13), channel_id=1, source_target_pairs={{0,14},{2,0},{4,2},{6,4},{8,6},{10,8},{12,10},{14,12},{1,15},{3,1}... | collective-permute-start | bytes 6291464 | tf_op jit(solution)/shard_map/ppermute | solution.py:108
  19.6 1.6 slice.345
  21.2 50.5 %collective-permute-done.1 = bf16[239,4096]{1,0:T(8,128)(2,1)S(1)} collective-permute-done((bf16[239,4096]{1,0:T(8,128)(2,1)}, bf16[239,4096]{1,0:T(8,128)(2,1)S(1)}, u32[]{:S(2)}, u32[]{:S(2)}) %collective-permute-start.1) | collective-permute-done | bytes 1957920 | tf_op jit(solution)/shard_map/ppermute | solution.py:103
  71.7 1.8 broadcast_select_fusion.1
  73.5 3.1 %multiply_reduce_fusion.1 = f32[751]{0:T(1024)S(1)} fusion(bf16[4096]{0:T(1024)(128)(2,1)S(1)} %convert_element_type.18, bf16[512,4096]{1,0:T(8,128)(2,1)S(1)} %copy-done.1, bf16[239,4096]{1,0:T(8,128)(2,1)S(1)} %broadcast_select_fusion.1), kind=kLoop, calls=%fused_computation.1 | loop fusion | flops 24608016 | bytes 6163388 | tf_op jit(solution)/shard_map/reduce_sum | solution.py:35
  76.6 5.5 %multiply_subtract_fusion = f32[751,751]{0,1:T(8,128)S(1)} fusion(f32[751]{0:T(1024)S(1)} %multiply_reduce_fusion.1, bf16[512,4096]{1,0:T(8,128)(2,1)S(1)} %copy-done.1, bf16[239,4096]{1,0:T(8,128)(2,1)S(1)} %broadcast_select_fusion.1, bf16[4096]{0:T(1024)(128)(2,1)S(1)} %convert_element_type.18), kind=kOutput, calls=%fused_computation.14 | convolution fusion | flops 4640445440 | bytes 8419392 | tf_op jit(solution)/shard_map/dot_general | solution.py:39
  82.2 0.9 slice_add_fusion.1
  83.0 0.8 slice_add_fusion
  83.9 0.8 slice_add_fusion.2
  84.7 0.7 slice_add_fusion.3
  85.9 0.6 slice_add_fusion.4
  87.0 0.6 slice_add_fusion.5
  89.2 20.6 %collective-permute-done.7 = bf16[256,4096]{1,0:T(8,128)(2,1)} collective-permute-done((bf16[256,4096]{1,0:T(8,128)(2,1)}, bf16[256,4096]{1,0:T(8,128)(2,1)}, u32[]{:S(2)}, u32[]{:S(2)}) %collective-permute-start.7) | collective-permute-done | bytes 2097184 | tf_op jit(solution)/shard_map/ppermute | solution.py:109
  109.9 2.5 pad_maximum_fusion
  112.4 2.9 %multiply_reduce_fusion = f32[751]{0:T(1024)S(1)} fusion(bf16[4096]{0:T(1024)(128)(2,1)S(1)} %convert_element_type.18, bf16[512,4096]{1,0:T(8,128)(2,1)S(1)} %pad_maximum_fusion, bf16[239,4096]{1,0:T(8,128)(2,1)S(1)} %broadcast_select_fusion), kind=kLoop, calls=%fused_computation | loop fusion | flops 24608016 | bytes 6163388 | tf_op jit(solution)/shard_map/reduce_sum | solution.py:35
  115.3 37.5 %collective-permute-done.4 = bf16[273,4096]{1,0:T(8,128)(2,1)} collective-permute-done((bf16[273,4096]{1,0:T(8,128)(2,1)}, bf16[273,4096]{1,0:T(8,128)(2,1)}, u32[]{:S(2)}, u32[]{:S(2)}) %collective-permute-start.4) | collective-permute-done | bytes 2236448 | tf_op jit(solution)/shard_map/ppermute | solution.py:105
  152.8 3.5 %multiply_reduce_fusion.2 = f32[512]{0:T(512)S(1)} fusion(bf16[4096]{0:T(1024)(128)(2,1)S(1)} %convert_element_type.18, bf16[239,4096]{1,0:T(8,128)(2,1)S(1)} %collective-permute-done.1, bf16[273,4096]{1,0:T(8,128)(2,1)} %collective-permute-done.4), kind=kLoop, calls=%fused_computation.2 | loop fusion | flops 16776704 | bytes 4204544 | tf_op jit(solution)/shard_map/reduce_sum | solution.py:35
  156.3 5.5 %multiply_subtract_fusion.1 = f32[751,512]{0,1:T(8,128)S(1)} fusion(f32[751]{0:T(1024)S(1)} %multiply_reduce_fusion, f32[512]{0:T(512)S(1)} %multiply_reduce_fusion.2, bf16[512,4096]{1,0:T(8,128)(2,1)S(1)} %pad_maximum_fusion, bf16[239,4096]{1,0:T(8,128)(2,1)S(1)} %broadcast_select_fusion, bf16[4096]{0:T(1024)(128)(2,1)S(1)} %convert_element_type.18, ...), kind=kOutput, calls=%fused_computation.29 | convolution fusion | flops 3182115328 | bytes 11897788 | tf_op jit(solution)/shard_map/dot_general | solution.py:47
  161.8 0.6 slice_add_fusion.8
  162.4 0.6 slice_add_fusion.7
  163.0 0.6 slice_add_fusion.6
  164.5 5.5 %multiply_subtract_fusion.2 = f32[751,512]{0,1:T(8,128)S(1)} fusion(f32[512]{0:T(512)S(1)} %multiply_reduce_fusion.2, f32[751]{0:T(1024)S(1)} %multiply_reduce_fusion.1, bf16[239,4096]{1,0:T(8,128)(2,1)S(1)} %collective-permute-done.1, bf16[273,4096]{1,0:T(8,128)(2,1)} %collective-permute-done.4, bf16[4096]{0:T(1024)(128)(2,1)S(1)} %convert_element_type.18, ...), kind=kOutput, calls=%fused_computation.30 | convolution fusion | flops 3182115328 | bytes 11897788 | tf_op jit(solution)/shard_map/dot_general | solution.py:47
  170.0 0.6 slice_add_fusion.11
  170.6 0.6 slice_add_fusion.10
  171.1 0.6 slice_add_fusion.9
  172.2 0.6 slice_add_fusion.22
  176.2 8.1 %collective-permute-done.3 = bf16[239,4096]{1,0:T(8,128)(2,1)} collective-permute-done((bf16[239,4096]{1,0:T(8,128)(2,1)S(1)}, bf16[239,4096]{1,0:T(8,128)(2,1)}, u32[]{:S(2)}, u32[]{:S(2)}) %collective-permute-start.3) | collective-permute-done | bytes 1957920 | tf_op jit(solution)/shard_map/ppermute | solution.py:116
  184.3 2.1 multiply_reduce_fusion.3
  186.5 3.7 %add_subtract_fusion = f32[751,239]{0,1:T(8,128)S(1)} fusion(f32[751]{0:T(1024)S(1)} %multiply_reduce_fusion, bf16[239,4096]{1,0:T(8,128)(2,1)} %collective-permute-done.3, bf16[4096]{0:T(1024)(128)(2,1)S(1)} %convert_element_type.18, f32[239]{0:T(256)S(1)} %multiply_reduce_fusion.3, bf16[512,4096]{1,0:T(8,128)(2,1)S(1)} %pad_maximum_fusion, ...), kind=kOutput, calls=%fused_computation.71 | convolution fusion | flops 1490347776 | bytes 8840188 | tf_op jit(solution)/shard_map/dot_general | solution.py:47
  194.0 3.7 %add_subtract_fusion.1 = f32[751,239]{0,1:T(8,128)S(1)} fusion(bf16[239,4096]{1,0:T(8,128)(2,1)} %collective-permute-done.3, bf16[4096]{0:T(1024)(128)(2,1)S(1)} %convert_element_type.18, f32[239]{0:T(256)S(1)} %multiply_reduce_fusion.3, f32[751]{0:T(1024)S(1)} %multiply_reduce_fusion.1, bf16[512,4096]{1,0:T(8,128)(2,1)S(1)} %copy-done.1, ...), kind=kOutput, calls=%fused_computation.72 | convolution fusion | flops 1490347776 | bytes 8840188 | tf_op jit(solution)/shard_map/dot_general | solution.py:47
  198.3 0.7 slice_add_fusion.17
  202.3 1.0 fusion.13
  203.4 3.6 %collective-permute-start.8 = (f32[2,512,256]{1,2,0:T(8,128)}, f32[2,512,256]{1,2,0:T(8,128)}, u32[]{:S(2)}, u32[]{:S(2)}) collective-permute-start(f32[2,512,256]{1,2,0:T(8,128)} %fusion.13), channel_id=1, source_target_pairs={{0,1},{1,0},{2,3},{3,2},{4,5},{5,4},{6,7},{7,6},{8,9},{9,8},{10,11... | collective-permute-start | bytes 3145736 | tf_op jit(solution)/shard_map/ppermute | solution.py:145
  207.0 0.9 constant_dynamic-slice_fusion
  207.8 29.0 %collective-permute-done.8 = f32[2,512,256]{1,2,0:T(8,128)} collective-permute-done((f32[2,512,256]{1,2,0:T(8,128)}, f32[2,512,256]{1,2,0:T(8,128)}, u32[]{:S(2)}, u32[]{:S(2)}) %collective-permute-start.8) | collective-permute-done | bytes 1048608 | tf_op jit(solution)/shard_map/ppermute | solution.py:145
  236.9 1.4 fusion.15
  239.1 3.4 %collective-permute-done.2 = f32[512,256]{0,1:T(8,128)} collective-permute-done((f32[512,256]{0,1:T(8,128)}, f32[512,256]{0,1:T(8,128)}, u32[]{:S(2)}, u32[]{:S(2)}) %collective-permute-start.2) | collective-permute-done | bytes 524320 | tf_op jit(solution)/shard_map/ppermute | solution.py:136
  242.5 1.1 add_bitcast_fusion
  243.9 5.9 %collective-permute-done.9 = f32[512,256]{0,1:T(8,128)S(1)} collective-permute-done((f32[512,256]{0,1:T(8,128)S(1)}, f32[512,256]{0,1:T(8,128)S(1)}, u32[]{:S(2)}, u32[]{:S(2)}) %collective-permute-start.9) | collective-permute-done | bytes 524320 | tf_op jit(solution)/shard_map/ppermute | solution.py:147
  249.9 3.3 %collective-permute-start.10 = (f32[512]{0:T(512)S(1)}, f32[512]{0:T(512)S(1)}, u32[]{:S(2)}, u32[]{:S(2)}) collective-permute-start(f32[512]{0:T(512)S(1)} %add.299), channel_id=1, source_target_pairs={{0,1},{1,0},{2,3},{3,2},{4,5},{5,4},{6,7},{7,6},{8,9},{9,8},{10,11... | collective-permute-start | bytes 6152 | tf_op jit(solution)/shard_map/ppermute | solution.py:155
  253.2 1.8 collective-permute-done.10
  255.2 5.6 %collective-permute-done.11 = f32[256]{0:T(256)S(1)} collective-permute-done((f32[256]{0:T(256)S(1)}, f32[256]{0:T(256)S(1)}, u32[]{:S(2)}, u32[]{:S(2)}) %collective-permute-start.11) | collective-permute-done | bytes 1056 | tf_op jit(solution)/shard_map/ppermute | solution.py:159
  261.5 1.6 copy.9
  (77 shorter events, 16.3 us)
Async XLA Ops:
  3.3 16.3 %copy-start = (bf16[512,4096]{1,0:T(8,128)(2,1)S(1)}, bf16[512,4096]{1,0:T(8,128)(2,1)}, u32[]{:S(2)}) copy-start(bf16[512,4096]{1,0:T(8,128)(2,1)} %param.3) | copy-start | bytes 12582916
  3.3 68.5 %collective-permute-start.1 = (bf16[239,4096]{1,0:T(8,128)(2,1)}, bf16[239,4096]{1,0:T(8,128)(2,1)S(1)}, u32[]{:S(2)}, u32[]{:S(2)}) collective-permute-start(bf16[239,4096]{1,0:T(8,128)(2,1)} %slice.324), channel_id=1, source_target_pairs={{0,2},{2,4},{4,6},{6,8},{8,10},{10,12},{12,14},{14,0},{1,3},{3,5},... | collective-permute-start | bytes 5873672 | tf_op jit(solution)/shard_map/ppermute | solution.py:103
  4.9 66.9 %collective-permute-start = (bf16[239,4096]{1,0:T(8,128)(2,1)}, bf16[239,4096]{1,0:T(8,128)(2,1)}, u32[]{:S(2)}, u32[]{:S(2)}) collective-permute-start(bf16[239,4096]{1,0:T(8,128)(2,1)} %slice.324), channel_id=1, source_target_pairs={{14,16},{30,32},{46,48},{62,64},{78,80},{94,96},{110,112},{15,17},... | collective-permute-start | bytes 5873672 | tf_op jit(solution)/shard_map/ppermute | solution.py:104
  6.1 82.5 %collective-permute-start.5 = (bf16[239,4096]{1,0:T(8,128)(2,1)}, bf16[239,4096]{1,0:T(8,128)(2,1)}, u32[]{:S(2)}, u32[]{:S(2)}) collective-permute-start(bf16[239,4096]{1,0:T(8,128)(2,1)} %slice.324), channel_id=1, source_target_pairs={{14,30},{30,46},{46,62},{62,78},{78,94},{94,110},{110,126},{15,31}... | collective-permute-start | bytes 5873672 | tf_op jit(solution)/shard_map/ppermute | solution.py:111
  12.9 76.4 %collective-permute-start.6 = (bf16[256,4096]{1,0:T(8,128)(2,1)}, bf16[256,4096]{1,0:T(8,128)(2,1)}, u32[]{:S(2)}, u32[]{:S(2)}) collective-permute-start(bf16[256,4096]{1,0:T(8,128)(2,1)} %get-tuple-element.13), channel_id=1, source_target_pairs={{0,14},{2,0},{4,2},{6,4},{8,6},{10,8},{12,10},{14,12},{1,15},{3,1}... | collective-permute-start | bytes 6291464 | tf_op jit(solution)/shard_map/ppermute | solution.py:108
  19.6 90.3 %collective-permute-start.7 = (bf16[256,4096]{1,0:T(8,128)(2,1)}, bf16[256,4096]{1,0:T(8,128)(2,1)}, u32[]{:S(2)}, u32[]{:S(2)}) collective-permute-start(bf16[256,4096]{1,0:T(8,128)(2,1)} %get-tuple-element.14), channel_id=1, source_target_pairs={{0,14},{2,0},{4,2},{6,4},{8,6},{10,8},{12,10},{14,12},{1,15},{3,1}... | collective-permute-start | bytes 6291464 | tf_op jit(solution)/shard_map/ppermute | solution.py:109
  19.6 1.6 copy-start.4
  21.2 52.3 %copy-start.1 = (bf16[512,4096]{1,0:T(8,128)(2,1)S(1)}, bf16[512,4096]{1,0:T(8,128)(2,1)}, u32[]{:S(2)}) copy-start(bf16[512,4096]{1,0:T(8,128)(2,1)} %param.3) | copy-start | bytes 12582916
  71.7 81.0 %collective-permute-start.4 = (bf16[273,4096]{1,0:T(8,128)(2,1)}, bf16[273,4096]{1,0:T(8,128)(2,1)}, u32[]{:S(2)}, u32[]{:S(2)}) collective-permute-start(bf16[273,4096]{1,0:T(8,128)(2,1)} %slice.345), channel_id=1, source_target_pairs={{0,2},{2,4},{4,6},{6,8},{8,10},{10,12},{12,14},{14,0},{1,3},{3,5},... | collective-permute-start | bytes 6709256 | tf_op jit(solution)/shard_map/ppermute | solution.py:105
  88.6 95.7 %collective-permute-start.3 = (bf16[239,4096]{1,0:T(8,128)(2,1)S(1)}, bf16[239,4096]{1,0:T(8,128)(2,1)}, u32[]{:S(2)}, u32[]{:S(2)}) collective-permute-start(bf16[239,4096]{1,0:T(8,128)(2,1)S(1)} %broadcast_select_fusion.1), channel_id=1, source_target_pairs={{0,2},{2,4},{4,6},{6,8},{8,10},{10,12},{12,14},{14,0},{1,3},{3,5},... | collective-permute-start | bytes 5873672 | tf_op jit(solution)/shard_map/ppermute | solution.py:116
  161.8 11.0 %copy-start.2 = (f32[751,512]{0,1:T(8,128)}, f32[751,512]{0,1:T(8,128)S(1)}, u32[]{:S(2)}) copy-start(f32[751,512]{0,1:T(8,128)S(1)} %multiply_subtract_fusion.1) | copy-start | bytes 4614148
  170.0 3.5 %copy-start.3 = (f32[751,512]{0,1:T(8,128)}, f32[751,512]{0,1:T(8,128)S(1)}, u32[]{:S(2)}) copy-start(f32[751,512]{0,1:T(8,128)S(1)} %multiply_subtract_fusion.2) | copy-start | bytes 4614148
  186.4 3.8 %slice-start = ((f32[751,512]{0,1:T(8,128)}), f32[751,239]{0,1:T(8,128)S(1)}, s32[]{:S(2)}) async-start(f32[751,512]{0,1:T(8,128)} %copy-done.2), calls=%async_computation | async-start | bytes 1474560 | tf_op jit(solution)/shard_map/slice | solution.py:83
  194.0 3.8 %slice-start.1 = ((f32[751,512]{0,1:T(8,128)}), f32[751,239]{0,1:T(8,128)S(1)}, s32[]{:S(2)}) async-start(f32[751,512]{0,1:T(8,128)} %copy-done.3), calls=%async_computation.1 | async-start | bytes 1474560 | tf_op jit(solution)/shard_map/slice | solution.py:83
  203.4 33.5 %collective-permute-start.8 = (f32[2,512,256]{1,2,0:T(8,128)}, f32[2,512,256]{1,2,0:T(8,128)}, u32[]{:S(2)}, u32[]{:S(2)}) collective-permute-start(f32[2,512,256]{1,2,0:T(8,128)} %fusion.13), channel_id=1, source_target_pairs={{0,1},{1,0},{2,3},{3,2},{4,5},{5,4},{6,7},{7,6},{8,9},{9,8},{10,11... | collective-permute-start | bytes 3145736 | tf_op jit(solution)/shard_map/ppermute | solution.py:145
  207.8 34.7 %collective-permute-start.2 = (f32[512,256]{0,1:T(8,128)}, f32[512,256]{0,1:T(8,128)}, u32[]{:S(2)}, u32[]{:S(2)}) collective-permute-start(f32[512,256]{0,1:T(8,128)} %constant_dynamic-slice_fusion), channel_id=1, source_target_pairs={{0,1},{1,0},{2,3},{3,2},{4,5},{5,4},{6,7},{7,6},{8,9},{9,8},{10,11... | collective-permute-start | bytes 1572872 | tf_op jit(solution)/shard_map/ppermute | solution.py:136
  238.4 11.4 %collective-permute-start.9 = (f32[512,256]{0,1:T(8,128)S(1)}, f32[512,256]{0,1:T(8,128)S(1)}, u32[]{:S(2)}, u32[]{:S(2)}) collective-permute-start(f32[512,256]{0,1:T(8,128)S(1)} %get-tuple-element.26), channel_id=1, source_target_pairs={{0,2},{2,4},{4,6},{6,8},{8,10},{10,12},{12,14},{14,0},{1,3},{3,5},... | collective-permute-start | bytes 1572872 | tf_op jit(solution)/shard_map/ppermute | solution.py:147
  249.9 5.2 %collective-permute-start.10 = (f32[512]{0:T(512)S(1)}, f32[512]{0:T(512)S(1)}, u32[]{:S(2)}, u32[]{:S(2)}) collective-permute-start(f32[512]{0:T(512)S(1)} %add.299), channel_id=1, source_target_pairs={{0,1},{1,0},{2,3},{3,2},{4,5},{5,4},{6,7},{7,6},{8,9},{9,8},{10,11... | collective-permute-start | bytes 6152 | tf_op jit(solution)/shard_map/ppermute | solution.py:155
  255.1 5.7 %collective-permute-start.11 = (f32[256]{0:T(256)S(1)}, f32[256]{0:T(256)S(1)}, u32[]{:S(2)}, u32[]{:S(2)}) collective-permute-start(f32[256]{0:T(256)S(1)} %dynamic_slice.19), channel_id=1, source_target_pairs={{0,2},{2,4},{4,6},{6,8},{8,10},{10,12},{12,14},{14,0},{1,3},{3,5},... | collective-permute-start | bytes 3080 | tf_op jit(solution)/shard_map/ppermute | solution.py:159
  255.1 6.0 %collective-permute-start.12 = (f32[256]{0:T(256)S(1)}, f32[256]{0:T(256)S(1)}, u32[]{:S(2)}, u32[]{:S(2)}) collective-permute-start(f32[256]{0:T(256)S(1)} %dynamic_slice.19), channel_id=1, source_target_pairs={{0,4},{2,6},{4,8},{6,10},{8,12},{10,14},{12,0},{14,2},{1,5},{3,7},... | collective-permute-start | bytes 3080 | tf_op jit(solution)/shard_map/ppermute | solution.py:159
